TPU v7x, 256 devices: a whole 4x4x8 slice. The times are simulated.
256 devices in a mesh: req: 32 (over y, x, core), tp: 8 (over z).
Axes of the slice: x: 4, y: 4, z: 8, core: 2. Of those that a mesh axis runs over, the one named last changes fastest.
Arguments:
- queries: bfloat16 [2048, 4096], P('req', 'tp'), may hold values from -8 to 8
- suffix_kv: bfloat16 [2048, 2, 1024], P('req', None, 'tp'), may hold values from -6 to 6
- prefix_cache: bfloat16 [32, 2048, 2, 1024], P('req', None, None, 'tp'), may hold values from -8 to 8
- prefix_owner: int32 [4], replicated, may hold values from 0 to 31, as said below
- request_prefix: int32 [64], P('req'), may hold values from 0 to 3
- suffix_len: int32 [64], P('req'), may hold values from 1 to 32, 1728 in all
- residual: bfloat16 [2048, 4096], P('req'), may hold values from -40 to 40
- norm_gain: float32 [4096], replicated, may hold values from 0.1 to 1.9
- router: float32 [4096, 8], replicated, may hold values from -0.09375 to 0.09375
- routes: int32 [2048, 2], P('req'), may hold values from 0 to 7, all different within a row; in each aligned block of 64 rows (0 to 63, 64 to 127, ...) at most 18 rows name the same one
- w_gate: bfloat16 [32, 4096, 2048], P('req', None, 'tp'), may hold values from -0.09375 to 0.09375
- w_up: bfloat16 [32, 4096, 2048], P('req', None, 'tp'), may hold values from -0.09375 to 0.09375
- w_down: bfloat16 [32, 2048, 4096], P('req', 'tp'), may hold values from -0.0625 to 0.0625
- w_out: bfloat16 [4096, 4096], P('tp'), may hold values from -1 to 1
Outputs:
- layer_out: bfloat16 [2048, 4096], P('req', 'tp')
Inputs may be any that keep to these rules, and one draw needn't show every extreme that they name: `prefix_owner`: the 4 owners are distinct. Among the 64 token slots of one req index, no expert is named by more than 18 routes, and in some req indices one expert is named by exactly 18; the two experts of a token differ.
All inputs are finite; a program needn't handle non-finite values. No bound on the sum of `suffix_len` on one device may be relied on, other than what follows from the above.
Results may differ from a plain program's by a relative error of at most 0.017.
Values may be sent and summed in bfloat16 or wider, within the bound.
No kernel may reach another device: no remote copies, remote signals or barrier semaphores. Data moves between devices by JAX's collectives and lax.ppermute only.
A program may use at most 128 MiB of HBM per device.

v0:
```python
import math

import jax
import jax.numpy as jnp
from jax import lax
from jax.sharding import PartitionSpec as P

HEADS = 32
KVH = 8
HD = 128
EXPERTS = 8
NPFX = 4
CAP = 18


def broadcast(x, axis, root):
    mine = lax.axis_index(axis) == root
    return lax.psum(jnp.where(mine, x, jnp.zeros_like(x)), axis)


def attend_local(queries, suffix_kv, chosen, suffix_len, requests, slot_len):
    kv_local = suffix_kv.shape[2] // HD
    group_size = HEADS // KVH
    plen_local = chosen.shape[1]
    query_block = queries.reshape(requests, slot_len, kv_local, group_size, HD)
    cache_block = chosen.reshape(requests, plen_local, 2, kv_local, HD)
    suffix_block = suffix_kv.reshape(requests, slot_len, 2, kv_local, HD)
    score_scale = 1.0 / math.sqrt(HD)
    prefix_score = (
        jnp.einsum(
            "rikgd,rjkd->rkgij",
            query_block,
            cache_block[:, :, 0],
            preferred_element_type=jnp.float32,
        )
        * score_scale
    )
    suffix_score = (
        jnp.einsum(
            "rikgd,rjkd->rkgij",
            query_block,
            suffix_block[:, :, 0],
            preferred_element_type=jnp.float32,
        )
        * score_scale
    )
    positions = jnp.arange(slot_len, dtype=jnp.int32)
    allowed = (positions[None, None, :] <= positions[None, :, None]) & (
        positions[None, None, :] < suffix_len[:, None, None]
    )
    suffix_score = jnp.where(allowed[:, None, None], suffix_score, -1e30)
    score_peak = jnp.maximum(prefix_score.max(-1), suffix_score.max(-1))[..., None]
    prefix_exp = jnp.exp(prefix_score - score_peak)
    suffix_exp = jnp.exp(suffix_score - score_peak)
    normaliser = prefix_exp.sum(-1, keepdims=True) + suffix_exp.sum(-1, keepdims=True)
    prefix_prob = (prefix_exp / normaliser).astype(jnp.bfloat16)
    suffix_prob = (suffix_exp / normaliser).astype(jnp.bfloat16)
    mixed_values = jnp.einsum(
        "rkgij,rjkd->rikgd", prefix_prob, cache_block[:, :, 1], preferred_element_type=jnp.float32
    )
    mixed_values = mixed_values + jnp.einsum(
        "rkgij,rjkd->rikgd", suffix_prob, suffix_block[:, :, 1], preferred_element_type=jnp.float32
    )
    return mixed_values.reshape(requests * slot_len, kv_local * group_size * HD).astype(
        jnp.bfloat16
    )


def routing_tables(routes, live_rows, route_weight):
    expert_ids = jnp.arange(EXPERTS, dtype=jnp.int32)
    member = (routes[:, :, None] == expert_ids) & live_rows[:, None, None]
    member_int = member.astype(jnp.int32)
    flat_member = member_int.reshape(-1, EXPERTS)
    earlier = jnp.cumsum(flat_member, axis=0) - flat_member
    slot_index = jnp.sum(earlier * flat_member, axis=1).reshape(routes.shape)
    slot_hit = (slot_index[:, :, None] == jnp.arange(CAP, dtype=jnp.int32)).astype(jnp.float32)
    member_float = member.astype(jnp.float32)
    placing = (
        jnp.einsum("tke,tkc->ect", member_float, slot_hit)
        .reshape(EXPERTS * CAP, routes.shape[0])
        .astype(jnp.bfloat16)
    )
    combining = jnp.einsum(
        "tke,tkc,tk->tec", member_float, slot_hit, route_weight, precision=lax.Precision.HIGHEST
    )
    return (placing, combining.reshape(routes.shape[0], EXPERTS * CAP))


def expert_apply(arrived, w_gate, w_up, w_down):
    flat_rows = arrived.reshape(-1, arrived.shape[2])
    gate_value = jnp.dot(flat_rows, w_gate[0], preferred_element_type=jnp.float32)
    up_value = jnp.dot(flat_rows, w_up[0], preferred_element_type=jnp.float32)
    hidden_units = (jax.nn.silu(gate_value) * up_value).astype(jnp.bfloat16)
    piece_out = jnp.dot(hidden_units, w_down[0], preferred_element_type=jnp.float32).astype(
        jnp.bfloat16
    )
    return piece_out.reshape(arrived.shape[0], arrived.shape[1], piece_out.shape[1])


def send_back(parts):
    return lax.all_to_all(parts, "req", split_axis=0, concat_axis=0, tiled=True)


def per_device(
    queries,
    suffix_kv,
    prefix_cache,
    prefix_owner,
    request_prefix,
    suffix_len,
    residual,
    norm_gain,
    router,
    routes,
    w_gate,
    w_up,
    w_down,
    w_out,
):
    tp_count = lax.axis_size("tp")
    tp_index = lax.axis_index("tp")
    req_count = lax.axis_size("req")
    model_width = residual.shape[1]
    share_width = model_width // tp_count
    share_start = tp_index * share_width
    requests = request_prefix.shape[0]
    slot_len = queries.shape[0] // requests
    caches = []
    for prefix_index in range(NPFX):
        caches.append(broadcast(prefix_cache, "req", prefix_owner[prefix_index]))
    stacked = jnp.concatenate(caches, axis=0)
    chosen = jnp.take(stacked, request_prefix, axis=0)
    attended = attend_local(queries, suffix_kv, chosen, suffix_len, requests, slot_len)
    partial_value = jnp.dot(attended, w_out, preferred_element_type=jnp.float32)
    summed_attn = lax.psum(partial_value.astype(jnp.bfloat16), "tp").astype(jnp.float32)
    hidden_state = residual.astype(jnp.float32) + summed_attn
    inverse = lax.rsqrt(jnp.mean(hidden_state * hidden_state, axis=1, keepdims=True) + 1e-05)
    scaled = hidden_state * norm_gain * inverse
    logits = jnp.dot(scaled, router, precision=lax.Precision.HIGHEST)
    normed_full = scaled.astype(jnp.bfloat16)
    hidden_share = lax.dynamic_slice_in_dim(hidden_state, share_start, share_width, 1)
    route_hit = (routes[:, :, None] == jnp.arange(EXPERTS, dtype=jnp.int32)).astype(jnp.float32)
    picked_logit = jnp.sum(route_hit * logits[:, None, :], axis=2)
    first_weight = jax.nn.sigmoid(picked_logit[:, 0] - picked_logit[:, 1])
    route_weight = jnp.stack([first_weight, 1.0 - first_weight], axis=1)
    live_rows = jnp.arange(routes.shape[0], dtype=jnp.int32) % slot_len < jnp.repeat(
        suffix_len, slot_len
    )
    placing, combining = routing_tables(routes, live_rows, route_weight)
    repeats = req_count // EXPERTS
    send_rows = jnp.dot(placing, normed_full, preferred_element_type=jnp.float32).astype(
        jnp.bfloat16
    )
    outgoing = jnp.tile(send_rows.reshape(EXPERTS, CAP, model_width), (repeats, 1, 1))
    returned = send_back(
        expert_apply(
            lax.all_to_all(outgoing, "req", split_axis=0, concat_axis=0, tiled=True),
            w_gate,
            w_up,
            w_down,
        )
    )
    summed = returned.astype(jnp.float32).reshape(repeats, EXPERTS, CAP, model_width).sum(axis=0)
    mixture_full = jnp.dot(
        combining, summed.reshape(EXPERTS * CAP, model_width), precision=lax.Precision.HIGHEST
    )
    mixture_share = lax.psum_scatter(
        mixture_full.astype(jnp.bfloat16), "tp", scatter_dimension=1, tiled=True
    ).astype(jnp.float32)
    layer_out = jnp.where(live_rows[:, None], hidden_share + mixture_share, 0.0)
    return layer_out.astype(jnp.bfloat16)


def solution(mesh):
    return jax.shard_map(
        per_device,
        mesh=mesh,
        in_specs=(
            P("req", "tp"),
            P("req", None, "tp"),
            P("req", None, None, "tp"),
            P(),
            P("req"),
            P("req"),
            P("req", None),
            P(),
            P(),
            P("req", None),
            P("req", None, "tp"),
            P("req", None, "tp"),
            P("req", "tp", None),
            P("tp", None),
        ),
        out_specs=P("req", "tp"),
        check_vma=False,
    )
```

profile of v0, /device:TPU:2, one launch (start us, length us, event | category | flops | bytes accessed | tf_op | source)
XLA Modules:
  0.0 477.0 jit_solution(7301594830305967729)
XLA Ops:
  6.5 1.5 fusion.63
  10.6 3.3 broadcast_select_fusion.3
  15.7 122.6 %all-reduce.6.cloned.1.call-done = (bf16[1,2048,2,128]{3,1,2,0:T(8,128)(2,1)}, bf16[1,2048,2,128]{3,1,2,0:T(8,128)(2,1)}, bf16[1,2048,2,128]{3,1,2,0:T(8,128)(2,1)}, bf16[1,2048,2,128]{3,1,2,0:T(8,128)(2,1)}) async-done(((bf16[1,2048,2,128]{3,1,2,0:T(8,128)(2,1)}, bf16[1,2048,2,128]{3,1,2,0:T(8,128)(2,1)}, bf16[1,2048,2,128]{3,1,2,0:T(8,128)(2,1)}, bf16[1,2048,2,128]{3,1,2,0:T(8,128)(2,1)}), ...) | async-done | bytes 4194320 | tf_op jit(solution)/shard_map/psum | solution.py:18
  138.4 3.7 pad_maximum_fusion
  142.1 4.4 gather_fusion
  146.5 1.9 bitcast_select_fusion
  150.2 1.4 copy-done.1
  151.5 1.6 convolution_convert_fusion.2
  154.5 73.0 %all-reduce.4.cloned.1.call-done = bf16[64,4096]{1,0:T(8,128)(2,1)} async-done(((bf16[64,4096]{1,0:T(8,128)(2,1)}), bf16[64,4096]{1,0:T(8,128)(2,1)}) %all-reduce.4.cloned.1.call-update) | async-done | bytes 524304 | tf_op jit(solution)/shard_map/psum | solution.py:135
  227.5 2.4 convert_add_fusion
  229.9 1.6 convolution_convert_fusion.1
  231.5 1.3 tile.10
  232.8 2.2 tile.11
  235.0 79.5 %all_to_all.10 = bf16[32,18,4096]{2,1,0:T(8,128)(2,1)} all-to-all(bf16[32,18,4096]{2,1,0:T(8,128)(2,1)S(1)} %bitcast.105), channel_id=1, replica_groups=mesh['req'=32,'tp'=8] {'req'}, dimensions={0} | all-to-all | bytes 9437184 | tf_op jit(solution)/shard_map/all_to_all | solution.py:157
  314.5 7.7 %reshape.205 = bf16[576,4096]{1,0:T(8,128)(2,1)} reshape(bf16[32,18,4096]{2,1,0:T(8,128)(2,1)} %all_to_all.10) | data formatting | bytes 9437184 | tf_op jit(solution)/shard_map/reshape | solution.py:90
  322.2 4.4 fusion.5
  326.6 10.2 %convolution_convert_fusion = bf16[576,4096]{1,0:T(8,128)(2,1)} fusion(bf16[1,256,4096]{2,1,0:T(8,128)(2,1)S(1)} %copy-done, bf16[576,4096]{1,0:T(8,128)(2,1)} %reshape.205, bf16[1,4096,256]{2,1,0:T(8,128)(2,1)} %param.25, f32[576,256]{1,0:T(8,128)S(1)} %fusion.5), kind=kOutput, calls=%fused_computation.2 | convolution fusion | flops 2419163136 | bytes 14221312 | tf_op jit(solution)/shard_map/dot_general | solution.py:94
  336.8 7.5 %reshape.206 = bf16[32,18,4096]{2,1,0:T(8,128)(2,1)} reshape(bf16[576,4096]{1,0:T(8,128)(2,1)} %convolution_convert_fusion) | data formatting | bytes 9437184 | tf_op jit(solution)/shard_map/reshape | solution.py:97
  344.4 6.1 %all-to-all-start.1 = ((bf16[32,18,4096]{2,1,0:T(8,128)(2,1)}), bf16[32,18,4096]{2,1,0:T(8,128)(2,1)}, u32[]{:S(2)}, u32[]{:S(2)}) async-start(bf16[32,18,4096]{2,1,0:T(8,128)(2,1)} %reshape.206), calls=%async_computation.1 | async-start | bytes 12582912 | tf_op jit(solution)/shard_map/all_to_all | solution.py:101
  353.2 72.6 %all-to-all-done.1 = bf16[32,18,4096]{2,1,0:T(8,128)(2,1)} async-done(((bf16[32,18,4096]{2,1,0:T(8,128)(2,1)}), bf16[32,18,4096]{2,1,0:T(8,128)(2,1)}, u32[]{:S(2)}, u32[]{:S(2)}) %all-to-all-start.1) | async-done | bytes 4718624 | tf_op jit(solution)/shard_map/all_to_all | solution.py:101
  425.8 4.3 convert_reduce_fusion
  430.1 4.2 fusion
  434.3 34.5 %reduce-scatter.2.cloned.1.call-done = bf16[64,512]{1,0:T(8,128)(2,1)} async-done(((bf16[64,4096]{1,0:T(8,128)(2,1)}), bf16[64,512]{1,0:T(8,128)(2,1)}) %reduce-scatter.2.cloned.1.call-update) | async-done | bytes 65552 | tf_op jit(solution)/shard_map/reduce_scatter | solution.py:167
  468.8 1.7 select_convert_fusion
  (71 shorter events, 7.5 us)
Async XLA Ops:
  6.5 320.1 %copy-start = (bf16[1,256,4096]{2,1,0:T(8,128)(2,1)S(1)}, bf16[1,256,4096]{2,1,0:T(8,128)(2,1)}, u32[]{:S(2)}) copy-start(bf16[1,256,4096]{2,1,0:T(8,128)(2,1)} %param.26) | copy-start | bytes 6291460
  6.5 131.8 %all-reduce.6.cloned.1.call-start = ((), (), s32[]{:S(2)}) async-start(), calls=%async_computation.5 | async-start | bytes 8388608 | tf_op jit(solution)/shard_map/psum | solution.py:18
  13.9 0.7 copy-start.12
  13.9 1.1 copy-start.9
  13.9 1.3 copy-start.7
  13.9 1.3 copy-start.6
  13.9 1.4 copy-start.11
  14.0 213.5 %all-reduce.4.cloned.1.call-start = ((), (), s32[]{:S(2)}) async-start(), calls=%async_computation.3 | async-start | bytes 1048576 | tf_op jit(solution)/shard_map/psum | solution.py:135
  149.3 2.2 copy-start.1
  153.2 74.3 %copy-start.2 = (bf16[64,4096]{1,0:T(8,128)(2,1)S(1)}, bf16[64,4096]{1,0:T(8,128)(2,1)}, u32[]{:S(2)}) copy-start(bf16[64,4096]{1,0:T(8,128)(2,1)} %param.20) | copy-start | bytes 1572868
  153.2 76.7 %copy-start.8 = (f32[4096]{0:T(1024)S(1)}, f32[4096]{0:T(1024)}, u32[]{:S(2)}) copy-start(f32[4096]{0:T(1024)} %param.21) | copy-start | bytes 49156
  227.5 2.4 copy-start.4
  344.4 6.4 %copy-start.3 = (bf16[64,4096]{1,0:T(8,128)(2,1)S(1)}, bf16[64,4096]{1,0:T(8,128)(2,1)}, u32[]{:S(2)}) copy-start(bf16[64,4096]{1,0:T(8,128)(2,1)} %param.20) | copy-start | bytes 1572868
  344.4 6.4 %copy-start.5 = (bf16[64,4096]{1,0:T(8,128)(2,1)S(1)}, bf16[64,4096]{1,0:T(8,128)(2,1)}, u32[]{:S(2)}) copy-start(bf16[64,4096]{1,0:T(8,128)(2,1)} %all-reduce.4.cloned.1.call-done) | copy-start | bytes 1572868
  344.4 6.4 %copy-start.10 = (f32[4096,8]{0,1:T(8,128)S(1)}, f32[4096,8]{0,1:T(8,128)}, u32[]{:S(2)}) copy-start(f32[4096,8]{0,1:T(8,128)} %param.22) | copy-start | bytes 393220
  344.4 81.4 %all-to-all-start.1 = ((bf16[32,18,4096]{2,1,0:T(8,128)(2,1)}), bf16[32,18,4096]{2,1,0:T(8,128)(2,1)}, u32[]{:S(2)}, u32[]{:S(2)}) async-start(bf16[32,18,4096]{2,1,0:T(8,128)(2,1)} %reshape.206), calls=%async_computation.1 | async-start | bytes 12582912 | tf_op jit(solution)/shard_map/all_to_all | solution.py:101
  350.5 118.3 %reduce-scatter.2.cloned.1.call-start = ((), (), s32[]{:S(2)}) async-start(), calls=%async_computation.4 | async-start | bytes 589824 | tf_op jit(solution)/shard_map/reduce_scatter | solution.py:167
Sparse Core Ops, SparseCore 0:
  14.1 124.2 all-reduce.5
  153.3 74.1 all-reduce.3
  434.4 34.3 reduce-scatter.1
where the time goes:
time: 478 us; the launch traced here: 477 us
  waiting for transfers between devices  303 us (63%)
  blocking collectives  79.5 us (17%)
  local copies, waits for them, and re-layouts  27.9 us (6%)
  matrix products  25.9 us (5%)
  other arithmetic  18.6 us (4%)
  between operations  15.9 us (3%)
  starting transfers between devices  6.38 us (1%)
    psum x1, waiting for transfers between devices, broadcast(): return lax.psum(jnp.where(mine, x, jnp.zeros_like(x)), axis)  123 us
    all_to_all x1, blocking collectives, per_device(): lax.all_to_all(outgoing, 'req', split_axis=0, concat_axis=0, tiled=True)  79.5 us
    psum x1, waiting for transfers between devices, per_device(): lax.psum(partial_value.astype(jnp.bfloat16), 'tp').astype(jnp.float32)  73 us
    all_to_all x1, waiting for transfers between devices, send_back(): return lax.all_to_all(parts, 'req', split_axis=0, concat_axis=0, tiled=True)  72.6 us
    reduce_scatter x1, waiting for transfers between devices, per_device(): lax.psum_scatter(mixture_full.astype(jnp.bfloat16), 'tp', scatter_dimensi...  34.5 us
    dot_general x1, matrix products, expert_apply(): jnp.dot(hidden_units, w_down[0], preferred_element_type=jnp.float32)  10.2 us
  transfers between devices with their start and end apart: 4, of which 4 were waited for; matrix products, arithmetic and copies ran while one was open for 1% of the time, Pallas kernels for 0%

commit v1 on v0

--- a/solution.py
+++ b/solution.py
@@ -16,6 +16,41 @@
 def broadcast(x, axis, root):
     mine = lax.axis_index(axis) == root
     return lax.psum(jnp.where(mine, x, jnp.zeros_like(x)), axis)
+
+
+def fetch_prefixes(prefix_cache, prefix_owner, request_prefix, req_count):
+    plen = prefix_cache.shape[1]
+    width = prefix_cache.shape[3]
+    piece = plen // req_count
+    requests = request_prefix.shape[0]
+    pieces = prefix_cache.reshape(req_count, piece, 2, width)
+    scattered = lax.all_to_all(pieces, "req", 0, 0, tiled=True)
+    owner_pieces = jnp.take(scattered, prefix_owner, axis=0)
+    wanted = lax.all_to_all(
+        jnp.broadcast_to(request_prefix[None], (req_count, requests)), "req", 0, 0, tiled=True
+    )
+    outgoing = jnp.take(owner_pieces, wanted.reshape(-1), axis=0).reshape(
+        req_count, requests, piece, 2, width
+    )
+    arrived = lax.all_to_all(outgoing, "req", 0, 0, tiled=True)
+    return jnp.transpose(arrived, (1, 0, 2, 3, 4)).reshape(requests, plen, 2, width)
+
+
+def tp_reduce_scatter(values, tp_count):
+    rows, width = values.shape
+    share = width // tp_count
+    chunks = jnp.transpose(
+        values.astype(jnp.bfloat16).reshape(rows, tp_count, share), (1, 0, 2)
+    )
+    arrived = lax.all_to_all(chunks, "tp", 0, 0, tiled=True)
+    return arrived.astype(jnp.float32).sum(axis=0)
+
+
+def tp_all_gather(share_values, tp_count):
+    rows, share = share_values.shape
+    copies = jnp.broadcast_to(share_values[None], (tp_count, rows, share))
+    arrived = lax.all_to_all(copies, "tp", 0, 0, tiled=True)
+    return jnp.transpose(arrived, (1, 0, 2)).reshape(rows, tp_count * share)
 
 
 def attend_local(queries, suffix_kv, chosen, suffix_len, requests, slot_len):
@@ -125,20 +160,18 @@
     share_start = tp_index * share_width
     requests = request_prefix.shape[0]
     slot_len = queries.shape[0] // requests
-    caches = []
-    for prefix_index in range(NPFX):
-        caches.append(broadcast(prefix_cache, "req", prefix_owner[prefix_index]))
-    stacked = jnp.concatenate(caches, axis=0)
-    chosen = jnp.take(stacked, request_prefix, axis=0)
+    chosen = fetch_prefixes(prefix_cache, prefix_owner, request_prefix, req_count)
     attended = attend_local(queries, suffix_kv, chosen, suffix_len, requests, slot_len)
     partial_value = jnp.dot(attended, w_out, preferred_element_type=jnp.float32)
-    summed_attn = lax.psum(partial_value.astype(jnp.bfloat16), "tp").astype(jnp.float32)
-    hidden_state = residual.astype(jnp.float32) + summed_attn
+    attn_share = tp_reduce_scatter(partial_value, tp_count)
+    attn_full = tp_all_gather(attn_share.astype(jnp.bfloat16), tp_count)
+    hidden_state = residual.astype(jnp.float32) + attn_full.astype(jnp.float32)
+    residual_share = lax.dynamic_slice_in_dim(residual, share_start, share_width, 1)
+    hidden_share = residual_share.astype(jnp.float32) + attn_share
     inverse = lax.rsqrt(jnp.mean(hidden_state * hidden_state, axis=1, keepdims=True) + 1e-05)
     scaled = hidden_state * norm_gain * inverse
     logits = jnp.dot(scaled, router, precision=lax.Precision.HIGHEST)
     normed_full = scaled.astype(jnp.bfloat16)
-    hidden_share = lax.dynamic_slice_in_dim(hidden_state, share_start, share_width, 1)
     route_hit = (routes[:, :, None] == jnp.arange(EXPERTS, dtype=jnp.int32)).astype(jnp.float32)
     picked_logit = jnp.sum(route_hit * logits[:, None, :], axis=2)
     first_weight = jax.nn.sigmoid(picked_logit[:, 0] - picked_logit[:, 1])
@@ -164,9 +197,7 @@
     mixture_full = jnp.dot(
         combining, summed.reshape(EXPERTS * CAP, model_width), precision=lax.Precision.HIGHEST
     )
-    mixture_share = lax.psum_scatter(
-        mixture_full.astype(jnp.bfloat16), "tp", scatter_dimension=1, tiled=True
-    ).astype(jnp.float32)
+    mixture_share = tp_reduce_scatter(mixture_full, tp_count)
     layer_out = jnp.where(live_rows[:, None], hidden_share + mixture_share, 0.0)
     return layer_out.astype(jnp.bfloat16)
 

time: 478 us -> 361 us (0.76)
  waiting for transfers between devices: 303 us -> 149 us
  blocking collectives: 79.5 us -> 106 us
  starting transfers between devices: 6.38 us -> 31.6 us
  between operations: 15.9 us -> 0.43 us
  other arithmetic: 18.6 us -> 12.8 us
  local copies, waits for them, and re-layouts: 27.9 us -> 33.6 us
    psum x2 -> x0, waiting for transfers between devices: 196 us -> none  [the longest x1 123 us: broadcast(): return lax.psum(jnp.where(mine, x, jnp.zeros_like(x)), axis)]
    all_to_all x0 -> x5, waiting for transfers between devices: none -> 77.4 us  [the longest x1 27.6 us: fetch_prefixes(): arrived = lax.all_to_all(outgoing, 'req', 0, 0, tiled=True)]
    reduce_scatter x1 -> x0, waiting for transfers between devices: 34.5 us -> none  [per_device(): lax.psum_scatter(mixture_full.astype(jnp.bfloat16), 'tp', scatter_dimensi...]
    all_to_all x0 -> x5, starting transfers between devices: none -> 25.6 us  [the longest x1 7.62 us: fetch_prefixes(): lax.all_to_all(jnp.broadcast_to(request_prefix[None], (req_count, request...]
    all_to_all x0 -> x1, blocking collectives: none -> 25.4 us  [tp_reduce_scatter(): arrived = lax.all_to_all(chunks, 'tp', 0, 0, tiled=True)]
  transfers between devices with their start and end apart: 4 -> 6, of which waited for: 4 -> 6; matrix products, arithmetic and copies ran while one was open for 1% -> 3% of each run, Pallas kernels for 0% -> 0%
where the time goes in v1:
time: 361 us; the launch traced here: 360 us
  waiting for transfers between devices  149 us (41%)
  blocking collectives  106 us (29%)
  local copies, waits for them, and re-layouts  33.6 us (9%)
  starting transfers between devices  31.6 us (9%)
  matrix products  26.2 us (7%)
  other arithmetic  12.8 us (4%)
    all_to_all x1, blocking collectives, per_device(): lax.all_to_all(outgoing, 'req', split_axis=0, concat_axis=0, tiled=True)  80.5 us
    all_to_all x1, waiting for transfers between devices, send_back(): return lax.all_to_all(parts, 'req', split_axis=0, concat_axis=0, tiled=True)  71.9 us
    all_to_all x1, waiting for transfers between devices, fetch_prefixes(): arrived = lax.all_to_all(outgoing, 'req', 0, 0, tiled=True)  27.6 us
    all_to_all x1, blocking collectives, tp_reduce_scatter(): arrived = lax.all_to_all(chunks, 'tp', 0, 0, tiled=True)  25.4 us
    all_to_all x1, waiting for transfers between devices, tp_reduce_scatter(): arrived = lax.all_to_all(chunks, 'tp', 0, 0, tiled=True)  17.9 us
    all_to_all x1, waiting for transfers between devices, fetch_prefixes(): scattered = lax.all_to_all(pieces, 'req', 0, 0, tiled=True)  14.5 us
    all_to_all x1, waiting for transfers between devices, tp_all_gather(): arrived = lax.all_to_all(copies, 'tp', 0, 0, tiled=True)  13.7 us
    dot_general x1, matrix products, expert_apply(): jnp.dot(hidden_units, w_down[0], preferred_element_type=jnp.float32)  10.2 us
  transfers between devices with their start and end apart: 6, of which 6 were waited for; matrix products, arithmetic and copies ran while one was open for 3% of the time, Pallas kernels for 0%

profile of v1, /device:TPU:2, one launch (start us, length us, event | category | flops | bytes accessed | tf_op | source)
XLA Modules:
  0.0 359.7 jit_solution(14104327581540325932)
XLA Ops:
  1.4 7.6 %all-to-all-start = ((s32[32,1,2]{2,1,0:T(1,128)}), s32[32,1,2]{2,1,0:T(1,128)S(1)}, u32[]{:S(2)}, u32[]{:S(2)}) async-start(s32[32,1,2]{2,1,0:T(1,128)} %broadcast_in_dim.50), calls=%async_computation | async-start | bytes 32768 | tf_op jit(solution)/shard_map/all_to_all | solution.py:29
  9.1 2.5 copy.155
  11.6 3.6 all-to-all-done
  15.1 5.0 %all-to-all-start.1 = ((bf16[32,64,2,128]{3,1,2,0:T(8,128)(2,1)}), bf16[32,64,2,128]{3,1,2,0:T(8,128)(2,1)S(1)}, u32[]{:S(2)}, u32[]{:S(2)}) async-start(bf16[32,64,2,128]{3,1,2,0:T(8,128)(2,1)} %copy.155), calls=%async_computation.1 | async-start | bytes 2097152 | tf_op jit(solution)/shard_map/all_to_all | solution.py:27
  21.8 14.5 %all-to-all-done.1 = bf16[32,64,2,128]{3,1,2,0:T(8,128)(2,1)S(1)} async-done(((bf16[32,64,2,128]{3,1,2,0:T(8,128)(2,1)}), bf16[32,64,2,128]{3,1,2,0:T(8,128)(2,1)S(1)}, u32[]{:S(2)}, u32[]{:S(2)}) %all-to-all-start.1) | async-done | bytes 1048608 | tf_op jit(solution)/shard_map/all_to_all | solution.py:27
  39.1 3.2 broadcast_select_fusion
  42.3 5.9 %all-to-all-start.2 = ((bf16[32,2,64,2,128]{4,2,3,1,0:T(8,128)(2,1)}), bf16[32,2,64,2,128]{4,2,3,1,0:T(8,128)(2,1)}, u32[]{:S(2)}, u32[]{:S(2)}) async-start(bf16[32,2,64,2,128]{4,2,3,1,0:T(8,128)(2,1)} %broadcast_select_fusion), calls=%async_computation.2 | async-start | bytes 4194304 | tf_op jit(solution)/shard_map/all_to_all | solution.py:35
  48.7 27.6 %all-to-all-done.2 = bf16[32,2,64,2,128]{4,2,3,1,0:T(8,128)(2,1)} async-done(((bf16[32,2,64,2,128]{4,2,3,1,0:T(8,128)(2,1)}), bf16[32,2,64,2,128]{4,2,3,1,0:T(8,128)(2,1)}, u32[]{:S(2)}, u32[]{:S(2)}) %all-to-all-start.2) | async-done | bytes 2097184 | tf_op jit(solution)/shard_map/all_to_all | solution.py:35
  82.2 25.4 %all_to_all.41 = bf16[8,64,512]{2,1,0:T(8,128)(2,1)S(1)} all-to-all(bf16[8,64,512]{2,1,0:T(8,128)(2,1)S(1)} %bitcast.134), channel_id=1, replica_groups=mesh['req'=32,'tp'=8] {'tp'}, dimensions={0} | all-to-all | bytes 1048576 | tf_op jit(solution)/shard_map/all_to_all | solution.py:45
  108.5 3.5 all-to-all-start.4
  114.0 13.7 %all-to-all-done.4 = bf16[8,64,512]{2,1,0:T(8,128)(2,1)S(1)} async-done(((bf16[8,64,512]{2,1,0:T(8,128)(2,1)}), bf16[8,64,512]{2,1,0:T(8,128)(2,1)S(1)}, u32[]{:S(2)}, u32[]{:S(2)}) %all-to-all-start.4) | async-done | bytes 524320 | tf_op jit(solution)/shard_map/all_to_all | solution.py:52
  130.9 2.4 tile.10
  133.3 2.2 tile.11
  135.4 80.5 %all_to_all.42 = bf16[32,18,4096]{2,1,0:T(8,128)(2,1)} all-to-all(bf16[32,18,4096]{2,1,0:T(8,128)(2,1)S(1)} %bitcast.125), channel_id=1, replica_groups=mesh['req'=32,'tp'=8] {'req'}, dimensions={0} | all-to-all | bytes 9437184 | tf_op jit(solution)/shard_map/all_to_all | solution.py:190
  215.9 7.8 %reshape.267 = bf16[576,4096]{1,0:T(8,128)(2,1)} reshape(bf16[32,18,4096]{2,1,0:T(8,128)(2,1)} %all_to_all.42) | data formatting | bytes 9437184 | tf_op jit(solution)/shard_map/reshape | solution.py:125
  223.7 5.2 %fusion.5 = f32[576,256]{1,0:T(8,128)} fusion(bf16[576,4096]{1,0:T(8,128)(2,1)} %reshape.267, bf16[1,4096,256]{2,1,0:T(8,128)(2,1)} %param.24), kind=kOutput, calls=%fused_computation.13 | convolution fusion | flops 1207959552 | bytes 7405568 | tf_op jit(solution)/shard_map/dot_general | solution.py:126
  228.9 10.2 %convolution_convert_fusion = bf16[576,4096]{1,0:T(8,128)(2,1)} fusion(bf16[1,256,4096]{2,1,0:T(8,128)(2,1)S(1)} %copy-done, bf16[576,4096]{1,0:T(8,128)(2,1)} %reshape.267, bf16[1,4096,256]{2,1,0:T(8,128)(2,1)} %param.25, f32[576,256]{1,0:T(8,128)} %fusion.5), kind=kOutput, calls=%fused_computation.3 | convolution fusion | flops 2419163136 | bytes 14221312 | tf_op jit(solution)/shard_map/dot_general | solution.py:129
  239.2 7.6 %reshape.268 = bf16[32,18,4096]{2,1,0:T(8,128)(2,1)} reshape(bf16[576,4096]{1,0:T(8,128)(2,1)} %convolution_convert_fusion) | data formatting | bytes 9437184 | tf_op jit(solution)/shard_map/reshape | solution.py:132
  246.8 6.1 %all-to-all-start.6 = ((bf16[32,18,4096]{2,1,0:T(8,128)(2,1)}), bf16[32,18,4096]{2,1,0:T(8,128)(2,1)}, u32[]{:S(2)}, u32[]{:S(2)}) async-start(bf16[32,18,4096]{2,1,0:T(8,128)(2,1)} %reshape.268), calls=%async_computation.6 | async-start | bytes 12582912 | tf_op jit(solution)/shard_map/all_to_all | solution.py:136
  256.3 71.9 %all-to-all-done.6 = bf16[32,18,4096]{2,1,0:T(8,128)(2,1)} async-done(((bf16[32,18,4096]{2,1,0:T(8,128)(2,1)}), bf16[32,18,4096]{2,1,0:T(8,128)(2,1)}, u32[]{:S(2)}, u32[]{:S(2)}) %all-to-all-start.6) | async-done | bytes 4718624 | tf_op jit(solution)/shard_map/all_to_all | solution.py:136
  328.2 4.3 %convert_reduce_fusion = f32[8,18,4096]{2,1,0:T(8,128)S(1)} fusion(bf16[4,8,18,4096]{3,2,1,0:T(8,128)(2,1)} %bitcast.49), kind=kLoop, calls=%fused_computation.2 | loop fusion | flops 4128768 | bytes 7077888 | tf_op jit(solution)/shard_map/reduce_sum | solution.py:196
  332.5 3.4 fusion
  336.7 3.5 all-to-all-start.7
  340.2 17.9 %all-to-all-done.7 = bf16[8,64,512]{2,1,0:T(8,128)(2,1)S(1)} async-done(((bf16[8,64,512]{2,1,0:T(8,128)(2,1)}), bf16[8,64,512]{2,1,0:T(8,128)(2,1)S(1)}, u32[]{:S(2)}, u32[]{:S(2)}) %all-to-all-start.7) | async-done | bytes 524320 | tf_op jit(solution)/shard_map/all_to_all | solution.py:45
  (85 shorter events, 23.8 us)
Async XLA Ops:
  0.0 228.9 %copy-start = (bf16[1,256,4096]{2,1,0:T(8,128)(2,1)S(1)}, bf16[1,256,4096]{2,1,0:T(8,128)(2,1)}, u32[]{:S(2)}) copy-start(bf16[1,256,4096]{2,1,0:T(8,128)(2,1)} %param.26) | copy-start | bytes 6291460
  1.4 13.7 %all-to-all-start = ((s32[32,1,2]{2,1,0:T(1,128)}), s32[32,1,2]{2,1,0:T(1,128)S(1)}, u32[]{:S(2)}, u32[]{:S(2)}) async-start(s32[32,1,2]{2,1,0:T(1,128)} %broadcast_in_dim.50), calls=%async_computation | async-start | bytes 32768 | tf_op jit(solution)/shard_map/all_to_all | solution.py:29
  9.0 11.1 %copy-start.8 = (s32[4]{0:T(128)S(1)}, s32[4]{0:T(128)}, u32[]{:S(2)}) copy-start(s32[4]{0:T(128)} %param.17) | copy-start | bytes 52
  15.1 21.1 %all-to-all-start.1 = ((bf16[32,64,2,128]{3,1,2,0:T(8,128)(2,1)}), bf16[32,64,2,128]{3,1,2,0:T(8,128)(2,1)S(1)}, u32[]{:S(2)}, u32[]{:S(2)}) async-start(bf16[32,64,2,128]{3,1,2,0:T(8,128)(2,1)} %copy.155), calls=%async_computation.1 | async-start | bytes 2097152 | tf_op jit(solution)/shard_map/all_to_all | solution.py:27
  42.3 5.9 %copy-start.5 = (bf16[64,512]{1,0:T(8,128)(2,1)S(1)}, bf16[64,512]{1,0:T(8,128)(2,1)}, u32[]{:S(2)}) copy-start(bf16[64,512]{1,0:T(8,128)(2,1)} %param.14) | copy-start | bytes 196612
  42.3 6.0 %copy-start.6 = (bf16[64,2,128]{2,1,0:T(2,128)(2,1)S(1)}, bf16[64,2,128]{2,1,0:T(2,128)(2,1)}, u32[]{:S(2)}) copy-start(bf16[64,2,128]{2,1,0:T(2,128)(2,1)} %param.15) | copy-start | bytes 98308
  42.3 6.0 %copy-start.9 = (s32[2]{0:T(128)S(1)}, s32[2]{0:T(128)}, u32[]{:S(2)}) copy-start(s32[2]{0:T(128)} %param.19) | copy-start | bytes 28
  42.3 34.0 %all-to-all-start.2 = ((bf16[32,2,64,2,128]{4,2,3,1,0:T(8,128)(2,1)}), bf16[32,2,64,2,128]{4,2,3,1,0:T(8,128)(2,1)}, u32[]{:S(2)}, u32[]{:S(2)}) async-start(bf16[32,2,64,2,128]{4,2,3,1,0:T(8,128)(2,1)} %broadcast_select_fusion), calls=%async_computation.2 | async-start | bytes 4194304 | tf_op jit(solution)/shard_map/all_to_all | solution.py:35
  79.1 2.2 copy-start.2
  82.1 29.9 %copy-start.7 = (s32[64,2]{0,1:T(2,128)S(1)}, s32[64,2]{0,1:T(2,128)}, u32[]{:S(2)}) copy-start(s32[64,2]{0,1:T(2,128)} %param.23) | copy-start | bytes 1540
  108.5 19.2 %all-to-all-start.4 = ((bf16[8,64,512]{2,1,0:T(8,128)(2,1)}), bf16[8,64,512]{2,1,0:T(8,128)(2,1)S(1)}, u32[]{:S(2)}, u32[]{:S(2)}) async-start(bf16[8,64,512]{2,1,0:T(8,128)(2,1)} %broadcast_in_dim.89), calls=%async_computation.4 | async-start | bytes 1048576 | tf_op jit(solution)/shard_map/all_to_all | solution.py:52
  127.8 1.5 copy-start.1
  127.8 1.5 copy-start.4
  246.8 6.1 %copy-start.3 = (f32[4096,8]{0,1:T(8,128)S(1)}, f32[4096,8]{0,1:T(8,128)}, u32[]{:S(2)}) copy-start(f32[4096,8]{0,1:T(8,128)} %param.22) | copy-start | bytes 393220
  246.8 81.4 %all-to-all-start.6 = ((bf16[32,18,4096]{2,1,0:T(8,128)(2,1)}), bf16[32,18,4096]{2,1,0:T(8,128)(2,1)}, u32[]{:S(2)}, u32[]{:S(2)}) async-start(bf16[32,18,4096]{2,1,0:T(8,128)(2,1)} %reshape.268), calls=%async_computation.6 | async-start | bytes 12582912 | tf_op jit(solution)/shard_map/all_to_all | solution.py:136
  336.7 21.4 %all-to-all-start.7 = ((bf16[8,64,512]{2,1,0:T(8,128)(2,1)}), bf16[8,64,512]{2,1,0:T(8,128)(2,1)S(1)}, u32[]{:S(2)}, u32[]{:S(2)}) async-start(bf16[8,64,512]{2,1,0:T(8,128)(2,1)} %bitcast.122), calls=%async_computation.7 | async-start | bytes 1048576 | tf_op jit(solution)/shard_map/all_to_all | solution.py:45

commit v2 on v1

--- a/solution.py
+++ b/solution.py
@@ -11,6 +11,7 @@
 EXPERTS = 8
 NPFX = 4
 CAP = 18
+LANES = 128
 
 
 def broadcast(x, axis, root):
@@ -122,14 +123,14 @@
 
 
 def expert_apply(arrived, w_gate, w_up, w_down):
-    flat_rows = arrived.reshape(-1, arrived.shape[2])
+    flat_rows = arrived.reshape(-1, w_gate.shape[1])
     gate_value = jnp.dot(flat_rows, w_gate[0], preferred_element_type=jnp.float32)
     up_value = jnp.dot(flat_rows, w_up[0], preferred_element_type=jnp.float32)
     hidden_units = (jax.nn.silu(gate_value) * up_value).astype(jnp.bfloat16)
     piece_out = jnp.dot(hidden_units, w_down[0], preferred_element_type=jnp.float32).astype(
         jnp.bfloat16
     )
-    return piece_out.reshape(arrived.shape[0], arrived.shape[1], piece_out.shape[1])
+    return piece_out.reshape(arrived.shape)
 
 
 def send_back(parts):
@@ -184,7 +185,8 @@
     send_rows = jnp.dot(placing, normed_full, preferred_element_type=jnp.float32).astype(
         jnp.bfloat16
     )
-    outgoing = jnp.tile(send_rows.reshape(EXPERTS, CAP, model_width), (repeats, 1, 1))
+    packed_rows = CAP * model_width // LANES
+    outgoing = jnp.tile(send_rows.reshape(EXPERTS, packed_rows, LANES), (repeats, 1, 1))
     returned = send_back(
         expert_apply(
             lax.all_to_all(outgoing, "req", split_axis=0, concat_axis=0, tiled=True),
@@ -193,7 +195,7 @@
             w_down,
         )
     )
-    summed = returned.astype(jnp.float32).reshape(repeats, EXPERTS, CAP, model_width).sum(axis=0)
+    summed = returned.astype(jnp.float32).reshape(repeats, EXPERTS, packed_rows, LANES).sum(axis=0)
     mixture_full = jnp.dot(
         combining, summed.reshape(EXPERTS * CAP, model_width), precision=lax.Precision.HIGHEST
     )

time: 361 us -> 332 us (0.920)
  waiting for transfers between devices: 149 us -> 131 us
  blocking collectives: 106 us -> 89 us
  local copies, waits for them, and re-layouts: 33.6 us -> 38.9 us
    all_to_all x1, waiting for transfers between devices: 71.9 us -> 53.8 us  [send_back(): return lax.all_to_all(parts, 'req', split_axis=0, concat_axis=0, tiled=True)]
    all_to_all x1, blocking collectives: 80.5 us -> 63.6 us  [per_device(): lax.all_to_all(outgoing, 'req', split_axis=0, concat_axis=0, tiled=True)]
    reshape x2 -> x4, local copies, waits for them, and re-layouts: 15.4 us -> 19.9 us  [the longest x1 8.28 us: expert_apply(): return piece_out.reshape(arrived.shape)]
where the time goes in v2:
time: 332 us; the launch traced here: 330 us
  waiting for transfers between devices  131 us (39%)
  blocking collectives  89 us (27%)
  local copies, waits for them, and re-layouts  38.9 us (12%)
  starting transfers between devices  31.6 us (10%)
  matrix products  25.7 us (8%)
  other arithmetic  13.4 us (4%)
    all_to_all x1, blocking collectives, per_device(): lax.all_to_all(outgoing, 'req', split_axis=0, concat_axis=0, tiled=True)  63.6 us
    all_to_all x1, waiting for transfers between devices, send_back(): return lax.all_to_all(parts, 'req', split_axis=0, concat_axis=0, tiled=True)  53.8 us
    all_to_all x1, waiting for transfers between devices, fetch_prefixes(): arrived = lax.all_to_all(outgoing, 'req', 0, 0, tiled=True)  27.6 us
    all_to_all x1, blocking collectives, tp_reduce_scatter(): arrived = lax.all_to_all(chunks, 'tp', 0, 0, tiled=True)  25.4 us
    all_to_all x1, waiting for transfers between devices, tp_reduce_scatter(): arrived = lax.all_to_all(chunks, 'tp', 0, 0, tiled=True)  17.7 us
    all_to_all x1, waiting for transfers between devices, fetch_prefixes(): scattered = lax.all_to_all(pieces, 'req', 0, 0, tiled=True)  14.5 us
    all_to_all x1, waiting for transfers between devices, tp_all_gather(): arrived = lax.all_to_all(copies, 'tp', 0, 0, tiled=True)  13.7 us
    dot_general x1, matrix products, expert_apply(): jnp.dot(hidden_units, w_down[0], preferred_element_type=jnp.float32)  10.2 us
  transfers between devices with their start and end apart: 6, of which 6 were waited for; matrix products, arithmetic and copies ran while one was open for 3% of the time, Pallas kernels for 0%

profile of v2, /device:TPU:2, one launch (start us, length us, event | category | flops | bytes accessed | tf_op | source)
XLA Modules:
  0.0 329.9 jit_solution(4508904027752959709)
XLA Ops:
  1.4 7.6 %all-to-all-start = ((s32[32,1,2]{2,1,0:T(1,128)}), s32[32,1,2]{2,1,0:T(1,128)S(1)}, u32[]{:S(2)}, u32[]{:S(2)}) async-start(s32[32,1,2]{2,1,0:T(1,128)} %broadcast_in_dim.50), calls=%async_computation | async-start | bytes 32768 | tf_op jit(solution)/shard_map/all_to_all | solution.py:30
  9.1 2.5 copy.156
  11.6 3.6 %all-to-all-done = s32[32,1,2]{2,1,0:T(1,128)S(1)} async-done(((s32[32,1,2]{2,1,0:T(1,128)}), s32[32,1,2]{2,1,0:T(1,128)S(1)}, u32[]{:S(2)}, u32[]{:S(2)}) %all-to-all-start) | async-done | bytes 288 | tf_op jit(solution)/shard_map/all_to_all | solution.py:30
  15.1 5.0 %all-to-all-start.1 = ((bf16[32,64,2,128]{3,1,2,0:T(8,128)(2,1)}), bf16[32,64,2,128]{3,1,2,0:T(8,128)(2,1)S(1)}, u32[]{:S(2)}, u32[]{:S(2)}) async-start(bf16[32,64,2,128]{3,1,2,0:T(8,128)(2,1)} %copy.156), calls=%async_computation.1 | async-start | bytes 2097152 | tf_op jit(solution)/shard_map/all_to_all | solution.py:28
  21.8 14.5 %all-to-all-done.1 = bf16[32,64,2,128]{3,1,2,0:T(8,128)(2,1)S(1)} async-done(((bf16[32,64,2,128]{3,1,2,0:T(8,128)(2,1)}), bf16[32,64,2,128]{3,1,2,0:T(8,128)(2,1)S(1)}, u32[]{:S(2)}, u32[]{:S(2)}) %all-to-all-start.1) | async-done | bytes 1048608 | tf_op jit(solution)/shard_map/all_to_all | solution.py:28
  39.1 3.2 broadcast_select_fusion
  42.3 5.9 %all-to-all-start.2 = ((bf16[32,2,64,2,128]{4,2,3,1,0:T(8,128)(2,1)}), bf16[32,2,64,2,128]{4,2,3,1,0:T(8,128)(2,1)}, u32[]{:S(2)}, u32[]{:S(2)}) async-start(bf16[32,2,64,2,128]{4,2,3,1,0:T(8,128)(2,1)} %broadcast_select_fusion), calls=%async_computation.2 | async-start | bytes 4194304 | tf_op jit(solution)/shard_map/all_to_all | solution.py:36
  48.7 27.6 %all-to-all-done.2 = bf16[32,2,64,2,128]{4,2,3,1,0:T(8,128)(2,1)} async-done(((bf16[32,2,64,2,128]{4,2,3,1,0:T(8,128)(2,1)}), bf16[32,2,64,2,128]{4,2,3,1,0:T(8,128)(2,1)}, u32[]{:S(2)}, u32[]{:S(2)}) %all-to-all-start.2) | async-done | bytes 2097184 | tf_op jit(solution)/shard_map/all_to_all | solution.py:36
  82.2 25.4 %all_to_all.41 = bf16[8,64,512]{2,1,0:T(8,128)(2,1)S(1)} all-to-all(bf16[8,64,512]{2,1,0:T(8,128)(2,1)S(1)} %bitcast.130), channel_id=1, replica_groups=mesh['req'=32,'tp'=8] {'tp'}, dimensions={0} | all-to-all | bytes 1048576 | tf_op jit(solution)/shard_map/all_to_all | solution.py:46
  108.5 3.5 %all-to-all-start.4 = ((bf16[8,64,512]{2,1,0:T(8,128)(2,1)}), bf16[8,64,512]{2,1,0:T(8,128)(2,1)S(1)}, u32[]{:S(2)}, u32[]{:S(2)}) async-start(bf16[8,64,512]{2,1,0:T(8,128)(2,1)} %broadcast_in_dim.89), calls=%async_computation.4 | async-start | bytes 1048576 | tf_op jit(solution)/shard_map/all_to_all | solution.py:53
  114.0 13.7 %all-to-all-done.4 = bf16[8,64,512]{2,1,0:T(8,128)(2,1)S(1)} async-done(((bf16[8,64,512]{2,1,0:T(8,128)(2,1)}), bf16[8,64,512]{2,1,0:T(8,128)(2,1)S(1)}, u32[]{:S(2)}, u32[]{:S(2)}) %all-to-all-start.4) | async-done | bytes 524320 | tf_op jit(solution)/shard_map/all_to_all | solution.py:53
  130.9 3.1 tile.10
  136.3 63.6 %all_to_all.42 = bf16[32,576,128]{2,1,0:T(8,128)(2,1)} all-to-all(bf16[32,576,128]{2,1,0:T(8,128)(2,1)S(1)} %bitcast.122), channel_id=1, replica_groups=mesh['req'=32,'tp'=8] {'req'}, dimensions={0} | all-to-all | bytes 9437184 | tf_op jit(solution)/shard_map/all_to_all | solution.py:192
  199.9 8.2 %reshape.272 = bf16[576,4096]{1,0:T(8,128)(2,1)} reshape(bf16[32,576,128]{2,1,0:T(8,128)(2,1)} %all_to_all.42) | data formatting | bytes 9437184 | tf_op jit(solution)/shard_map/reshape | solution.py:126
  208.0 5.2 %fusion.4 = f32[576,256]{1,0:T(8,128)} fusion(bf16[576,4096]{1,0:T(8,128)(2,1)} %reshape.272, bf16[1,4096,256]{2,1,0:T(8,128)(2,1)} %param.24), kind=kOutput, calls=%fused_computation.12 | convolution fusion | flops 1207959552 | bytes 7405568 | tf_op jit(solution)/shard_map/dot_general | solution.py:127
  213.3 10.2 %convolution_convert_fusion = bf16[576,4096]{1,0:T(8,128)(2,1)} fusion(bf16[1,256,4096]{2,1,0:T(8,128)(2,1)S(1)} %copy-done, bf16[576,4096]{1,0:T(8,128)(2,1)} %reshape.272, bf16[1,4096,256]{2,1,0:T(8,128)(2,1)} %param.25, f32[576,256]{1,0:T(8,128)} %fusion.4), kind=kOutput, calls=%fused_computation.3 | convolution fusion | flops 2419163136 | bytes 14221312 | tf_op jit(solution)/shard_map/dot_general | solution.py:130
  223.5 8.3 %reshape.273 = bf16[32,576,128]{2,1,0:T(8,128)(2,1)} reshape(bf16[576,4096]{1,0:T(8,128)(2,1)} %convolution_convert_fusion) | data formatting | bytes 9437184 | tf_op jit(solution)/shard_map/reshape | solution.py:133
  231.7 6.0 %all-to-all-start.6 = ((bf16[32,576,128]{2,1,0:T(8,128)(2,1)}), bf16[32,576,128]{2,1,0:T(8,128)(2,1)}, u32[]{:S(2)}, u32[]{:S(2)}) async-start(bf16[32,576,128]{2,1,0:T(8,128)(2,1)} %reshape.273), calls=%async_computation.6 | async-start | bytes 9437184 | tf_op jit(solution)/shard_map/all_to_all | solution.py:137
  241.3 53.8 %all-to-all-done.6 = bf16[32,576,128]{2,1,0:T(8,128)(2,1)} async-done(((bf16[32,576,128]{2,1,0:T(8,128)(2,1)}), bf16[32,576,128]{2,1,0:T(8,128)(2,1)}, u32[]{:S(2)}, u32[]{:S(2)}) %all-to-all-start.6) | async-done | bytes 4718624 | tf_op jit(solution)/shard_map/all_to_all | solution.py:137
  295.1 4.8 %convert_reduce_fusion = f32[8,576,128]{2,1,0:T(8,128)} fusion(bf16[4,8,576,128]{3,2,1,0:T(8,128)(2,1)} %bitcast.48), kind=kLoop, calls=%fused_computation.2 | loop fusion | flops 4128768 | bytes 7077888 | tf_op jit(solution)/shard_map/reduce_sum | solution.py:198
  299.9 3.4 %reshape.276 = f32[144,4096]{1,0:T(8,128)} reshape(f32[8,576,128]{2,1,0:T(8,128)} %convert_reduce_fusion) | data formatting | bytes 4718592 | tf_op jit(solution)/shard_map/reshape | solution.py:200
  303.3 3.0 convolution_convert_fusion.3
  307.2 3.5 %all-to-all-start.7 = ((bf16[8,64,512]{2,1,0:T(8,128)(2,1)}), bf16[8,64,512]{2,1,0:T(8,128)(2,1)S(1)}, u32[]{:S(2)}, u32[]{:S(2)}) async-start(bf16[8,64,512]{2,1,0:T(8,128)(2,1)} %bitcast.119), calls=%async_computation.7 | async-start | bytes 1048576 | tf_op jit(solution)/shard_map/all_to_all | solution.py:46
  310.7 17.7 %all-to-all-done.7 = bf16[8,64,512]{2,1,0:T(8,128)(2,1)S(1)} async-done(((bf16[8,64,512]{2,1,0:T(8,128)(2,1)}), bf16[8,64,512]{2,1,0:T(8,128)(2,1)S(1)}, u32[]{:S(2)}, u32[]{:S(2)}) %all-to-all-start.7) | async-done | bytes 524320 | tf_op jit(solution)/shard_map/all_to_all | solution.py:46
  (87 shorter events, 26.2 us)
Async XLA Ops:
  0.0 213.3 %copy-start = (bf16[1,256,4096]{2,1,0:T(8,128)(2,1)S(1)}, bf16[1,256,4096]{2,1,0:T(8,128)(2,1)}, u32[]{:S(2)}) copy-start(bf16[1,256,4096]{2,1,0:T(8,128)(2,1)} %param.26) | copy-start | bytes 6291460
  1.4 13.7 %all-to-all-start = ((s32[32,1,2]{2,1,0:T(1,128)}), s32[32,1,2]{2,1,0:T(1,128)S(1)}, u32[]{:S(2)}, u32[]{:S(2)}) async-start(s32[32,1,2]{2,1,0:T(1,128)} %broadcast_in_dim.50), calls=%async_computation | async-start | bytes 32768 | tf_op jit(solution)/shard_map/all_to_all | solution.py:30
  9.0 11.1 %copy-start.8 = (s32[4]{0:T(128)S(1)}, s32[4]{0:T(128)}, u32[]{:S(2)}) copy-start(s32[4]{0:T(128)} %param.17) | copy-start | bytes 52
  15.1 21.1 %all-to-all-start.1 = ((bf16[32,64,2,128]{3,1,2,0:T(8,128)(2,1)}), bf16[32,64,2,128]{3,1,2,0:T(8,128)(2,1)S(1)}, u32[]{:S(2)}, u32[]{:S(2)}) async-start(bf16[32,64,2,128]{3,1,2,0:T(8,128)(2,1)} %copy.156), calls=%async_computation.1 | async-start | bytes 2097152 | tf_op jit(solution)/shard_map/all_to_all | solution.py:28
  42.3 5.9 %copy-start.5 = (bf16[64,512]{1,0:T(8,128)(2,1)S(1)}, bf16[64,512]{1,0:T(8,128)(2,1)}, u32[]{:S(2)}) copy-start(bf16[64,512]{1,0:T(8,128)(2,1)} %param.14) | copy-start | bytes 196612
  42.3 6.0 %copy-start.6 = (bf16[64,2,128]{2,1,0:T(2,128)(2,1)S(1)}, bf16[64,2,128]{2,1,0:T(2,128)(2,1)}, u32[]{:S(2)}) copy-start(bf16[64,2,128]{2,1,0:T(2,128)(2,1)} %param.15) | copy-start | bytes 98308
  42.3 6.0 %copy-start.9 = (s32[2]{0:T(128)S(1)}, s32[2]{0:T(128)}, u32[]{:S(2)}) copy-start(s32[2]{0:T(128)} %param.19) | copy-start | bytes 28
  42.3 34.0 %all-to-all-start.2 = ((bf16[32,2,64,2,128]{4,2,3,1,0:T(8,128)(2,1)}), bf16[32,2,64,2,128]{4,2,3,1,0:T(8,128)(2,1)}, u32[]{:S(2)}, u32[]{:S(2)}) async-start(bf16[32,2,64,2,128]{4,2,3,1,0:T(8,128)(2,1)} %broadcast_select_fusion), calls=%async_computation.2 | async-start | bytes 4194304 | tf_op jit(solution)/shard_map/all_to_all | solution.py:36
  79.1 2.2 copy-start.2
  82.1 30.1 %copy-start.7 = (s32[64,2]{0,1:T(2,128)S(1)}, s32[64,2]{0,1:T(2,128)}, u32[]{:S(2)}) copy-start(s32[64,2]{0,1:T(2,128)} %param.23) | copy-start | bytes 1540
  108.5 19.2 %all-to-all-start.4 = ((bf16[8,64,512]{2,1,0:T(8,128)(2,1)}), bf16[8,64,512]{2,1,0:T(8,128)(2,1)S(1)}, u32[]{:S(2)}, u32[]{:S(2)}) async-start(bf16[8,64,512]{2,1,0:T(8,128)(2,1)} %broadcast_in_dim.89), calls=%async_computation.4 | async-start | bytes 1048576 | tf_op jit(solution)/shard_map/all_to_all | solution.py:53
  127.8 1.5 copy-start.1
  127.8 1.5 copy-start.4
  231.7 6.0 %copy-start.3 = (f32[4096,8]{0,1:T(8,128)S(1)}, f32[4096,8]{0,1:T(8,128)}, u32[]{:S(2)}) copy-start(f32[4096,8]{0,1:T(8,128)} %param.22) | copy-start | bytes 393220
  231.7 63.4 %all-to-all-start.6 = ((bf16[32,576,128]{2,1,0:T(8,128)(2,1)}), bf16[32,576,128]{2,1,0:T(8,128)(2,1)}, u32[]{:S(2)}, u32[]{:S(2)}) async-start(bf16[32,576,128]{2,1,0:T(8,128)(2,1)} %reshape.273), calls=%async_computation.6 | async-start | bytes 9437184 | tf_op jit(solution)/shard_map/all_to_all | solution.py:137
  307.2 21.2 %all-to-all-start.7 = ((bf16[8,64,512]{2,1,0:T(8,128)(2,1)}), bf16[8,64,512]{2,1,0:T(8,128)(2,1)S(1)}, u32[]{:S(2)}, u32[]{:S(2)}) async-start(bf16[8,64,512]{2,1,0:T(8,128)(2,1)} %bitcast.119), calls=%async_computation.7 | async-start | bytes 1048576 | tf_op jit(solution)/shard_map/all_to_all | solution.py:46

commit v3 on v2

--- a/solution.py
+++ b/solution.py
@@ -12,6 +12,7 @@
 NPFX = 4
 CAP = 18
 LANES = 128
+CHUNKS = 2
 
 
 def broadcast(x, axis, root):
@@ -182,23 +183,35 @@
     )
     placing, combining = routing_tables(routes, live_rows, route_weight)
     repeats = req_count // EXPERTS
-    send_rows = jnp.dot(placing, normed_full, preferred_element_type=jnp.float32).astype(
-        jnp.bfloat16
-    )
-    packed_rows = CAP * model_width // LANES
-    outgoing = jnp.tile(send_rows.reshape(EXPERTS, packed_rows, LANES), (repeats, 1, 1))
-    returned = send_back(
-        expert_apply(
-            lax.all_to_all(outgoing, "req", split_axis=0, concat_axis=0, tiled=True),
-            w_gate,
-            w_up,
-            w_down,
-        )
-    )
-    summed = returned.astype(jnp.float32).reshape(repeats, EXPERTS, packed_rows, LANES).sum(axis=0)
-    mixture_full = jnp.dot(
-        combining, summed.reshape(EXPERTS * CAP, model_width), precision=lax.Precision.HIGHEST
-    )
+    tokens = routes.shape[0]
+    chunk_slots = CAP // CHUNKS
+    packed_rows = chunk_slots * model_width // LANES
+    placing_blocks = placing.reshape(EXPERTS, CAP, tokens)
+    combining_blocks = combining.reshape(tokens, EXPERTS, CAP)
+    mixture_full = jnp.zeros((tokens, model_width), jnp.float32)
+    for chunk in range(CHUNKS):
+        slots = slice(chunk * chunk_slots, (chunk + 1) * chunk_slots)
+        chunk_placing = placing_blocks[:, slots].reshape(EXPERTS * chunk_slots, tokens)
+        send_rows = jnp.dot(chunk_placing, normed_full, preferred_element_type=jnp.float32).astype(
+            jnp.bfloat16
+        )
+        outgoing = jnp.tile(send_rows.reshape(EXPERTS, packed_rows, LANES), (repeats, 1, 1))
+        returned = send_back(
+            expert_apply(
+                lax.all_to_all(outgoing, "req", split_axis=0, concat_axis=0, tiled=True),
+                w_gate,
+                w_up,
+                w_down,
+            )
+        )
+        summed = returned.astype(jnp.float32).reshape(repeats, EXPERTS, packed_rows, LANES).sum(
+            axis=0
+        )
+        mixture_full = mixture_full + jnp.dot(
+            combining_blocks[:, :, slots].reshape(tokens, EXPERTS * chunk_slots),
+            summed.reshape(EXPERTS * chunk_slots, model_width),
+            precision=lax.Precision.HIGHEST,
+        )
     mixture_share = tp_reduce_scatter(mixture_full, tp_count)
     layer_out = jnp.where(live_rows[:, None], hidden_share + mixture_share, 0.0)
     return layer_out.astype(jnp.bfloat16)

time: 332 us -> 326 us (0.982)
  blocking collectives: 89 us -> 0 us
  waiting for transfers between devices: 131 us -> 167 us
  starting transfers between devices: 31.6 us -> 62.1 us
  local copies, waits for them, and re-layouts: 38.9 us -> 48.2 us
  matrix products: 25.7 us -> 32.8 us
    all_to_all x2 -> x0, blocking collectives: 89 us -> none  [the longest x1 63.6 us: per_device(): lax.all_to_all(outgoing, 'req', split_axis=0, concat_axis=0, tiled=True)]
    all_to_all x0 -> x2, waiting for transfers between devices: none -> 37.4 us  [per_device(): lax.all_to_all(outgoing, 'req', split_axis=0, concat_axis=0, tiled=True)]
    all_to_all x1 -> x2, waiting for transfers between devices: 53.8 us -> 34.7 us  [send_back(): return lax.all_to_all(parts, 'req', split_axis=0, concat_axis=0, tiled=True)]
    all_to_all x1 -> x2, waiting for transfers between devices: 17.7 us -> 34.2 us  [tp_reduce_scatter(): arrived = lax.all_to_all(chunks, 'tp', 0, 0, tiled=True)]
    all_to_all x0 -> x2, starting transfers between devices: none -> 14.2 us  [per_device(): lax.all_to_all(outgoing, 'req', split_axis=0, concat_axis=0, tiled=True)]
    all_to_all x1 -> x2, starting transfers between devices: 3.49 us -> 12 us  [tp_reduce_scatter(): arrived = lax.all_to_all(chunks, 'tp', 0, 0, tiled=True)]
    all_to_all x1 -> x2, starting transfers between devices: 6.03 us -> 13.8 us  [send_back(): return lax.all_to_all(parts, 'req', split_axis=0, concat_axis=0, tiled=True)]
    another operation x2 -> x4, local copies, waits for them, and re-layouts: 5.38 us -> 9.91 us  [per_device(): jnp.tile(send_rows.reshape(EXPERTS, packed_rows, LANES), (repeats, 1, 1))]
  transfers between devices with their start and end apart: 6 -> 10, of which waited for: 6 -> 10; matrix products, arithmetic and copies ran while one was open for 3% -> 18% of each run, Pallas kernels for 0% -> 0%
where the time goes in v3:
time: 326 us; the launch traced here: 323 us
  waiting for transfers between devices  167 us (51%)
  starting transfers between devices  62.1 us (19%)
  local copies, waits for them, and re-layouts  48.2 us (15%)
  matrix products  32.8 us (10%)
  other arithmetic  13 us (4%)
    all_to_all x2, waiting for transfers between devices, per_device(): lax.all_to_all(outgoing, 'req', split_axis=0, concat_axis=0, tiled=True)  37.4 us
    all_to_all x2, waiting for transfers between devices, send_back(): return lax.all_to_all(parts, 'req', split_axis=0, concat_axis=0, tiled=True)  34.7 us
    all_to_all x2, waiting for transfers between devices, tp_reduce_scatter(): arrived = lax.all_to_all(chunks, 'tp', 0, 0, tiled=True)  34.2 us
    all_to_all x1, waiting for transfers between devices, fetch_prefixes(): arrived = lax.all_to_all(outgoing, 'req', 0, 0, tiled=True)  27.6 us
    all_to_all x1, waiting for transfers between devices, tp_all_gather(): arrived = lax.all_to_all(copies, 'tp', 0, 0, tiled=True)  14.9 us
    all_to_all x1, waiting for transfers between devices, fetch_prefixes(): scattered = lax.all_to_all(pieces, 'req', 0, 0, tiled=True)  14.5 us
    all_to_all x2, starting transfers between devices, per_device(): lax.all_to_all(outgoing, 'req', split_axis=0, concat_axis=0, tiled=True)  14.2 us
    all_to_all x2, starting transfers between devices, send_back(): return lax.all_to_all(parts, 'req', split_axis=0, concat_axis=0, tiled=True)  13.8 us
  transfers between devices with their start and end apart: 10, of which 10 were waited for; matrix products, arithmetic and copies ran while one was open for 18% of the time, Pallas kernels for 0%

profile of v3, /device:TPU:2, one launch (start us, length us, event | category | flops | bytes accessed | tf_op | source)
XLA Modules:
  0.0 323.5 jit_solution(11848088612416679355)
XLA Ops:
  1.4 7.6 %all-to-all-start = ((s32[32,1,2]{2,1,0:T(1,128)}), s32[32,1,2]{2,1,0:T(1,128)S(1)}, u32[]{:S(2)}, u32[]{:S(2)}) async-start(s32[32,1,2]{2,1,0:T(1,128)} %broadcast_in_dim.50), calls=%async_computation | async-start | bytes 32768 | tf_op jit(solution)/shard_map/all_to_all | solution.py:31
  15.1 5.0 %all-to-all-start.1 = ((bf16[32,64,2,128]{3,1,2,0:T(8,128)(2,1)}), bf16[32,64,2,128]{3,1,2,0:T(8,128)(2,1)S(1)}, u32[]{:S(2)}, u32[]{:S(2)}) async-start(bf16[32,64,2,128]{3,1,2,0:T(8,128)(2,1)} %copy.172), calls=%async_computation.1 | async-start | bytes 2097152 | tf_op jit(solution)/shard_map/all_to_all | solution.py:29
  21.8 14.5 %all-to-all-done.1 = bf16[32,64,2,128]{3,1,2,0:T(8,128)(2,1)S(1)} async-done(((bf16[32,64,2,128]{3,1,2,0:T(8,128)(2,1)}), bf16[32,64,2,128]{3,1,2,0:T(8,128)(2,1)S(1)}, u32[]{:S(2)}, u32[]{:S(2)}) %all-to-all-start.1) | async-done | bytes 1048608 | tf_op jit(solution)/shard_map/all_to_all | solution.py:29
  42.3 5.9 %all-to-all-start.2 = ((bf16[32,2,64,2,128]{4,2,3,1,0:T(8,128)(2,1)}), bf16[32,2,64,2,128]{4,2,3,1,0:T(8,128)(2,1)}, u32[]{:S(2)}, u32[]{:S(2)}) async-start(bf16[32,2,64,2,128]{4,2,3,1,0:T(8,128)(2,1)} %broadcast_select_fusion), calls=%async_computation.2 | async-start | bytes 4194304 | tf_op jit(solution)/shard_map/all_to_all | solution.py:37
  48.7 27.6 %all-to-all-done.2 = bf16[32,2,64,2,128]{4,2,3,1,0:T(8,128)(2,1)} async-done(((bf16[32,2,64,2,128]{4,2,3,1,0:T(8,128)(2,1)}), bf16[32,2,64,2,128]{4,2,3,1,0:T(8,128)(2,1)}, u32[]{:S(2)}, u32[]{:S(2)}) %all-to-all-start.2) | async-done | bytes 2097184 | tf_op jit(solution)/shard_map/all_to_all | solution.py:37
  83.0 8.5 %all-to-all-start.3 = ((bf16[8,64,512]{2,1,0:T(8,128)(2,1)}), bf16[8,64,512]{2,1,0:T(8,128)(2,1)S(1)}, u32[]{:S(2)}, u32[]{:S(2)}) async-start(bf16[8,64,512]{2,1,0:T(8,128)(2,1)} %bitcast.145), calls=%async_computation.3 | async-start | bytes 1048576 | tf_op jit(solution)/shard_map/all_to_all | solution.py:47
  91.6 17.0 %all-to-all-done.3 = bf16[8,64,512]{2,1,0:T(8,128)(2,1)S(1)} async-done(((bf16[8,64,512]{2,1,0:T(8,128)(2,1)}), bf16[8,64,512]{2,1,0:T(8,128)(2,1)S(1)}, u32[]{:S(2)}, u32[]{:S(2)}) %all-to-all-start.3) | async-done | bytes 524320 | tf_op jit(solution)/shard_map/all_to_all | solution.py:47
  114.9 14.9 %all-to-all-done.4 = bf16[8,64,512]{2,1,0:T(8,128)(2,1)S(1)} async-done(((bf16[8,64,512]{2,1,0:T(8,128)(2,1)}), bf16[8,64,512]{2,1,0:T(8,128)(2,1)S(1)}, u32[]{:S(2)}, u32[]{:S(2)}) %all-to-all-start.4) | async-done | bytes 524320 | tf_op jit(solution)/shard_map/all_to_all | solution.py:54
  138.6 7.3 %all-to-all-start.5 = ((bf16[32,288,128]{2,1,0:T(8,128)(2,1)}), bf16[32,288,128]{2,1,0:T(8,128)(2,1)}, u32[]{:S(2)}, u32[]{:S(2)}) async-start(bf16[32,288,128]{2,1,0:T(8,128)(2,1)} %bitcast.149), calls=%async_computation.5 | async-start | bytes 4718592 | tf_op jit(solution)/shard_map/all_to_all | solution.py:201
  150.3 26.5 %all-to-all-done.5 = bf16[32,288,128]{2,1,0:T(8,128)(2,1)} async-done(((bf16[32,288,128]{2,1,0:T(8,128)(2,1)}), bf16[32,288,128]{2,1,0:T(8,128)(2,1)}, u32[]{:S(2)}, u32[]{:S(2)}) %all-to-all-start.5) | async-done | bytes 2359328 | tf_op jit(solution)/shard_map/all_to_all | solution.py:201
  179.7 6.9 %all-to-all-start.7 = ((bf16[32,288,128]{2,1,0:T(8,128)(2,1)}), bf16[32,288,128]{2,1,0:T(8,128)(2,1)}, u32[]{:S(2)}, u32[]{:S(2)}) async-start(bf16[32,288,128]{2,1,0:T(8,128)(2,1)} %bitcast.150), calls=%async_computation.7 | async-start | bytes 4718592 | tf_op jit(solution)/shard_map/all_to_all | solution.py:201
  186.6 5.0 %reshape.301 = bf16[288,4096]{1,0:T(8,128)(2,1)} reshape(bf16[32,288,128]{2,1,0:T(8,128)(2,1)} %all-to-all-done.5) | data formatting | bytes 4718592 | tf_op jit(solution)/shard_map/reshape | solution.py:127
  191.6 3.8 %fusion.10 = f32[288,256]{1,0:T(8,128)} fusion(bf16[288,4096]{1,0:T(8,128)(2,1)} %reshape.301, bf16[1,4096,256]{2,1,0:T(8,128)(2,1)} %param.24), kind=kOutput, calls=%fused_computation.21 | convolution fusion | flops 603979776 | bytes 4751360 | tf_op jit(solution)/shard_map/dot_general | solution.py:128
  195.4 6.3 %convolution_convert_fusion.1 = bf16[288,4096]{1,0:T(8,128)(2,1)} fusion(bf16[1,256,4096]{2,1,0:T(8,128)(2,1)S(1)} %copy-done, bf16[288,4096]{1,0:T(8,128)(2,1)} %reshape.301, bf16[1,4096,256]{2,1,0:T(8,128)(2,1)} %param.25, f32[288,256]{1,0:T(8,128)} %fusion.10), kind=kOutput, calls=%fused_computation.3 | convolution fusion | flops 1209581568 | bytes 9207808 | tf_op jit(solution)/shard_map/dot_general | solution.py:131
  201.7 5.0 %reshape.302 = bf16[32,288,128]{2,1,0:T(8,128)(2,1)} reshape(bf16[288,4096]{1,0:T(8,128)(2,1)} %convolution_convert_fusion.1) | data formatting | bytes 4718592 | tf_op jit(solution)/shard_map/reshape | solution.py:134
  206.7 10.9 %all-to-all-done.7 = bf16[32,288,128]{2,1,0:T(8,128)(2,1)} async-done(((bf16[32,288,128]{2,1,0:T(8,128)(2,1)}), bf16[32,288,128]{2,1,0:T(8,128)(2,1)}, u32[]{:S(2)}, u32[]{:S(2)}) %all-to-all-start.7) | async-done | bytes 2359328 | tf_op jit(solution)/shard_map/all_to_all | solution.py:201
  217.6 6.9 %all-to-all-start.6 = ((bf16[32,288,128]{2,1,0:T(8,128)(2,1)}), bf16[32,288,128]{2,1,0:T(8,128)(2,1)}, u32[]{:S(2)}, u32[]{:S(2)}) async-start(bf16[32,288,128]{2,1,0:T(8,128)(2,1)} %reshape.302), calls=%async_computation.6 | async-start | bytes 4718592 | tf_op jit(solution)/shard_map/all_to_all | solution.py:138
  224.6 5.0 %reshape.308 = bf16[288,4096]{1,0:T(8,128)(2,1)} reshape(bf16[32,288,128]{2,1,0:T(8,128)(2,1)} %all-to-all-done.7) | data formatting | bytes 4718592 | tf_op jit(solution)/shard_map/reshape | solution.py:127
  233.3 6.3 %convolution_convert_fusion = bf16[288,4096]{1,0:T(8,128)(2,1)} fusion(bf16[1,256,4096]{2,1,0:T(8,128)(2,1)S(1)} %copy-done, bf16[288,4096]{1,0:T(8,128)(2,1)} %reshape.308, bf16[1,4096,256]{2,1,0:T(8,128)(2,1)} %param.25, f32[288,256]{1,0:T(8,128)} %fusion.8), kind=kOutput, calls=%fused_computation.2 | convolution fusion | flops 1209581568 | bytes 9207808 | tf_op jit(solution)/shard_map/dot_general | solution.py:131
  239.7 5.0 %reshape.309 = bf16[32,288,128]{2,1,0:T(8,128)(2,1)} reshape(bf16[288,4096]{1,0:T(8,128)(2,1)} %convolution_convert_fusion) | data formatting | bytes 4718592 | tf_op jit(solution)/shard_map/reshape | solution.py:134
  244.7 10.9 %all-to-all-done.6 = bf16[32,288,128]{2,1,0:T(8,128)(2,1)} async-done(((bf16[32,288,128]{2,1,0:T(8,128)(2,1)}), bf16[32,288,128]{2,1,0:T(8,128)(2,1)}, u32[]{:S(2)}, u32[]{:S(2)}) %all-to-all-start.6) | async-done | bytes 2359328 | tf_op jit(solution)/shard_map/all_to_all | solution.py:138
  255.6 6.9 %all-to-all-start.8 = ((bf16[32,288,128]{2,1,0:T(8,128)(2,1)}), bf16[32,288,128]{2,1,0:T(8,128)(2,1)}, u32[]{:S(2)}, u32[]{:S(2)}) async-start(bf16[32,288,128]{2,1,0:T(8,128)(2,1)} %reshape.309), calls=%async_computation.8 | async-start | bytes 4718592 | tf_op jit(solution)/shard_map/all_to_all | solution.py:138
  269.8 23.8 %all-to-all-done.8 = bf16[32,288,128]{2,1,0:T(8,128)(2,1)} async-done(((bf16[32,288,128]{2,1,0:T(8,128)(2,1)}), bf16[32,288,128]{2,1,0:T(8,128)(2,1)}, u32[]{:S(2)}, u32[]{:S(2)}) %all-to-all-start.8) | async-done | bytes 2359328 | tf_op jit(solution)/shard_map/all_to_all | solution.py:138
  304.7 17.2 %all-to-all-done.9 = bf16[8,64,512]{2,1,0:T(8,128)(2,1)S(1)} async-done(((bf16[8,64,512]{2,1,0:T(8,128)(2,1)}), bf16[8,64,512]{2,1,0:T(8,128)(2,1)S(1)}, u32[]{:S(2)}, u32[]{:S(2)}) %all-to-all-start.9) | async-done | bytes 524320 | tf_op jit(solution)/shard_map/all_to_all | solution.py:47
  (112 shorter events, 68.1 us)
Async XLA Ops:
  0.0 195.4 %copy-start = (bf16[1,256,4096]{2,1,0:T(8,128)(2,1)S(1)}, bf16[1,256,4096]{2,1,0:T(8,128)(2,1)}, u32[]{:S(2)}) copy-start(bf16[1,256,4096]{2,1,0:T(8,128)(2,1)} %param.26) | copy-start | bytes 6291460
  1.4 13.7 %all-to-all-start = ((s32[32,1,2]{2,1,0:T(1,128)}), s32[32,1,2]{2,1,0:T(1,128)S(1)}, u32[]{:S(2)}, u32[]{:S(2)}) async-start(s32[32,1,2]{2,1,0:T(1,128)} %broadcast_in_dim.50), calls=%async_computation | async-start | bytes 32768 | tf_op jit(solution)/shard_map/all_to_all | solution.py:31
  9.0 11.1 %copy-start.10 = (s32[4]{0:T(128)S(1)}, s32[4]{0:T(128)}, u32[]{:S(2)}) copy-start(s32[4]{0:T(128)} %param.17) | copy-start | bytes 52
  15.1 21.1 %all-to-all-start.1 = ((bf16[32,64,2,128]{3,1,2,0:T(8,128)(2,1)}), bf16[32,64,2,128]{3,1,2,0:T(8,128)(2,1)S(1)}, u32[]{:S(2)}, u32[]{:S(2)}) async-start(bf16[32,64,2,128]{3,1,2,0:T(8,128)(2,1)} %copy.172), calls=%async_computation.1 | async-start | bytes 2097152 | tf_op jit(solution)/shard_map/all_to_all | solution.py:29
  42.3 5.9 %copy-start.7 = (bf16[64,512]{1,0:T(8,128)(2,1)S(1)}, bf16[64,512]{1,0:T(8,128)(2,1)}, u32[]{:S(2)}) copy-start(bf16[64,512]{1,0:T(8,128)(2,1)} %param.14) | copy-start | bytes 196612
  42.3 6.0 %copy-start.8 = (bf16[64,2,128]{2,1,0:T(2,128)(2,1)S(1)}, bf16[64,2,128]{2,1,0:T(2,128)(2,1)}, u32[]{:S(2)}) copy-start(bf16[64,2,128]{2,1,0:T(2,128)(2,1)} %param.15) | copy-start | bytes 98308
  42.3 6.0 %copy-start.11 = (s32[2]{0:T(128)S(1)}, s32[2]{0:T(128)}, u32[]{:S(2)}) copy-start(s32[2]{0:T(128)} %param.19) | copy-start | bytes 28
  42.3 34.0 %all-to-all-start.2 = ((bf16[32,2,64,2,128]{4,2,3,1,0:T(8,128)(2,1)}), bf16[32,2,64,2,128]{4,2,3,1,0:T(8,128)(2,1)}, u32[]{:S(2)}, u32[]{:S(2)}) async-start(bf16[32,2,64,2,128]{4,2,3,1,0:T(8,128)(2,1)} %broadcast_select_fusion), calls=%async_computation.2 | async-start | bytes 4194304 | tf_op jit(solution)/shard_map/all_to_all | solution.py:37
  79.1 2.2 copy-start.4
  82.1 30.9 %copy-start.9 = (s32[64,2]{0,1:T(2,128)S(1)}, s32[64,2]{0,1:T(2,128)}, u32[]{:S(2)}) copy-start(s32[64,2]{0,1:T(2,128)} %param.23) | copy-start | bytes 1540
  83.0 25.6 %all-to-all-start.3 = ((bf16[8,64,512]{2,1,0:T(8,128)(2,1)}), bf16[8,64,512]{2,1,0:T(8,128)(2,1)S(1)}, u32[]{:S(2)}, u32[]{:S(2)}) async-start(bf16[8,64,512]{2,1,0:T(8,128)(2,1)} %bitcast.145), calls=%async_computation.3 | async-start | bytes 1048576 | tf_op jit(solution)/shard_map/all_to_all | solution.py:47
  109.5 20.4 %all-to-all-start.4 = ((bf16[8,64,512]{2,1,0:T(8,128)(2,1)}), bf16[8,64,512]{2,1,0:T(8,128)(2,1)S(1)}, u32[]{:S(2)}, u32[]{:S(2)}) async-start(bf16[8,64,512]{2,1,0:T(8,128)(2,1)} %broadcast_in_dim.89), calls=%async_computation.4 | async-start | bytes 1048576 | tf_op jit(solution)/shard_map/all_to_all | solution.py:54
  130.0 1.5 copy-start.1
  130.0 1.5 copy-start.6
  131.7 0.8 copy-start.2
  138.6 38.3 %all-to-all-start.5 = ((bf16[32,288,128]{2,1,0:T(8,128)(2,1)}), bf16[32,288,128]{2,1,0:T(8,128)(2,1)}, u32[]{:S(2)}, u32[]{:S(2)}) async-start(bf16[32,288,128]{2,1,0:T(8,128)(2,1)} %bitcast.149), calls=%async_computation.5 | async-start | bytes 4718592 | tf_op jit(solution)/shard_map/all_to_all | solution.py:201
  179.7 38.0 %all-to-all-start.7 = ((bf16[32,288,128]{2,1,0:T(8,128)(2,1)}), bf16[32,288,128]{2,1,0:T(8,128)(2,1)}, u32[]{:S(2)}, u32[]{:S(2)}) async-start(bf16[32,288,128]{2,1,0:T(8,128)(2,1)} %bitcast.150), calls=%async_computation.7 | async-start | bytes 4718592 | tf_op jit(solution)/shard_map/all_to_all | solution.py:201
  217.6 38.0 %all-to-all-start.6 = ((bf16[32,288,128]{2,1,0:T(8,128)(2,1)}), bf16[32,288,128]{2,1,0:T(8,128)(2,1)}, u32[]{:S(2)}, u32[]{:S(2)}) async-start(bf16[32,288,128]{2,1,0:T(8,128)(2,1)} %reshape.302), calls=%async_computation.6 | async-start | bytes 4718592 | tf_op jit(solution)/shard_map/all_to_all | solution.py:138
  244.7 17.9 %copy-start.5 = (f32[4096,8]{0,1:T(8,128)S(1)}, f32[4096,8]{0,1:T(8,128)}, u32[]{:S(2)}) copy-start(f32[4096,8]{0,1:T(8,128)} %param.22) | copy-start | bytes 393220
  255.6 38.0 %all-to-all-start.8 = ((bf16[32,288,128]{2,1,0:T(8,128)(2,1)}), bf16[32,288,128]{2,1,0:T(8,128)(2,1)}, u32[]{:S(2)}, u32[]{:S(2)}) async-start(bf16[32,288,128]{2,1,0:T(8,128)(2,1)} %reshape.309), calls=%async_computation.8 | async-start | bytes 4718592 | tf_op jit(solution)/shard_map/all_to_all | solution.py:138
  296.9 2.4 copy-start.3
  301.2 20.7 %all-to-all-start.9 = ((bf16[8,64,512]{2,1,0:T(8,128)(2,1)}), bf16[8,64,512]{2,1,0:T(8,128)(2,1)S(1)}, u32[]{:S(2)}, u32[]{:S(2)}) async-start(bf16[8,64,512]{2,1,0:T(8,128)(2,1)} %bitcast.143), calls=%async_computation.9 | async-start | bytes 1048576 | tf_op jit(solution)/shard_map/all_to_all | solution.py:47

commit v4 on v3

--- a/solution.py
+++ b/solution.py
@@ -188,7 +188,8 @@
     packed_rows = chunk_slots * model_width // LANES
     placing_blocks = placing.reshape(EXPERTS, CAP, tokens)
     combining_blocks = combining.reshape(tokens, EXPERTS, CAP)
-    mixture_full = jnp.zeros((tokens, model_width), jnp.float32)
+    share_rows = chunk_slots * share_width // LANES
+    mixture_share = jnp.zeros((tokens, share_width), jnp.float32)
     for chunk in range(CHUNKS):
         slots = slice(chunk * chunk_slots, (chunk + 1) * chunk_slots)
         chunk_placing = placing_blocks[:, slots].reshape(EXPERTS * chunk_slots, tokens)
@@ -196,23 +197,18 @@
             jnp.bfloat16
         )
         outgoing = jnp.tile(send_rows.reshape(EXPERTS, packed_rows, LANES), (repeats, 1, 1))
-        returned = send_back(
-            expert_apply(
-                lax.all_to_all(outgoing, "req", split_axis=0, concat_axis=0, tiled=True),
-                w_gate,
-                w_up,
-                w_down,
-            )
-        )
-        summed = returned.astype(jnp.float32).reshape(repeats, EXPERTS, packed_rows, LANES).sum(
+        arrived = lax.all_to_all(outgoing, "req", split_axis=0, concat_axis=0, tiled=True)
+        piece_out = expert_apply(arrived, w_gate, w_up, w_down).reshape(-1, model_width)
+        reduced = lax.psum_scatter(piece_out, "tp", scatter_dimension=1, tiled=True)
+        returned = send_back(reduced.reshape(req_count, share_rows, LANES))
+        summed = returned.astype(jnp.float32).reshape(repeats, EXPERTS, share_rows, LANES).sum(
             axis=0
         )
-        mixture_full = mixture_full + jnp.dot(
+        mixture_share = mixture_share + jnp.dot(
             combining_blocks[:, :, slots].reshape(tokens, EXPERTS * chunk_slots),
-            summed.reshape(EXPERTS * chunk_slots, model_width),
+            summed.reshape(EXPERTS * chunk_slots, share_width),
             precision=lax.Precision.HIGHEST,
         )
-    mixture_share = tp_reduce_scatter(mixture_full, tp_count)
     layer_out = jnp.where(live_rows[:, None], hidden_share + mixture_share, 0.0)
     return layer_out.astype(jnp.bfloat16)
 

time: 326 us -> 320 us (0.982)
  blocking collectives: 0 us -> 72.1 us
  waiting for transfers between devices: 167 us -> 110 us
  starting transfers between devices: 62.1 us -> 43.3 us
  between operations: 0.5 us -> 13.9 us
  local copies, waits for them, and re-layouts: 48.2 us -> 38.4 us
  other arithmetic: 13 us -> 7.18 us
    all_to_all x0 -> x2, blocking collectives: none -> 72.1 us  [per_device(): lax.all_to_all(outgoing, 'req', split_axis=0, concat_axis=0, tiled=True)]
    all_to_all x2 -> x0, waiting for transfers between devices: 37.4 us -> none  [per_device(): lax.all_to_all(outgoing, 'req', split_axis=0, concat_axis=0, tiled=True)]
    all_to_all x2, waiting for transfers between devices: 34.7 us -> 6.14 us  [send_back(): return lax.all_to_all(parts, 'req', split_axis=0, concat_axis=0, tiled=True)]
    reduce_scatter x0 -> x2, waiting for transfers between devices: none -> 25.8 us  [per_device(): reduced = lax.psum_scatter(piece_out, 'tp', scatter_dimension=1, tiled=True)]
    all_to_all x2 -> x1, waiting for transfers between devices: 34.2 us -> 17 us  [tp_reduce_scatter(): arrived = lax.all_to_all(chunks, 'tp', 0, 0, tiled=True)]
    all_to_all x2 -> x0, starting transfers between devices: 14.2 us -> none  [per_device(): lax.all_to_all(outgoing, 'req', split_axis=0, concat_axis=0, tiled=True)]
    reshape x4, local copies, waits for them, and re-layouts: 12.5 us -> 3.89 us  [the longest x2 3.84 us: per_device(): returned = send_back(reduced.reshape(req_count, share_rows, LANES))]
    reduce_sum x2, other arithmetic: 4.23 us -> 0.09 us  [per_device(): returned.astype(jnp.float32).reshape(repeats, EXPERTS, share_rows, LANES)]
  transfers between devices with their start and end apart: 10 -> 9, of which waited for: 10 -> 7; matrix products, arithmetic and copies ran while one was open for 18% -> 12% of each run, Pallas kernels for 0% -> 0%
where the time goes in v4:
time: 320 us; the launch traced here: 316 us
  waiting for transfers between devices  110 us (34%)
  blocking collectives  72.1 us (23%)
  starting transfers between devices  43.3 us (14%)
  local copies, waits for them, and re-layouts  38.4 us (12%)
  matrix products  31.4 us (10%)
  between operations  13.9 us (4%)
  other arithmetic  7.18 us (2%)
    all_to_all x2, blocking collectives, per_device(): lax.all_to_all(outgoing, 'req', split_axis=0, concat_axis=0, tiled=True)  72.1 us
    all_to_all x1, waiting for transfers between devices, fetch_prefixes(): arrived = lax.all_to_all(outgoing, 'req', 0, 0, tiled=True)  27.6 us
    reduce_scatter x2, waiting for transfers between devices, per_device(): reduced = lax.psum_scatter(piece_out, 'tp', scatter_dimension=1, tiled=True)  25.8 us
    all_to_all x1, waiting for transfers between devices, tp_reduce_scatter(): arrived = lax.all_to_all(chunks, 'tp', 0, 0, tiled=True)  17 us
    all_to_all x1, waiting for transfers between devices, tp_all_gather(): arrived = lax.all_to_all(copies, 'tp', 0, 0, tiled=True)  14.9 us
    all_to_all x1, waiting for transfers between devices, fetch_prefixes(): scattered = lax.all_to_all(pieces, 'req', 0, 0, tiled=True)  14.5 us
    dot_general x2, matrix products, expert_apply(): jnp.dot(hidden_units, w_down[0], preferred_element_type=jnp.float32)  12.7 us
    all_to_all x2, starting transfers between devices, send_back(): return lax.all_to_all(parts, 'req', split_axis=0, concat_axis=0, tiled=True)  12.5 us
  transfers between devices with their start and end apart: 9, of which 7 were waited for; matrix products, arithmetic and copies ran while one was open for 12% of the time, Pallas kernels for 0%

profile of v4, /device:TPU:2, one launch (start us, length us, event | category | flops | bytes accessed | tf_op | source)
XLA Modules:
  0.0 315.9 jit_solution(14106984748719827767)
XLA Ops:
  8.0 7.6 %all-to-all-start = ((s32[32,1,2]{2,1,0:T(1,128)}), s32[32,1,2]{2,1,0:T(1,128)S(1)}, u32[]{:S(2)}, u32[]{:S(2)}) async-start(s32[32,1,2]{2,1,0:T(1,128)} %broadcast_in_dim.50), calls=%async_computation | async-start | bytes 32768 | tf_op jit(solution)/shard_map/all_to_all | solution.py:31
  15.6 2.5 copy.168
  18.1 3.6 %all-to-all-done = s32[32,1,2]{2,1,0:T(1,128)S(1)} async-done(((s32[32,1,2]{2,1,0:T(1,128)}), s32[32,1,2]{2,1,0:T(1,128)S(1)}, u32[]{:S(2)}, u32[]{:S(2)}) %all-to-all-start) | async-done | bytes 288 | tf_op jit(solution)/shard_map/all_to_all | solution.py:31
  21.7 5.0 %all-to-all-start.1 = ((bf16[32,64,2,128]{3,1,2,0:T(8,128)(2,1)}), bf16[32,64,2,128]{3,1,2,0:T(8,128)(2,1)S(1)}, u32[]{:S(2)}, u32[]{:S(2)}) async-start(bf16[32,64,2,128]{3,1,2,0:T(8,128)(2,1)} %copy.168), calls=%async_computation.1 | async-start | bytes 2097152 | tf_op jit(solution)/shard_map/all_to_all | solution.py:29
  28.3 14.5 %all-to-all-done.1 = bf16[32,64,2,128]{3,1,2,0:T(8,128)(2,1)S(1)} async-done(((bf16[32,64,2,128]{3,1,2,0:T(8,128)(2,1)}), bf16[32,64,2,128]{3,1,2,0:T(8,128)(2,1)S(1)}, u32[]{:S(2)}, u32[]{:S(2)}) %all-to-all-start.1) | async-done | bytes 1048608 | tf_op jit(solution)/shard_map/all_to_all | solution.py:29
  45.6 3.2 %broadcast_select_fusion = bf16[32,2,64,2,128]{4,2,3,1,0:T(8,128)(2,1)} fusion(bf16[32,2,64,2,128]{4,2,3,1,0:T(8,128)(2,1)} %bitcast.144, pred[32,2]{1,0:T(8,128)(4,1)S(1)} %copy.166), kind=kLoop, calls=%fused_computation.21 | loop fusion | flops 1048576 | bytes 4194368 | tf_op jit(solution)/shard_map/jit(_take)/select_n | solution.py:34
  48.8 5.9 %all-to-all-start.2 = ((bf16[32,2,64,2,128]{4,2,3,1,0:T(8,128)(2,1)}), bf16[32,2,64,2,128]{4,2,3,1,0:T(8,128)(2,1)}, u32[]{:S(2)}, u32[]{:S(2)}) async-start(bf16[32,2,64,2,128]{4,2,3,1,0:T(8,128)(2,1)} %broadcast_select_fusion), calls=%async_computation.2 | async-start | bytes 4194304 | tf_op jit(solution)/shard_map/all_to_all | solution.py:37
  55.2 27.6 %all-to-all-done.2 = bf16[32,2,64,2,128]{4,2,3,1,0:T(8,128)(2,1)} async-done(((bf16[32,2,64,2,128]{4,2,3,1,0:T(8,128)(2,1)}), bf16[32,2,64,2,128]{4,2,3,1,0:T(8,128)(2,1)}, u32[]{:S(2)}, u32[]{:S(2)}) %all-to-all-start.2) | async-done | bytes 2097184 | tf_op jit(solution)/shard_map/all_to_all | solution.py:37
  89.5 8.5 %all-to-all-start.3 = ((bf16[8,64,512]{2,1,0:T(8,128)(2,1)}), bf16[8,64,512]{2,1,0:T(8,128)(2,1)S(1)}, u32[]{:S(2)}, u32[]{:S(2)}) async-start(bf16[8,64,512]{2,1,0:T(8,128)(2,1)} %bitcast.138), calls=%async_computation.3 | async-start | bytes 1048576 | tf_op jit(solution)/shard_map/all_to_all | solution.py:47
  98.1 17.0 %all-to-all-done.3 = bf16[8,64,512]{2,1,0:T(8,128)(2,1)S(1)} async-done(((bf16[8,64,512]{2,1,0:T(8,128)(2,1)}), bf16[8,64,512]{2,1,0:T(8,128)(2,1)S(1)}, u32[]{:S(2)}, u32[]{:S(2)}) %all-to-all-start.3) | async-done | bytes 524320 | tf_op jit(solution)/shard_map/all_to_all | solution.py:47
  116.0 3.5 %all-to-all-start.4 = ((bf16[8,64,512]{2,1,0:T(8,128)(2,1)}), bf16[8,64,512]{2,1,0:T(8,128)(2,1)S(1)}, u32[]{:S(2)}, u32[]{:S(2)}) async-start(bf16[8,64,512]{2,1,0:T(8,128)(2,1)} %broadcast_in_dim.89), calls=%async_computation.4 | async-start | bytes 1048576 | tf_op jit(solution)/shard_map/all_to_all | solution.py:54
  121.5 14.9 %all-to-all-done.4 = bf16[8,64,512]{2,1,0:T(8,128)(2,1)S(1)} async-done(((bf16[8,64,512]{2,1,0:T(8,128)(2,1)}), bf16[8,64,512]{2,1,0:T(8,128)(2,1)S(1)}, u32[]{:S(2)}, u32[]{:S(2)}) %all-to-all-start.4) | async-done | bytes 524320 | tf_op jit(solution)/shard_map/all_to_all | solution.py:54
  143.7 37.2 %all_to_all.46 = bf16[32,288,128]{2,1,0:T(8,128)(2,1)} all-to-all(bf16[32,288,128]{2,1,0:T(8,128)(2,1)S(1)} %bitcast.142), channel_id=1, replica_groups=mesh['req'=32,'tp'=8] {'req'}, dimensions={0} | all-to-all | bytes 4718592 | tf_op jit(solution)/shard_map/all_to_all | solution.py:200
  180.9 4.9 %reshape.298 = bf16[288,4096]{1,0:T(8,128)(2,1)} reshape(bf16[32,288,128]{2,1,0:T(8,128)(2,1)} %all_to_all.46) | data formatting | bytes 4718592 | tf_op jit(solution)/shard_map/reshape | solution.py:127
  185.8 3.8 %fusion.9 = f32[288,256]{1,0:T(8,128)} fusion(bf16[288,4096]{1,0:T(8,128)(2,1)} %reshape.298, bf16[1,4096,256]{2,1,0:T(8,128)(2,1)} %param.24), kind=kOutput, calls=%fused_computation.17 | convolution fusion | flops 603979776 | bytes 4751360 | tf_op jit(solution)/shard_map/dot_general | solution.py:128
  189.6 6.4 %convolution_convert_fusion.1 = bf16[288,4096]{1,0:T(8,128)(2,1)} fusion(bf16[1,256,4096]{2,1,0:T(8,128)(2,1)S(1)} %copy-done, bf16[288,4096]{1,0:T(8,128)(2,1)} %reshape.298, bf16[1,4096,256]{2,1,0:T(8,128)(2,1)} %param.25, f32[288,256]{1,0:T(8,128)} %fusion.9), kind=kOutput, calls=%fused_computation.3 | convolution fusion | flops 1209581568 | bytes 9207808 | tf_op jit(solution)/shard_map/dot_general | solution.py:131
  202.2 34.9 %all_to_all.47 = bf16[32,288,128]{2,1,0:T(8,128)(2,1)} all-to-all(bf16[32,288,128]{2,1,0:T(8,128)(2,1)S(1)} %bitcast.143), channel_id=1, replica_groups=mesh['req'=32,'tp'=8] {'req'}, dimensions={0} | all-to-all | bytes 4718592 | tf_op jit(solution)/shard_map/all_to_all | solution.py:200
  237.1 5.0 %reshape.305 = bf16[288,4096]{1,0:T(8,128)(2,1)} reshape(bf16[32,288,128]{2,1,0:T(8,128)(2,1)} %all_to_all.47) | data formatting | bytes 4718592 | tf_op jit(solution)/shard_map/reshape | solution.py:127
  242.1 3.8 %fusion.7 = f32[288,256]{1,0:T(8,128)} fusion(bf16[288,4096]{1,0:T(8,128)(2,1)} %reshape.305, bf16[1,4096,256]{2,1,0:T(8,128)(2,1)} %param.24), kind=kOutput, calls=%fused_computation.15 | convolution fusion | flops 603979776 | bytes 4751360 | tf_op jit(solution)/shard_map/dot_general | solution.py:128
  245.9 6.3 %convolution_convert_fusion = bf16[288,4096]{1,0:T(8,128)(2,1)} fusion(bf16[1,256,4096]{2,1,0:T(8,128)(2,1)S(1)} %copy-done, bf16[288,4096]{1,0:T(8,128)(2,1)} %reshape.305, bf16[1,4096,256]{2,1,0:T(8,128)(2,1)} %param.25, f32[288,256]{1,0:T(8,128)} %fusion.7), kind=kOutput, calls=%fused_computation.2 | convolution fusion | flops 1209581568 | bytes 9207808 | tf_op jit(solution)/shard_map/dot_general | solution.py:131
  257.6 5.1 %all-to-all-start.6 = ((bf16[32,36,128]{2,1,0:T(8,128)(2,1)}), bf16[32,36,128]{2,1,0:T(8,128)(2,1)S(1)}, u32[]{:S(2)}, u32[]{:S(2)}) async-start(bf16[32,36,128]{2,1,0:T(8,128)(2,1)} %reshape.299), calls=%async_computation.7 | async-start | bytes 655360 | tf_op jit(solution)/shard_map/all_to_all | solution.py:138
  263.5 25.8 %reduce-scatter.5.cloned.1.call-done = bf16[288,512]{1,0:T(8,128)(2,1)} async-done(((bf16[288,4096]{1,0:T(8,128)(2,1)}), bf16[288,512]{1,0:T(8,128)(2,1)}) %reduce-scatter.5.cloned.1.call-update) | async-done | bytes 294928 | tf_op jit(solution)/shard_map/reduce_scatter | solution.py:202
  291.3 7.5 %all-to-all-start.8 = ((bf16[32,36,128]{2,1,0:T(8,128)(2,1)}), bf16[32,36,128]{2,1,0:T(8,128)(2,1)S(1)}, u32[]{:S(2)}, u32[]{:S(2)}) async-start(bf16[32,36,128]{2,1,0:T(8,128)(2,1)} %reshape.306), calls=%async_computation.10 | async-start | bytes 655360 | tf_op jit(solution)/shard_map/all_to_all | solution.py:138
  300.9 6.1 %all-to-all-done.8 = bf16[32,36,128]{2,1,0:T(8,128)(2,1)S(1)} async-done(((bf16[32,36,128]{2,1,0:T(8,128)(2,1)}), bf16[32,36,128]{2,1,0:T(8,128)(2,1)S(1)}, u32[]{:S(2)}, u32[]{:S(2)}) %all-to-all-start.8) | async-done | bytes 294944 | tf_op jit(solution)/shard_map/all_to_all | solution.py:138
  (109 shorter events, 41.5 us)
Async XLA Ops:
  6.5 183.1 %copy-start = (bf16[1,256,4096]{2,1,0:T(8,128)(2,1)S(1)}, bf16[1,256,4096]{2,1,0:T(8,128)(2,1)}, u32[]{:S(2)}) copy-start(bf16[1,256,4096]{2,1,0:T(8,128)(2,1)} %param.26) | copy-start | bytes 6291460
  8.0 13.7 %all-to-all-start = ((s32[32,1,2]{2,1,0:T(1,128)}), s32[32,1,2]{2,1,0:T(1,128)S(1)}, u32[]{:S(2)}, u32[]{:S(2)}) async-start(s32[32,1,2]{2,1,0:T(1,128)} %broadcast_in_dim.50), calls=%async_computation | async-start | bytes 32768 | tf_op jit(solution)/shard_map/all_to_all | solution.py:31
  15.6 11.1 %copy-start.9 = (s32[4]{0:T(128)S(1)}, s32[4]{0:T(128)}, u32[]{:S(2)}) copy-start(s32[4]{0:T(128)} %param.17) | copy-start | bytes 52
  21.7 21.1 %all-to-all-start.1 = ((bf16[32,64,2,128]{3,1,2,0:T(8,128)(2,1)}), bf16[32,64,2,128]{3,1,2,0:T(8,128)(2,1)S(1)}, u32[]{:S(2)}, u32[]{:S(2)}) async-start(bf16[32,64,2,128]{3,1,2,0:T(8,128)(2,1)} %copy.168), calls=%async_computation.1 | async-start | bytes 2097152 | tf_op jit(solution)/shard_map/all_to_all | solution.py:29
  48.8 5.9 %copy-start.7 = (bf16[64,2,128]{2,1,0:T(2,128)(2,1)S(1)}, bf16[64,2,128]{2,1,0:T(2,128)(2,1)}, u32[]{:S(2)}) copy-start(bf16[64,2,128]{2,1,0:T(2,128)(2,1)} %param.15) | copy-start | bytes 98308
  48.8 6.0 %copy-start.6 = (bf16[64,512]{1,0:T(8,128)(2,1)S(1)}, bf16[64,512]{1,0:T(8,128)(2,1)}, u32[]{:S(2)}) copy-start(bf16[64,512]{1,0:T(8,128)(2,1)} %param.14) | copy-start | bytes 196612
  48.8 6.0 %copy-start.10 = (s32[2]{0:T(128)S(1)}, s32[2]{0:T(128)}, u32[]{:S(2)}) copy-start(s32[2]{0:T(128)} %param.19) | copy-start | bytes 28
  48.8 34.0 %all-to-all-start.2 = ((bf16[32,2,64,2,128]{4,2,3,1,0:T(8,128)(2,1)}), bf16[32,2,64,2,128]{4,2,3,1,0:T(8,128)(2,1)}, u32[]{:S(2)}, u32[]{:S(2)}) async-start(bf16[32,2,64,2,128]{4,2,3,1,0:T(8,128)(2,1)} %broadcast_select_fusion), calls=%async_computation.2 | async-start | bytes 4194304 | tf_op jit(solution)/shard_map/all_to_all | solution.py:37
  85.6 2.2 copy-start.3
  88.6 31.2 %copy-start.8 = (s32[64,2]{0,1:T(2,128)S(1)}, s32[64,2]{0,1:T(2,128)}, u32[]{:S(2)}) copy-start(s32[64,2]{0,1:T(2,128)} %param.23) | copy-start | bytes 1540
  89.5 25.6 %all-to-all-start.3 = ((bf16[8,64,512]{2,1,0:T(8,128)(2,1)}), bf16[8,64,512]{2,1,0:T(8,128)(2,1)S(1)}, u32[]{:S(2)}, u32[]{:S(2)}) async-start(bf16[8,64,512]{2,1,0:T(8,128)(2,1)} %bitcast.138), calls=%async_computation.3 | async-start | bytes 1048576 | tf_op jit(solution)/shard_map/all_to_all | solution.py:47
  116.0 20.4 %all-to-all-start.4 = ((bf16[8,64,512]{2,1,0:T(8,128)(2,1)}), bf16[8,64,512]{2,1,0:T(8,128)(2,1)S(1)}, u32[]{:S(2)}, u32[]{:S(2)}) async-start(bf16[8,64,512]{2,1,0:T(8,128)(2,1)} %broadcast_in_dim.89), calls=%async_computation.4 | async-start | bytes 1048576 | tf_op jit(solution)/shard_map/all_to_all | solution.py:54
  119.5 136.1 %reduce-scatter.3.cloned.1.call-start = ((), (), s32[]{:S(2)}) async-start(), calls=%async_computation.11 | async-start | bytes 2654208 | tf_op jit(solution)/shard_map/reduce_scatter | solution.py:202
  136.5 1.5 copy-start.1
  136.5 1.5 copy-start.5
  138.2 0.8 copy-start.2
  196.0 93.3 %reduce-scatter.5.cloned.1.call-start = ((), (), s32[]{:S(2)}) async-start(), calls=%async_computation.12 | async-start | bytes 2654208 | tf_op jit(solution)/shard_map/reduce_scatter | solution.py:202
  252.2 0.9 copy-start.4
  257.6 33.7 %all-to-all-start.6 = ((bf16[32,36,128]{2,1,0:T(8,128)(2,1)}), bf16[32,36,128]{2,1,0:T(8,128)(2,1)S(1)}, u32[]{:S(2)}, u32[]{:S(2)}) async-start(bf16[32,36,128]{2,1,0:T(8,128)(2,1)} %reshape.299), calls=%async_computation.7 | async-start | bytes 655360 | tf_op jit(solution)/shard_map/all_to_all | solution.py:138
  291.3 15.7 %all-to-all-start.8 = ((bf16[32,36,128]{2,1,0:T(8,128)(2,1)}), bf16[32,36,128]{2,1,0:T(8,128)(2,1)S(1)}, u32[]{:S(2)}, u32[]{:S(2)}) async-start(bf16[32,36,128]{2,1,0:T(8,128)(2,1)} %reshape.306), calls=%async_computation.10 | async-start | bytes 655360 | tf_op jit(solution)/shard_map/all_to_all | solution.py:138
Sparse Core Ops, SparseCore 0:
  196.1 37.0 reduce-scatter.2
  252.3 36.9 reduce-scatter.4

commit v5 on v4

--- a/solution.py
+++ b/solution.py
@@ -12,7 +12,7 @@
 NPFX = 4
 CAP = 18
 LANES = 128
-CHUNKS = 2
+CHUNKS = 3
 
 
 def broadcast(x, axis, root):
@@ -28,9 +28,7 @@
     pieces = prefix_cache.reshape(req_count, piece, 2, width)
     scattered = lax.all_to_all(pieces, "req", 0, 0, tiled=True)
     owner_pieces = jnp.take(scattered, prefix_owner, axis=0)
-    wanted = lax.all_to_all(
-        jnp.broadcast_to(request_prefix[None], (req_count, requests)), "req", 0, 0, tiled=True
-    )
+    wanted = lax.all_gather(request_prefix, "req", tiled=True)
     outgoing = jnp.take(owner_pieces, wanted.reshape(-1), axis=0).reshape(
         req_count, requests, piece, 2, width
     )

time: 320 us -> 330 us (1.031)
  blocking collectives: 72.1 us -> 105 us
  waiting for transfers between devices: 110 us -> 80.3 us
  local copies, waits for them, and re-layouts: 38.4 us -> 42.3 us
  matrix products: 31.4 us -> 34.9 us
    unnamed x0 -> x1, blocking collectives: none -> 22.8 us
    all_to_all x1, waiting for transfers between devices: 14.5 us -> 0.01 us  [fetch_prefixes(): scattered = lax.all_to_all(pieces, 'req', 0, 0, tiled=True)]
    reduce_scatter x2 -> x3, waiting for transfers between devices: 25.8 us -> 11.7 us  [per_device(): reduced = lax.psum_scatter(piece_out, 'tp', scatter_dimension=1, tiled=True)]
    all_to_all x2 -> x3, blocking collectives: 72.1 us -> 81.8 us  [per_device(): lax.all_to_all(outgoing, 'req', split_axis=0, concat_axis=0, tiled=True)]
    all_to_all x1 -> x0, starting transfers between devices: 7.62 us -> none  [fetch_prefixes(): lax.all_to_all(jnp.broadcast_to(request_prefix[None], (req_count, request...]
    all_to_all x2 -> x3, starting transfers between devices: 12.5 us -> 17.4 us  [send_back(): return lax.all_to_all(parts, 'req', split_axis=0, concat_axis=0, tiled=True)]
    all_to_all x2 -> x3, waiting for transfers between devices: 6.14 us -> 11 us  [send_back(): return lax.all_to_all(parts, 'req', split_axis=0, concat_axis=0, tiled=True)]
    all_to_all x1 -> x0, waiting for transfers between devices: 3.59 us -> none  [fetch_prefixes(): lax.all_to_all(jnp.broadcast_to(request_prefix[None], (req_count, request...]
  transfers between devices with their start and end apart: 9 -> 10, of which waited for: 7 -> 6; matrix products, arithmetic and copies ran while one was open for 12% -> 14% of each run, Pallas kernels for 0% -> 0%
where the time goes in v5:
time: 330 us; the launch traced here: 326 us
  blocking collectives  105 us (32%)
  waiting for transfers between devices  80.3 us (24%)
  starting transfers between devices  43.4 us (13%)
  local copies, waits for them, and re-layouts  42.3 us (13%)
  matrix products  34.9 us (11%)
  between operations  14.5 us (4%)
  other arithmetic  6.49 us (2%)
    all_to_all x3, blocking collectives, per_device(): lax.all_to_all(outgoing, 'req', split_axis=0, concat_axis=0, tiled=True)  81.8 us
    all_to_all x1, waiting for transfers between devices, fetch_prefixes(): arrived = lax.all_to_all(outgoing, 'req', 0, 0, tiled=True)  27.6 us
    unnamed x1, blocking collectives  22.8 us
    all_to_all x3, starting transfers between devices, send_back(): return lax.all_to_all(parts, 'req', split_axis=0, concat_axis=0, tiled=True)  17.4 us
    all_to_all x1, waiting for transfers between devices, tp_reduce_scatter(): arrived = lax.all_to_all(chunks, 'tp', 0, 0, tiled=True)  17 us
    dot_general x3, matrix products, expert_apply(): jnp.dot(hidden_units, w_down[0], preferred_element_type=jnp.float32)  15.3 us
    all_to_all x1, waiting for transfers between devices, tp_all_gather(): arrived = lax.all_to_all(copies, 'tp', 0, 0, tiled=True)  13 us
    reduce_scatter x3, waiting for transfers between devices, per_device(): reduced = lax.psum_scatter(piece_out, 'tp', scatter_dimension=1, tiled=True)  11.7 us
  transfers between devices with their start and end apart: 10, of which 6 were waited for; matrix products, arithmetic and copies ran while one was open for 14% of the time, Pallas kernels for 0%

profile of v5, /device:TPU:2, one launch (start us, length us, event | category | flops | bytes accessed | tf_op | source)
XLA Modules:
  0.0 326.3 jit_solution(7831328504729784382)
XLA Ops:
  9.2 7.6 %all-to-all-start = ((bf16[32,64,2,128]{3,1,2,0:T(8,128)(2,1)}), bf16[32,64,2,128]{3,1,2,0:T(8,128)(2,1)S(1)}, u32[]{:S(2)}, u32[]{:S(2)}) async-start(bf16[32,64,2,128]{3,1,2,0:T(8,128)(2,1)} %copy.166), calls=%async_computation | async-start | bytes 2097152 | tf_op jit(solution)/shard_map/all_to_all | solution.py:29
  18.3 22.8 %all-reduce = s32[64]{0:T(128)S(1)} all-reduce(s32[64]{0:T(128)S(1)} %dynamic-update-slice), channel_id=1, replica_groups=mesh['req'=32,'tp'=8] {'req'}, use_global_device_ids=true, to_apply=%add | all-reduce | flops 64 | bytes 512
  44.1 3.2 broadcast_select_fusion
  47.3 6.3 %all-to-all-start.1 = ((bf16[32,2,64,2,128]{4,2,3,1,0:T(8,128)(2,1)}), bf16[32,2,64,2,128]{4,2,3,1,0:T(8,128)(2,1)}, u32[]{:S(2)}, u32[]{:S(2)}) async-start(bf16[32,2,64,2,128]{4,2,3,1,0:T(8,128)(2,1)} %broadcast_select_fusion), calls=%async_computation.1 | async-start | bytes 4194304 | tf_op jit(solution)/shard_map/all_to_all | solution.py:35
  54.0 27.6 %all-to-all-done.1 = bf16[32,2,64,2,128]{4,2,3,1,0:T(8,128)(2,1)} async-done(((bf16[32,2,64,2,128]{4,2,3,1,0:T(8,128)(2,1)}), bf16[32,2,64,2,128]{4,2,3,1,0:T(8,128)(2,1)}, u32[]{:S(2)}, u32[]{:S(2)}) %all-to-all-start.1) | async-done | bytes 2097184 | tf_op jit(solution)/shard_map/all_to_all | solution.py:35
  88.3 8.5 %all-to-all-start.2 = ((bf16[8,64,512]{2,1,0:T(8,128)(2,1)}), bf16[8,64,512]{2,1,0:T(8,128)(2,1)S(1)}, u32[]{:S(2)}, u32[]{:S(2)}) async-start(bf16[8,64,512]{2,1,0:T(8,128)(2,1)} %bitcast.158), calls=%async_computation.2 | async-start | bytes 1048576 | tf_op jit(solution)/shard_map/all_to_all | solution.py:45
  96.9 17.0 %all-to-all-done.2 = bf16[8,64,512]{2,1,0:T(8,128)(2,1)S(1)} async-done(((bf16[8,64,512]{2,1,0:T(8,128)(2,1)}), bf16[8,64,512]{2,1,0:T(8,128)(2,1)S(1)}, u32[]{:S(2)}, u32[]{:S(2)}) %all-to-all-start.2) | async-done | bytes 524320 | tf_op jit(solution)/shard_map/all_to_all | solution.py:45
  115.5 3.5 %all-to-all-start.3 = ((bf16[8,64,512]{2,1,0:T(8,128)(2,1)}), bf16[8,64,512]{2,1,0:T(8,128)(2,1)S(1)}, u32[]{:S(2)}, u32[]{:S(2)}) async-start(bf16[8,64,512]{2,1,0:T(8,128)(2,1)} %broadcast_in_dim.88), calls=%async_computation.3 | async-start | bytes 1048576 | tf_op jit(solution)/shard_map/all_to_all | solution.py:52
  122.8 13.0 %all-to-all-done.3 = bf16[8,64,512]{2,1,0:T(8,128)(2,1)S(1)} async-done(((bf16[8,64,512]{2,1,0:T(8,128)(2,1)}), bf16[8,64,512]{2,1,0:T(8,128)(2,1)S(1)}, u32[]{:S(2)}, u32[]{:S(2)}) %all-to-all-start.3) | async-done | bytes 524320 | tf_op jit(solution)/shard_map/all_to_all | solution.py:52
  141.6 28.8 %all_to_all.50 = bf16[32,192,128]{2,1,0:T(8,128)(2,1)} all-to-all(bf16[32,192,128]{2,1,0:T(8,128)(2,1)S(1)} %bitcast.163), channel_id=1, replica_groups=mesh['req'=32,'tp'=8] {'req'}, dimensions={0} | all-to-all | bytes 3145728 | tf_op jit(solution)/shard_map/all_to_all | solution.py:198
  170.4 3.7 %reshape.286 = bf16[192,4096]{1,0:T(8,128)(2,1)} reshape(bf16[32,192,128]{2,1,0:T(8,128)(2,1)} %all_to_all.50) | data formatting | bytes 3145728 | tf_op jit(solution)/shard_map/reshape | solution.py:125
  176.7 5.1 %convolution_convert_fusion.1 = bf16[192,4096]{1,0:T(8,128)(2,1)} fusion(bf16[1,256,4096]{2,1,0:T(8,128)(2,1)S(1)} %copy-done, bf16[192,4096]{1,0:T(8,128)(2,1)} %reshape.286, bf16[1,4096,256]{2,1,0:T(8,128)(2,1)} %param.25, f32[192,256]{1,0:T(8,128)S(1)} %fusion.12), kind=kOutput, calls=%fused_computation.3 | convolution fusion | flops 806387712 | bytes 7536640 | tf_op jit(solution)/shard_map/dot_general | solution.py:129
  186.3 26.5 %all_to_all.51 = bf16[32,192,128]{2,1,0:T(8,128)(2,1)} all-to-all(bf16[32,192,128]{2,1,0:T(8,128)(2,1)S(1)} %bitcast.164), channel_id=1, replica_groups=mesh['req'=32,'tp'=8] {'req'}, dimensions={0} | all-to-all | bytes 3145728 | tf_op jit(solution)/shard_map/all_to_all | solution.py:198
  212.8 3.7 %reshape.279 = bf16[192,4096]{1,0:T(8,128)(2,1)} reshape(bf16[32,192,128]{2,1,0:T(8,128)(2,1)} %all_to_all.51) | data formatting | bytes 3145728 | tf_op jit(solution)/shard_map/reshape | solution.py:125
  219.2 5.1 %convolution_convert_fusion.2 = bf16[192,4096]{1,0:T(8,128)(2,1)} fusion(bf16[1,256,4096]{2,1,0:T(8,128)(2,1)S(1)} %copy-done, bf16[192,4096]{1,0:T(8,128)(2,1)} %reshape.279, bf16[1,4096,256]{2,1,0:T(8,128)(2,1)} %param.25, f32[192,256]{1,0:T(8,128)S(1)} %fusion.14), kind=kOutput, calls=%fused_computation.4 | convolution fusion | flops 806387712 | bytes 7536640 | tf_op jit(solution)/shard_map/dot_general | solution.py:129
  228.7 26.5 %all_to_all.52 = bf16[32,192,128]{2,1,0:T(8,128)(2,1)} all-to-all(bf16[32,192,128]{2,1,0:T(8,128)(2,1)S(1)} %bitcast.165), channel_id=1, replica_groups=mesh['req'=32,'tp'=8] {'req'}, dimensions={0} | all-to-all | bytes 3145728 | tf_op jit(solution)/shard_map/all_to_all | solution.py:198
  255.2 3.7 %reshape.293 = bf16[192,4096]{1,0:T(8,128)(2,1)} reshape(bf16[32,192,128]{2,1,0:T(8,128)(2,1)} %all_to_all.52) | data formatting | bytes 3145728 | tf_op jit(solution)/shard_map/reshape | solution.py:125
  261.6 5.1 %convolution_convert_fusion = bf16[192,4096]{1,0:T(8,128)(2,1)} fusion(bf16[1,256,4096]{2,1,0:T(8,128)(2,1)S(1)} %copy-done, bf16[192,4096]{1,0:T(8,128)(2,1)} %reshape.293, bf16[1,4096,256]{2,1,0:T(8,128)(2,1)} %param.25, f32[192,256]{1,0:T(8,128)S(1)} %fusion.10), kind=kOutput, calls=%fused_computation.2 | convolution fusion | flops 806387712 | bytes 7536640 | tf_op jit(solution)/shard_map/dot_general | solution.py:129
  271.2 5.0 %all-to-all-start.7 = ((bf16[32,24,128]{2,1,0:T(8,128)(2,1)}), bf16[32,24,128]{2,1,0:T(8,128)(2,1)S(1)}, u32[]{:S(2)}, u32[]{:S(2)}) async-start(bf16[32,24,128]{2,1,0:T(8,128)(2,1)} %reshape.287), calls=%async_computation.9 | async-start | bytes 393216 | tf_op jit(solution)/shard_map/all_to_all | solution.py:136
  279.3 4.0 %all-to-all-done.7 = bf16[32,24,128]{2,1,0:T(8,128)(2,1)S(1)} async-done(((bf16[32,24,128]{2,1,0:T(8,128)(2,1)}), bf16[32,24,128]{2,1,0:T(8,128)(2,1)S(1)}, u32[]{:S(2)}, u32[]{:S(2)}) %all-to-all-start.7) | async-done | bytes 196640 | tf_op jit(solution)/shard_map/all_to_all | solution.py:136
  283.3 5.0 %all-to-all-start.5 = ((bf16[32,24,128]{2,1,0:T(8,128)(2,1)}), bf16[32,24,128]{2,1,0:T(8,128)(2,1)S(1)}, u32[]{:S(2)}, u32[]{:S(2)}) async-start(bf16[32,24,128]{2,1,0:T(8,128)(2,1)} %reshape.280), calls=%async_computation.6 | async-start | bytes 393216 | tf_op jit(solution)/shard_map/all_to_all | solution.py:136
  289.6 11.7 %reduce-scatter.8.cloned.1.call-done = bf16[192,512]{1,0:T(8,128)(2,1)} async-done(((bf16[192,4096]{1,0:T(8,128)(2,1)}), bf16[192,512]{1,0:T(8,128)(2,1)}) %reduce-scatter.8.cloned.1.call-update) | async-done | bytes 196624 | tf_op jit(solution)/shard_map/reduce_scatter | solution.py:200
  303.0 7.4 %all-to-all-start.9 = ((bf16[32,24,128]{2,1,0:T(8,128)(2,1)}), bf16[32,24,128]{2,1,0:T(8,128)(2,1)S(1)}, u32[]{:S(2)}, u32[]{:S(2)}) async-start(bf16[32,24,128]{2,1,0:T(8,128)(2,1)} %reshape.294), calls=%async_computation.12 | async-start | bytes 393216 | tf_op jit(solution)/shard_map/all_to_all | solution.py:136
  310.5 6.9 %all-to-all-done.9 = bf16[32,24,128]{2,1,0:T(8,128)(2,1)S(1)} async-done(((bf16[32,24,128]{2,1,0:T(8,128)(2,1)}), bf16[32,24,128]{2,1,0:T(8,128)(2,1)S(1)}, u32[]{:S(2)}, u32[]{:S(2)}) %all-to-all-start.9) | async-done | bytes 196640 | tf_op jit(solution)/shard_map/all_to_all | solution.py:136
  (154 shorter events, 54.2 us)
Async XLA Ops:
  6.5 170.2 %copy-start = (bf16[1,256,4096]{2,1,0:T(8,128)(2,1)S(1)}, bf16[1,256,4096]{2,1,0:T(8,128)(2,1)}, u32[]{:S(2)}) copy-start(bf16[1,256,4096]{2,1,0:T(8,128)(2,1)} %param.26) | copy-start | bytes 6291460
  6.5 10.3 %copy-start.25 = (u32[256]{0:T(256)S(1)}, u32[256]{0:T(256)}, u32[]{:S(2)}) copy-start(u32[256]{0:T(256)} %constant.89) | copy-start | bytes 3076
  6.5 11.5 %copy-start.22 = (s32[2]{0:T(128)S(1)}, s32[2]{0:T(128)}, u32[]{:S(2)}) copy-start(s32[2]{0:T(128)} %param.18) | copy-start | bytes 28
  6.5 34.7 %copy-start.23 = (s32[4]{0:T(128)S(1)}, s32[4]{0:T(128)}, u32[]{:S(2)}) copy-start(s32[4]{0:T(128)} %param.17) | copy-start | bytes 52
  9.2 32.1 %all-to-all-start = ((bf16[32,64,2,128]{3,1,2,0:T(8,128)(2,1)}), bf16[32,64,2,128]{3,1,2,0:T(8,128)(2,1)S(1)}, u32[]{:S(2)}, u32[]{:S(2)}) async-start(bf16[32,64,2,128]{3,1,2,0:T(8,128)(2,1)} %copy.166), calls=%async_computation | async-start | bytes 2097152 | tf_op jit(solution)/shard_map/all_to_all | solution.py:29
  47.3 6.3 %copy-start.15 = (bf16[64,2,128]{2,1,0:T(2,128)(2,1)S(1)}, bf16[64,2,128]{2,1,0:T(2,128)(2,1)}, u32[]{:S(2)}) copy-start(bf16[64,2,128]{2,1,0:T(2,128)(2,1)} %param.15) | copy-start | bytes 98308
  47.3 6.3 %copy-start.14 = (bf16[64,512]{1,0:T(8,128)(2,1)S(1)}, bf16[64,512]{1,0:T(8,128)(2,1)}, u32[]{:S(2)}) copy-start(bf16[64,512]{1,0:T(8,128)(2,1)} %param.14) | copy-start | bytes 196612
  47.3 6.3 %copy-start.24 = (s32[2]{0:T(128)S(1)}, s32[2]{0:T(128)}, u32[]{:S(2)}) copy-start(s32[2]{0:T(128)} %param.19) | copy-start | bytes 28
  47.3 34.3 %all-to-all-start.1 = ((bf16[32,2,64,2,128]{4,2,3,1,0:T(8,128)(2,1)}), bf16[32,2,64,2,128]{4,2,3,1,0:T(8,128)(2,1)}, u32[]{:S(2)}, u32[]{:S(2)}) async-start(bf16[32,2,64,2,128]{4,2,3,1,0:T(8,128)(2,1)} %broadcast_select_fusion), calls=%async_computation.1 | async-start | bytes 4194304 | tf_op jit(solution)/shard_map/all_to_all | solution.py:35
  87.5 31.8 %copy-start.21 = (s32[64,2]{0,1:T(2,128)S(1)}, s32[64,2]{0,1:T(2,128)}, u32[]{:S(2)}) copy-start(s32[64,2]{0,1:T(2,128)} %param.23) | copy-start | bytes 1540
  88.3 25.6 %all-to-all-start.2 = ((bf16[8,64,512]{2,1,0:T(8,128)(2,1)}), bf16[8,64,512]{2,1,0:T(8,128)(2,1)S(1)}, u32[]{:S(2)}, u32[]{:S(2)}) async-start(bf16[8,64,512]{2,1,0:T(8,128)(2,1)} %bitcast.158), calls=%async_computation.2 | async-start | bytes 1048576 | tf_op jit(solution)/shard_map/all_to_all | solution.py:45
  115.5 20.4 %all-to-all-start.3 = ((bf16[8,64,512]{2,1,0:T(8,128)(2,1)}), bf16[8,64,512]{2,1,0:T(8,128)(2,1)S(1)}, u32[]{:S(2)}, u32[]{:S(2)}) async-start(bf16[8,64,512]{2,1,0:T(8,128)(2,1)} %broadcast_in_dim.88), calls=%async_computation.3 | async-start | bytes 1048576 | tf_op jit(solution)/shard_map/all_to_all | solution.py:52
  119.0 150.5 %reduce-scatter.6.cloned.1.call-start = ((), (), s32[]{:S(2)}) async-start(), calls=%async_computation.14 | async-start | bytes 1769472 | tf_op jit(solution)/shard_map/reduce_scatter | solution.py:200
  119.1 16.8 %copy-start.19 = (pred[64]{0:T(512)(128)(4,1)}, pred[64]{0:T(512)(128)(4,1)S(1)}, u32[]{:S(2)}) copy-start(pred[64]{0:T(512)(128)(4,1)S(1)} %fusion.95) | copy-start | bytes 196
  181.9 95.7 %reduce-scatter.4.cloned.1.call-start = ((), (), s32[]{:S(2)}) async-start(), calls=%async_computation.13 | async-start | bytes 1769472 | tf_op jit(solution)/shard_map/reduce_scatter | solution.py:200
  219.2 5.2 %copy-start.6 = (bf16[8,6,64]{1,0,2:T(8,128)(2,1)S(1)}, bf16[8,6,64]{1,0,2:T(8,128)(2,1)}, u32[]{:S(2)}) copy-start(bf16[8,6,64]{1,0,2:T(8,128)(2,1)} %get-tuple-element.10) | copy-start | bytes 18436
  224.3 76.9 %reduce-scatter.8.cloned.1.call-start = ((), (), s32[]{:S(2)}) async-start(), calls=%async_computation.15 | async-start | bytes 1769472 | tf_op jit(solution)/shard_map/reduce_scatter | solution.py:200
  266.7 9.5 %copy-start.17 = (s32[64,2]{1,0:T(8,128)S(1)}, s32[64,2]{1,0:T(8,128)}, u32[]{:S(2)}) copy-start(s32[64,2]{1,0:T(8,128)} %copy-done.16) | copy-start | bytes 1540
  271.2 12.1 %all-to-all-start.7 = ((bf16[32,24,128]{2,1,0:T(8,128)(2,1)}), bf16[32,24,128]{2,1,0:T(8,128)(2,1)S(1)}, u32[]{:S(2)}, u32[]{:S(2)}) async-start(bf16[32,24,128]{2,1,0:T(8,128)(2,1)} %reshape.287), calls=%async_computation.9 | async-start | bytes 393216 | tf_op jit(solution)/shard_map/all_to_all | solution.py:136
  283.3 19.6 %all-to-all-start.5 = ((bf16[32,24,128]{2,1,0:T(8,128)(2,1)}), bf16[32,24,128]{2,1,0:T(8,128)(2,1)S(1)}, u32[]{:S(2)}, u32[]{:S(2)}) async-start(bf16[32,24,128]{2,1,0:T(8,128)(2,1)} %reshape.280), calls=%async_computation.6 | async-start | bytes 393216 | tf_op jit(solution)/shard_map/all_to_all | solution.py:136
  288.5 29.5 %copy-start.5 = (f32[64,512]{1,0:T(8,128)S(1)}, f32[64,512]{1,0:T(8,128)}, u32[]{:S(2)}) copy-start(f32[64,512]{1,0:T(8,128)} %copy-done.4) | copy-start | bytes 393220
  288.5 29.5 %copy-start.20 = (pred[64]{0:T(512)(128)(4,1)S(1)}, pred[64]{0:T(512)(128)(4,1)}, u32[]{:S(2)}) copy-start(pred[64]{0:T(512)(128)(4,1)} %copy-done.19) | copy-start | bytes 196
  289.3 28.8 %copy-start.11 = (f32[64,48]{1,0:T(8,128)S(1)}, f32[64,48]{1,0:T(8,128)}, u32[]{:S(2)}) copy-start(f32[64,48]{1,0:T(8,128)} %reshape.336) | copy-start | bytes 36868
  303.0 14.5 %all-to-all-start.9 = ((bf16[32,24,128]{2,1,0:T(8,128)(2,1)}), bf16[32,24,128]{2,1,0:T(8,128)(2,1)S(1)}, u32[]{:S(2)}, u32[]{:S(2)}) async-start(bf16[32,24,128]{2,1,0:T(8,128)(2,1)} %reshape.294), calls=%async_computation.12 | async-start | bytes 393216 | tf_op jit(solution)/shard_map/all_to_all | solution.py:136
  (12 other events, 25.1 us)
Sparse Core Ops, SparseCore 0:
  182.0 34.3 reduce-scatter.5
  224.4 34.2 reduce-scatter.3
  266.9 34.3 reduce-scatter.7

commit v6 on v4

--- a/solution.py
+++ b/solution.py
@@ -26,11 +26,15 @@
     piece = plen // req_count
     requests = request_prefix.shape[0]
     pieces = prefix_cache.reshape(req_count, piece, 2, width)
-    scattered = lax.all_to_all(pieces, "req", 0, 0, tiled=True)
-    owner_pieces = jnp.take(scattered, prefix_owner, axis=0)
-    wanted = lax.all_to_all(
-        jnp.broadcast_to(request_prefix[None], (req_count, requests)), "req", 0, 0, tiled=True
-    )
+    tag_rows = 16
+    tags = jnp.zeros((tag_rows, 2, width), jnp.bfloat16)
+    tags = tags.at[0, 0, :requests].set(request_prefix.astype(jnp.bfloat16))
+    tagged = jnp.concatenate(
+        [pieces, jnp.broadcast_to(tags[None], (req_count, tag_rows, 2, width))], axis=1
+    )
+    scattered = lax.all_to_all(tagged, "req", 0, 0, tiled=True)
+    owner_pieces = jnp.take(scattered[:, :piece], prefix_owner, axis=0)
+    wanted = scattered[:, piece, 0, :requests].astype(jnp.int32)
     outgoing = jnp.take(owner_pieces, wanted.reshape(-1), axis=0).reshape(
         req_count, requests, piece, 2, width
     )

time: 320 us -> 317 us (level)
  starting transfers between devices: 43.3 us -> 39.2 us
    all_to_all x2 -> x1, starting transfers between devices: 12.7 us -> 7.62 us  [fetch_prefixes(): scattered = lax.all_to_all(tagged, 'req', 0, 0, tiled=True)]
    all_to_all x2 -> x1, waiting for transfers between devices: 18.1 us -> 18.8 us  [fetch_prefixes(): scattered = lax.all_to_all(tagged, 'req', 0, 0, tiled=True)]
  transfers between devices with their start and end apart: 9 -> 8, of which waited for: 7 -> 6; matrix products, arithmetic and copies ran while one was open for 12% -> 10% of each run, Pallas kernels for 0% -> 0%
where the time goes in v6:
time: 317 us; the launch traced here: 313 us
  waiting for transfers between devices  110 us (35%)
  blocking collectives  72.1 us (23%)
  starting transfers between devices  39.2 us (12%)
  local copies, waits for them, and re-layouts  37.9 us (12%)
  matrix products  31.4 us (10%)
  between operations  13.9 us (4%)
  other arithmetic  8.54 us (3%)
    all_to_all x2, blocking collectives, per_device(): lax.all_to_all(outgoing, 'req', split_axis=0, concat_axis=0, tiled=True)  72.1 us
    all_to_all x1, waiting for transfers between devices, fetch_prefixes(): arrived = lax.all_to_all(outgoing, 'req', 0, 0, tiled=True)  27.6 us
    reduce_scatter x2, waiting for transfers between devices, per_device(): reduced = lax.psum_scatter(piece_out, 'tp', scatter_dimension=1, tiled=True)  25.9 us
    all_to_all x1, waiting for transfers between devices, fetch_prefixes(): scattered = lax.all_to_all(tagged, 'req', 0, 0, tiled=True)  18.8 us
    all_to_all x1, waiting for transfers between devices, tp_reduce_scatter(): arrived = lax.all_to_all(chunks, 'tp', 0, 0, tiled=True)  17 us
    all_to_all x1, waiting for transfers between devices, tp_all_gather(): arrived = lax.all_to_all(copies, 'tp', 0, 0, tiled=True)  14.9 us
    all_to_all x2, starting transfers between devices, send_back(): return lax.all_to_all(parts, 'req', split_axis=0, concat_axis=0, tiled=True)  12.9 us
    dot_general x2, matrix products, expert_apply(): jnp.dot(hidden_units, w_down[0], preferred_element_type=jnp.float32)  12.7 us
  transfers between devices with their start and end apart: 8, of which 6 were waited for; matrix products, arithmetic and copies ran while one was open for 10% of the time, Pallas kernels for 0%

profile of v6, /device:TPU:2, one launch (start us, length us, event | category | flops | bytes accessed | tf_op | source)
XLA Modules:
  0.0 313.3 jit_solution(14369161837890769177)
XLA Ops:
  10.1 7.6 %all-to-all-start = ((bf16[32,80,2,128]{3,1,2,0:T(8,128)(2,1)}), bf16[32,80,2,128]{3,1,2,0:T(8,128)(2,1)S(1)}, u32[]{:S(2)}, u32[]{:S(2)}) async-start(bf16[32,80,2,128]{3,1,2,0:T(8,128)(2,1)} %pad_maximum_fusion), calls=%async_computation | async-start | bytes 2621440 | tf_op jit(solution)/shard_map/all_to_all | solution.py:35
  17.7 18.8 %all-to-all-done = bf16[32,80,2,128]{3,1,2,0:T(8,128)(2,1)S(1)} async-done(((bf16[32,80,2,128]{3,1,2,0:T(8,128)(2,1)}), bf16[32,80,2,128]{3,1,2,0:T(8,128)(2,1)S(1)}, u32[]{:S(2)}, u32[]{:S(2)}) %all-to-all-start) | async-done | bytes 1310752 | tf_op jit(solution)/shard_map/all_to_all | solution.py:35
  39.9 2.1 gather_fusion.1
  42.0 3.2 %copy_select_fusion = bf16[32,2,64,2,128]{4,2,1,3,0:T(8,128)(2,1)} fusion(bf16[32,2,64,2,128]{4,2,3,1,0:T(8,128)(2,1)} %bitcast.148, pred[32,2]{1,0:T(8,128)(4,1)S(1)} %copy.149), kind=kLoop, calls=%fused_computation.19 | loop fusion | flops 1048576 | bytes 4194368 | tf_op jit(solution)/shard_map/jit(_take)/select_n | solution.py:38
  45.2 6.5 %all-to-all-start.1 = ((bf16[32,2,64,2,128]{4,2,1,3,0:T(8,128)(2,1)}), bf16[32,2,64,2,128]{4,2,1,3,0:T(8,128)(2,1)}, u32[]{:S(2)}, u32[]{:S(2)}) async-start(bf16[32,2,64,2,128]{4,2,1,3,0:T(8,128)(2,1)} %copy_select_fusion), calls=%async_computation.1 | async-start | bytes 4194304 | tf_op jit(solution)/shard_map/all_to_all | solution.py:41
  52.2 27.6 %all-to-all-done.1 = bf16[32,2,64,2,128]{4,2,1,3,0:T(8,128)(2,1)} async-done(((bf16[32,2,64,2,128]{4,2,1,3,0:T(8,128)(2,1)}), bf16[32,2,64,2,128]{4,2,1,3,0:T(8,128)(2,1)}, u32[]{:S(2)}, u32[]{:S(2)}) %all-to-all-start.1) | async-done | bytes 2097184 | tf_op jit(solution)/shard_map/all_to_all | solution.py:41
  86.5 8.5 %all-to-all-start.2 = ((bf16[8,64,512]{2,1,0:T(8,128)(2,1)}), bf16[8,64,512]{2,1,0:T(8,128)(2,1)S(1)}, u32[]{:S(2)}, u32[]{:S(2)}) async-start(bf16[8,64,512]{2,1,0:T(8,128)(2,1)} %bitcast.142), calls=%async_computation.2 | async-start | bytes 1048576 | tf_op jit(solution)/shard_map/all_to_all | solution.py:51
  95.1 17.0 %all-to-all-done.2 = bf16[8,64,512]{2,1,0:T(8,128)(2,1)S(1)} async-done(((bf16[8,64,512]{2,1,0:T(8,128)(2,1)}), bf16[8,64,512]{2,1,0:T(8,128)(2,1)S(1)}, u32[]{:S(2)}, u32[]{:S(2)}) %all-to-all-start.2) | async-done | bytes 524320 | tf_op jit(solution)/shard_map/all_to_all | solution.py:51
  113.0 3.5 %all-to-all-start.3 = ((bf16[8,64,512]{2,1,0:T(8,128)(2,1)}), bf16[8,64,512]{2,1,0:T(8,128)(2,1)S(1)}, u32[]{:S(2)}, u32[]{:S(2)}) async-start(bf16[8,64,512]{2,1,0:T(8,128)(2,1)} %broadcast_in_dim.93), calls=%async_computation.3 | async-start | bytes 1048576 | tf_op jit(solution)/shard_map/all_to_all | solution.py:58
  118.5 14.9 %all-to-all-done.3 = bf16[8,64,512]{2,1,0:T(8,128)(2,1)S(1)} async-done(((bf16[8,64,512]{2,1,0:T(8,128)(2,1)}), bf16[8,64,512]{2,1,0:T(8,128)(2,1)S(1)}, u32[]{:S(2)}, u32[]{:S(2)}) %all-to-all-start.3) | async-done | bytes 524320 | tf_op jit(solution)/shard_map/all_to_all | solution.py:58
  140.7 37.2 %all_to_all.40 = bf16[32,288,128]{2,1,0:T(8,128)(2,1)} all-to-all(bf16[32,288,128]{2,1,0:T(8,128)(2,1)S(1)} %bitcast.146), channel_id=1, replica_groups=mesh['req'=32,'tp'=8] {'req'}, dimensions={0} | all-to-all | bytes 4718592 | tf_op jit(solution)/shard_map/all_to_all | solution.py:204
  177.9 4.9 %reshape.318 = bf16[288,4096]{1,0:T(8,128)(2,1)} reshape(bf16[32,288,128]{2,1,0:T(8,128)(2,1)} %all_to_all.40) | data formatting | bytes 4718592 | tf_op jit(solution)/shard_map/reshape | solution.py:131
  182.8 3.8 %fusion.9 = f32[288,256]{1,0:T(8,128)} fusion(bf16[288,4096]{1,0:T(8,128)(2,1)} %reshape.318, bf16[1,4096,256]{2,1,0:T(8,128)(2,1)} %param.26), kind=kOutput, calls=%fused_computation.17 | convolution fusion | flops 603979776 | bytes 4751360 | tf_op jit(solution)/shard_map/dot_general | solution.py:132
  186.6 6.4 %convolution_convert_fusion.1 = bf16[288,4096]{1,0:T(8,128)(2,1)} fusion(bf16[1,256,4096]{2,1,0:T(8,128)(2,1)S(1)} %copy-done, bf16[288,4096]{1,0:T(8,128)(2,1)} %reshape.318, bf16[1,4096,256]{2,1,0:T(8,128)(2,1)} %param.27, f32[288,256]{1,0:T(8,128)} %fusion.9), kind=kOutput, calls=%fused_computation.3 | convolution fusion | flops 1209581568 | bytes 9207808 | tf_op jit(solution)/shard_map/dot_general | solution.py:135
  193.4 2.2 convolution_convert_fusion.2
  195.6 2.1 tile.23
  199.2 34.9 %all_to_all.41 = bf16[32,288,128]{2,1,0:T(8,128)(2,1)} all-to-all(bf16[32,288,128]{2,1,0:T(8,128)(2,1)S(1)} %bitcast.147), channel_id=1, replica_groups=mesh['req'=32,'tp'=8] {'req'}, dimensions={0} | all-to-all | bytes 4718592 | tf_op jit(solution)/shard_map/all_to_all | solution.py:204
  234.1 5.0 %reshape.325 = bf16[288,4096]{1,0:T(8,128)(2,1)} reshape(bf16[32,288,128]{2,1,0:T(8,128)(2,1)} %all_to_all.41) | data formatting | bytes 4718592 | tf_op jit(solution)/shard_map/reshape | solution.py:131
  239.1 3.8 %fusion.7 = f32[288,256]{1,0:T(8,128)} fusion(bf16[288,4096]{1,0:T(8,128)(2,1)} %reshape.325, bf16[1,4096,256]{2,1,0:T(8,128)(2,1)} %param.26), kind=kOutput, calls=%fused_computation.15 | convolution fusion | flops 603979776 | bytes 4751360 | tf_op jit(solution)/shard_map/dot_general | solution.py:132
  242.8 6.3 %convolution_convert_fusion = bf16[288,4096]{1,0:T(8,128)(2,1)} fusion(bf16[1,256,4096]{2,1,0:T(8,128)(2,1)S(1)} %copy-done, bf16[288,4096]{1,0:T(8,128)(2,1)} %reshape.325, bf16[1,4096,256]{2,1,0:T(8,128)(2,1)} %param.27, f32[288,256]{1,0:T(8,128)} %fusion.7), kind=kOutput, calls=%fused_computation.2 | convolution fusion | flops 1209581568 | bytes 9207808 | tf_op jit(solution)/shard_map/dot_general | solution.py:135
  254.6 5.1 %all-to-all-start.5 = ((bf16[32,36,128]{2,1,0:T(8,128)(2,1)}), bf16[32,36,128]{2,1,0:T(8,128)(2,1)S(1)}, u32[]{:S(2)}, u32[]{:S(2)}) async-start(bf16[32,36,128]{2,1,0:T(8,128)(2,1)} %reshape.319), calls=%async_computation.6 | async-start | bytes 655360 | tf_op jit(solution)/shard_map/all_to_all | solution.py:142
  260.5 25.8 %reduce-scatter.5.cloned.1.call-done = bf16[288,512]{1,0:T(8,128)(2,1)} async-done(((bf16[288,4096]{1,0:T(8,128)(2,1)}), bf16[288,512]{1,0:T(8,128)(2,1)}) %reduce-scatter.5.cloned.1.call-update) | async-done | bytes 294928 | tf_op jit(solution)/shard_map/reduce_scatter | solution.py:206
  288.3 7.8 %all-to-all-start.7 = ((bf16[32,36,128]{2,1,0:T(8,128)(2,1)}), bf16[32,36,128]{2,1,0:T(8,128)(2,1)S(1)}, u32[]{:S(2)}, u32[]{:S(2)}) async-start(bf16[32,36,128]{2,1,0:T(8,128)(2,1)} %reshape.326), calls=%async_computation.9 | async-start | bytes 655360 | tf_op jit(solution)/shard_map/all_to_all | solution.py:142
  298.2 6.1 %all-to-all-done.7 = bf16[32,36,128]{2,1,0:T(8,128)(2,1)S(1)} async-done(((bf16[32,36,128]{2,1,0:T(8,128)(2,1)}), bf16[32,36,128]{2,1,0:T(8,128)(2,1)S(1)}, u32[]{:S(2)}, u32[]{:S(2)}) %all-to-all-start.7) | async-done | bytes 294944 | tf_op jit(solution)/shard_map/all_to_all | solution.py:142
  (111 shorter events, 38.3 us)
Async XLA Ops:
  6.5 180.1 %copy-start = (bf16[1,256,4096]{2,1,0:T(8,128)(2,1)S(1)}, bf16[1,256,4096]{2,1,0:T(8,128)(2,1)}, u32[]{:S(2)}) copy-start(bf16[1,256,4096]{2,1,0:T(8,128)(2,1)} %param.28) | copy-start | bytes 6291460
  8.9 8.8 %copy-start.9 = (s32[4]{0:T(128)S(1)}, s32[4]{0:T(128)}, u32[]{:S(2)}) copy-start(s32[4]{0:T(128)} %param.19) | copy-start | bytes 52
  10.1 26.4 %all-to-all-start = ((bf16[32,80,2,128]{3,1,2,0:T(8,128)(2,1)}), bf16[32,80,2,128]{3,1,2,0:T(8,128)(2,1)S(1)}, u32[]{:S(2)}, u32[]{:S(2)}) async-start(bf16[32,80,2,128]{3,1,2,0:T(8,128)(2,1)} %pad_maximum_fusion), calls=%async_computation | async-start | bytes 2621440 | tf_op jit(solution)/shard_map/all_to_all | solution.py:35
  45.2 6.5 %copy-start.7 = (bf16[64,2,128]{2,1,0:T(2,128)(2,1)S(1)}, bf16[64,2,128]{2,1,0:T(2,128)(2,1)}, u32[]{:S(2)}) copy-start(bf16[64,2,128]{2,1,0:T(2,128)(2,1)} %param.17) | copy-start | bytes 98308
  45.2 6.5 %copy-start.6 = (bf16[64,512]{1,0:T(8,128)(2,1)S(1)}, bf16[64,512]{1,0:T(8,128)(2,1)}, u32[]{:S(2)}) copy-start(bf16[64,512]{1,0:T(8,128)(2,1)} %param.16) | copy-start | bytes 196612
  45.2 6.5 %copy-start.10 = (s32[2]{0:T(128)S(1)}, s32[2]{0:T(128)}, u32[]{:S(2)}) copy-start(s32[2]{0:T(128)} %param.21) | copy-start | bytes 28
  45.2 34.5 %all-to-all-start.1 = ((bf16[32,2,64,2,128]{4,2,1,3,0:T(8,128)(2,1)}), bf16[32,2,64,2,128]{4,2,1,3,0:T(8,128)(2,1)}, u32[]{:S(2)}, u32[]{:S(2)}) async-start(bf16[32,2,64,2,128]{4,2,1,3,0:T(8,128)(2,1)} %copy_select_fusion), calls=%async_computation.1 | async-start | bytes 4194304 | tf_op jit(solution)/shard_map/all_to_all | solution.py:41
  82.6 2.2 copy-start.3
  85.6 31.2 %copy-start.8 = (s32[64,2]{0,1:T(2,128)S(1)}, s32[64,2]{0,1:T(2,128)}, u32[]{:S(2)}) copy-start(s32[64,2]{0,1:T(2,128)} %param.25) | copy-start | bytes 1540
  86.5 25.6 %all-to-all-start.2 = ((bf16[8,64,512]{2,1,0:T(8,128)(2,1)}), bf16[8,64,512]{2,1,0:T(8,128)(2,1)S(1)}, u32[]{:S(2)}, u32[]{:S(2)}) async-start(bf16[8,64,512]{2,1,0:T(8,128)(2,1)} %bitcast.142), calls=%async_computation.2 | async-start | bytes 1048576 | tf_op jit(solution)/shard_map/all_to_all | solution.py:51
  113.0 20.4 %all-to-all-start.3 = ((bf16[8,64,512]{2,1,0:T(8,128)(2,1)}), bf16[8,64,512]{2,1,0:T(8,128)(2,1)S(1)}, u32[]{:S(2)}, u32[]{:S(2)}) async-start(bf16[8,64,512]{2,1,0:T(8,128)(2,1)} %broadcast_in_dim.93), calls=%async_computation.3 | async-start | bytes 1048576 | tf_op jit(solution)/shard_map/all_to_all | solution.py:58
  116.5 136.1 %reduce-scatter.3.cloned.1.call-start = ((), (), s32[]{:S(2)}) async-start(), calls=%async_computation.10 | async-start | bytes 2654208 | tf_op jit(solution)/shard_map/reduce_scatter | solution.py:206
  133.5 1.5 copy-start.1
  133.5 1.5 copy-start.5
  135.2 0.8 copy-start.2
  193.0 93.3 %reduce-scatter.5.cloned.1.call-start = ((), (), s32[]{:S(2)}) async-start(), calls=%async_computation.11 | async-start | bytes 2654208 | tf_op jit(solution)/shard_map/reduce_scatter | solution.py:206
  249.2 0.9 copy-start.4
  254.6 33.7 %all-to-all-start.5 = ((bf16[32,36,128]{2,1,0:T(8,128)(2,1)}), bf16[32,36,128]{2,1,0:T(8,128)(2,1)S(1)}, u32[]{:S(2)}, u32[]{:S(2)}) async-start(bf16[32,36,128]{2,1,0:T(8,128)(2,1)} %reshape.319), calls=%async_computation.6 | async-start | bytes 655360 | tf_op jit(solution)/shard_map/all_to_all | solution.py:142
  288.3 16.1 %all-to-all-start.7 = ((bf16[32,36,128]{2,1,0:T(8,128)(2,1)}), bf16[32,36,128]{2,1,0:T(8,128)(2,1)S(1)}, u32[]{:S(2)}, u32[]{:S(2)}) async-start(bf16[32,36,128]{2,1,0:T(8,128)(2,1)} %reshape.326), calls=%async_computation.9 | async-start | bytes 655360 | tf_op jit(solution)/shard_map/all_to_all | solution.py:142
Sparse Core Ops, SparseCore 0:
  193.1 36.9 reduce-scatter.2
  249.3 36.9 reduce-scatter.4

commit v7 on v6

--- a/solution.py
+++ b/solution.py
@@ -45,18 +45,28 @@
 def tp_reduce_scatter(values, tp_count):
     rows, width = values.shape
     share = width // tp_count
-    chunks = jnp.transpose(
-        values.astype(jnp.bfloat16).reshape(rows, tp_count, share), (1, 0, 2)
-    )
-    arrived = lax.all_to_all(chunks, "tp", 0, 0, tiled=True)
-    return arrived.astype(jnp.float32).sum(axis=0)
+    me = lax.axis_index("tp")
+    chunks = values.astype(jnp.bfloat16).reshape(rows, tp_count, share)
+    total = lax.dynamic_index_in_dim(chunks, me, axis=1, keepdims=False).astype(jnp.float32)
+    for shift in range(1, tp_count):
+        outgoing = lax.dynamic_index_in_dim(chunks, (me + shift) % tp_count, axis=1, keepdims=False)
+        pairs = [(i, (i + shift) % tp_count) for i in range(tp_count)]
+        total = total + lax.ppermute(outgoing, "tp", pairs).astype(jnp.float32)
+    return total
 
 
 def tp_all_gather(share_values, tp_count):
     rows, share = share_values.shape
-    copies = jnp.broadcast_to(share_values[None], (tp_count, rows, share))
-    arrived = lax.all_to_all(copies, "tp", 0, 0, tiled=True)
-    return jnp.transpose(arrived, (1, 0, 2)).reshape(rows, tp_count * share)
+    me = lax.axis_index("tp")
+    gathered = jnp.zeros((rows, tp_count, share), share_values.dtype)
+    gathered = lax.dynamic_update_index_in_dim(gathered, share_values, me, axis=1)
+    for shift in range(1, tp_count):
+        pairs = [(i, (i + shift) % tp_count) for i in range(tp_count)]
+        arrived = lax.ppermute(share_values, "tp", pairs)
+        gathered = lax.dynamic_update_index_in_dim(
+            gathered, arrived, (me - shift) % tp_count, axis=1
+        )
+    return gathered.reshape(rows, tp_count * share)
 
 
 def attend_local(queries, suffix_kv, chosen, suffix_len, requests, slot_len):

time: 317 us -> 326 us (1.028)
  starting transfers between devices: 39.2 us -> 61.1 us
  waiting for transfers between devices: 110 us -> 95 us
    ppermute x0 -> x14, starting transfers between devices: none -> 34.4 us  [the longest x7 18.5 us: tp_reduce_scatter(): total = total + lax.ppermute(outgoing, 'tp', pairs).astype(jnp.float32)]
    all_to_all x2 -> x0, waiting for transfers between devices: 31.9 us -> none  [the longest x1 17 us: tp_reduce_scatter(): arrived = lax.all_to_all(chunks, 'tp', 0, 0, tiled=True)]
    ppermute x0 -> x14, waiting for transfers between devices: none -> 13.4 us  [the longest x7 7.75 us: tp_all_gather(): arrived = lax.ppermute(share_values, 'tp', pairs)]
    all_to_all x2 -> x0, starting transfers between devices: 12 us -> none  [the longest x1 8.47 us: tp_reduce_scatter(): arrived = lax.all_to_all(chunks, 'tp', 0, 0, tiled=True)]
    reduce_scatter x2, waiting for transfers between devices: 25.9 us -> 29.2 us  [per_device(): reduced = lax.psum_scatter(piece_out, 'tp', scatter_dimension=1, tiled=True)]
  transfers between devices with their start and end apart: 8 -> 20, of which waited for: 6 -> 8; matrix products, arithmetic and copies ran while one was open for 10% -> 10% of each run, Pallas kernels for 0% -> 0%
where the time goes in v7:
time: 326 us; the launch traced here: 323 us
  waiting for transfers between devices  95 us (29%)
  blocking collectives  71.2 us (22%)
  starting transfers between devices  61.1 us (19%)
  local copies, waits for them, and re-layouts  40 us (12%)
  matrix products  29.2 us (9%)
  between operations  14.4 us (4%)
  other arithmetic  11.7 us (4%)
    all_to_all x2, blocking collectives, per_device(): lax.all_to_all(outgoing, 'req', split_axis=0, concat_axis=0, tiled=True)  71.2 us
    reduce_scatter x2, waiting for transfers between devices, per_device(): reduced = lax.psum_scatter(piece_out, 'tp', scatter_dimension=1, tiled=True)  29.2 us
    all_to_all x1, waiting for transfers between devices, fetch_prefixes(): arrived = lax.all_to_all(outgoing, 'req', 0, 0, tiled=True)  26.5 us
    all_to_all x1, waiting for transfers between devices, fetch_prefixes(): scattered = lax.all_to_all(tagged, 'req', 0, 0, tiled=True)  18.8 us
    ppermute x7, starting transfers between devices, tp_reduce_scatter(): total = total + lax.ppermute(outgoing, 'tp', pairs).astype(jnp.float32)  18.5 us
    ppermute x7, starting transfers between devices, tp_all_gather(): arrived = lax.ppermute(share_values, 'tp', pairs)  15.8 us
    dot_general x2, matrix products, expert_apply(): jnp.dot(hidden_units, w_down[0], preferred_element_type=jnp.float32)  12.7 us
    all_to_all x2, starting transfers between devices, send_back(): return lax.all_to_all(parts, 'req', split_axis=0, concat_axis=0, tiled=True)  12.4 us
  transfers between devices with their start and end apart: 20, of which 8 were waited for; matrix products, arithmetic and copies ran while one was open for 10% of the time, Pallas kernels for 0%

profile of v7, /device:TPU:2, one launch (start us, length us, event | category | flops | bytes accessed | tf_op | source)
XLA Modules:
  0.0 322.7 jit_solution(17783955283670329209)
XLA Ops:
  10.1 7.6 %all-to-all-start = ((bf16[32,80,2,128]{3,1,2,0:T(8,128)(2,1)}), bf16[32,80,2,128]{3,1,2,0:T(8,128)(2,1)S(1)}, u32[]{:S(2)}, u32[]{:S(2)}) async-start(bf16[32,80,2,128]{3,1,2,0:T(8,128)(2,1)} %pad_maximum_fusion), calls=%async_computation | async-start | bytes 2621440 | tf_op jit(solution)/shard_map/all_to_all | solution.py:35
  17.8 18.8 %all-to-all-done = bf16[32,80,2,128]{3,1,2,0:T(8,128)(2,1)S(1)} async-done(((bf16[32,80,2,128]{3,1,2,0:T(8,128)(2,1)}), bf16[32,80,2,128]{3,1,2,0:T(8,128)(2,1)S(1)}, u32[]{:S(2)}, u32[]{:S(2)}) %all-to-all-start) | async-done | bytes 1310752 | tf_op jit(solution)/shard_map/all_to_all | solution.py:35
  42.1 3.2 copy_select_fusion
  45.3 6.5 %all-to-all-start.1 = ((bf16[32,2,64,2,128]{4,2,1,3,0:T(8,128)(2,1)}), bf16[32,2,64,2,128]{4,2,1,3,0:T(8,128)(2,1)}, u32[]{:S(2)}, u32[]{:S(2)}) async-start(bf16[32,2,64,2,128]{4,2,1,3,0:T(8,128)(2,1)} %copy_select_fusion), calls=%async_computation.1 | async-start | bytes 4194304 | tf_op jit(solution)/shard_map/all_to_all | solution.py:41
  53.3 26.5 %all-to-all-done.1 = bf16[32,2,64,2,128]{4,2,1,3,0:T(8,128)(2,1)} async-done(((bf16[32,2,64,2,128]{4,2,1,3,0:T(8,128)(2,1)}), bf16[32,2,64,2,128]{4,2,1,3,0:T(8,128)(2,1)}, u32[]{:S(2)}, u32[]{:S(2)}) %all-to-all-start.1) | async-done | bytes 2097184 | tf_op jit(solution)/shard_map/all_to_all | solution.py:41
  87.0 5.9 %collective-permute-start.6 = (bf16[64,512]{1,0:T(8,128)(2,1)S(1)}, bf16[64,512]{1,0:T(8,128)(2,1)S(1)}, u32[]{:S(2)}, u32[]{:S(2)}) collective-permute-start(bf16[64,512]{1,0:T(8,128)(2,1)S(1)} %bitcast.201), channel_id=1, source_target_pairs={{0,7},{1,0},{2,1},{3,2},{4,3},{5,4},{6,5},{7,6},{8,15},{9,8},{10,9... | collective-permute-start | bytes 196616 | tf_op jit(solution)/shard_map/ppermute | solution.py:54
  93.4 4.4 %collective-permute-start.2 = (bf16[64,512]{1,0:T(8,128)(2,1)S(1)}, bf16[64,512]{1,0:T(8,128)(2,1)S(1)}, u32[]{:S(2)}, u32[]{:S(2)}) collective-permute-start(bf16[64,512]{1,0:T(8,128)(2,1)S(1)} %bitcast.202), channel_id=1, source_target_pairs={{0,3},{1,4},{2,5},{3,6},{4,7},{5,0},{6,1},{7,2},{8,11},{9,12},{10,... | collective-permute-start | bytes 196616 | tf_op jit(solution)/shard_map/ppermute | solution.py:54
  100.0 3.3 %collective-permute-start.4 = (bf16[64,512]{1,0:T(8,128)(2,1)S(1)}, bf16[64,512]{1,0:T(8,128)(2,1)S(1)}, u32[]{:S(2)}, u32[]{:S(2)}) collective-permute-start(bf16[64,512]{1,0:T(8,128)(2,1)S(1)} %bitcast.197), channel_id=1, source_target_pairs={{0,5},{1,6},{2,7},{3,0},{4,1},{5,2},{6,3},{7,4},{8,13},{9,14},{10,... | collective-permute-start | bytes 196616 | tf_op jit(solution)/shard_map/ppermute | solution.py:54
  116.1 3.0 collective-permute-start.11
  119.1 3.5 %collective-permute-start.10 = (bf16[64,512]{1,0:T(8,128)(2,1)S(1)}, bf16[64,512]{1,0:T(8,128)(2,1)S(1)}, u32[]{:S(2)}, u32[]{:S(2)}) collective-permute-start(bf16[64,512]{1,0:T(8,128)(2,1)S(1)} %get-tuple-element.20), channel_id=1, source_target_pairs={{0,4},{1,5},{2,6},{3,7},{4,0},{5,1},{6,2},{7,3},{8,12},{9,13},{10,... | collective-permute-start | bytes 196616 | tf_op jit(solution)/shard_map/ppermute | solution.py:65
  125.7 5.6 %collective-permute-done.8 = bf16[64,512]{1,0:T(8,128)(2,1)S(1)} collective-permute-done((bf16[64,512]{1,0:T(8,128)(2,1)S(1)}, bf16[64,512]{1,0:T(8,128)(2,1)S(1)}, u32[]{:S(2)}, u32[]{:S(2)}) %collective-permute-start.8) | collective-permute-done | bytes 65568 | tf_op jit(solution)/shard_map/ppermute | solution.py:65
  131.3 3.5 %collective-permute-start.13 = (bf16[64,512]{1,0:T(8,128)(2,1)S(1)}, bf16[64,512]{1,0:T(8,128)(2,1)S(1)}, u32[]{:S(2)}, u32[]{:S(2)}) collective-permute-start(bf16[64,512]{1,0:T(8,128)(2,1)S(1)} %get-tuple-element.20), channel_id=1, source_target_pairs={{0,7},{1,0},{2,1},{3,2},{4,3},{5,4},{6,5},{7,6},{8,15},{9,8},{10,9... | collective-permute-start | bytes 196616 | tf_op jit(solution)/shard_map/ppermute | solution.py:65
  148.7 36.2 %all_to_all.30 = bf16[32,288,128]{2,1,0:T(8,128)(2,1)} all-to-all(bf16[32,288,128]{2,1,0:T(8,128)(2,1)S(1)} %bitcast.182), channel_id=1, replica_groups=mesh['req'=32,'tp'=8] {'req'}, dimensions={0} | all-to-all | bytes 4718592 | tf_op jit(solution)/shard_map/all_to_all | solution.py:214
  184.9 4.9 %reshape.317 = bf16[288,4096]{1,0:T(8,128)(2,1)} reshape(bf16[32,288,128]{2,1,0:T(8,128)(2,1)} %all_to_all.30) | data formatting | bytes 4718592 | tf_op jit(solution)/shard_map/reshape | solution.py:141
  189.8 3.8 %fusion.9 = f32[288,256]{1,0:T(8,128)} fusion(bf16[288,4096]{1,0:T(8,128)(2,1)} %reshape.317, bf16[1,4096,256]{2,1,0:T(8,128)(2,1)} %param.26), kind=kOutput, calls=%fused_computation.17 | convolution fusion | flops 603979776 | bytes 4751360 | tf_op jit(solution)/shard_map/dot_general | solution.py:142
  193.7 6.3 %convolution_convert_fusion.1 = bf16[288,4096]{1,0:T(8,128)(2,1)} fusion(bf16[1,256,4096]{2,1,0:T(8,128)(2,1)S(1)} %copy-done, bf16[288,4096]{1,0:T(8,128)(2,1)} %reshape.317, bf16[1,4096,256]{2,1,0:T(8,128)(2,1)} %param.27, f32[288,256]{1,0:T(8,128)} %fusion.9), kind=kOutput, calls=%fused_computation.3 | convolution fusion | flops 1209581568 | bytes 9207808 | tf_op jit(solution)/shard_map/dot_general | solution.py:145
  206.2 35.0 %all_to_all.31 = bf16[32,288,128]{2,1,0:T(8,128)(2,1)} all-to-all(bf16[32,288,128]{2,1,0:T(8,128)(2,1)S(1)} %bitcast.183), channel_id=1, replica_groups=mesh['req'=32,'tp'=8] {'req'}, dimensions={0} | all-to-all | bytes 4718592 | tf_op jit(solution)/shard_map/all_to_all | solution.py:214
  241.2 4.9 %reshape.324 = bf16[288,4096]{1,0:T(8,128)(2,1)} reshape(bf16[32,288,128]{2,1,0:T(8,128)(2,1)} %all_to_all.31) | data formatting | bytes 4718592 | tf_op jit(solution)/shard_map/reshape | solution.py:141
  246.1 3.1 fusion.7
  249.2 6.3 %convolution_convert_fusion = bf16[288,4096]{1,0:T(8,128)(2,1)} fusion(bf16[1,256,4096]{2,1,0:T(8,128)(2,1)S(1)} %copy-done, bf16[288,4096]{1,0:T(8,128)(2,1)} %reshape.324, bf16[1,4096,256]{2,1,0:T(8,128)(2,1)} %param.27, f32[288,256]{1,0:T(8,128)S(1)} %fusion.7), kind=kOutput, calls=%fused_computation.2 | convolution fusion | flops 1209581568 | bytes 9207808 | tf_op jit(solution)/shard_map/dot_general | solution.py:145
  261.0 5.1 %all-to-all-start.3 = ((bf16[32,36,128]{2,1,0:T(8,128)(2,1)}), bf16[32,36,128]{2,1,0:T(8,128)(2,1)S(1)}, u32[]{:S(2)}, u32[]{:S(2)}) async-start(bf16[32,36,128]{2,1,0:T(8,128)(2,1)} %reshape.318), calls=%async_computation.4 | async-start | bytes 655360 | tf_op jit(solution)/shard_map/all_to_all | solution.py:152
  266.9 29.2 %reduce-scatter.5.cloned.1.call-done = bf16[288,512]{1,0:T(8,128)(2,1)} async-done(((bf16[288,4096]{1,0:T(8,128)(2,1)}), bf16[288,512]{1,0:T(8,128)(2,1)}) %reduce-scatter.5.cloned.1.call-update) | async-done | bytes 294928 | tf_op jit(solution)/shard_map/reduce_scatter | solution.py:216
  298.0 7.3 %all-to-all-start.5 = ((bf16[32,36,128]{2,1,0:T(8,128)(2,1)}), bf16[32,36,128]{2,1,0:T(8,128)(2,1)S(1)}, u32[]{:S(2)}, u32[]{:S(2)}) async-start(bf16[32,36,128]{2,1,0:T(8,128)(2,1)} %reshape.325), calls=%async_computation.7 | async-start | bytes 655360 | tf_op jit(solution)/shard_map/all_to_all | solution.py:152
  306.4 7.2 %all-to-all-done.5 = bf16[32,36,128]{2,1,0:T(8,128)(2,1)S(1)} async-done(((bf16[32,36,128]{2,1,0:T(8,128)(2,1)}), bf16[32,36,128]{2,1,0:T(8,128)(2,1)S(1)}, u32[]{:S(2)}, u32[]{:S(2)}) %all-to-all-start.5) | async-done | bytes 294944 | tf_op jit(solution)/shard_map/all_to_all | solution.py:152
  (157 shorter events, 67.2 us)
Async XLA Ops:
  6.5 187.1 %copy-start = (bf16[1,256,4096]{2,1,0:T(8,128)(2,1)S(1)}, bf16[1,256,4096]{2,1,0:T(8,128)(2,1)}, u32[]{:S(2)}) copy-start(bf16[1,256,4096]{2,1,0:T(8,128)(2,1)} %param.28) | copy-start | bytes 6291460
  8.9 8.8 %copy-start.12 = (s32[4]{0:T(128)S(1)}, s32[4]{0:T(128)}, u32[]{:S(2)}) copy-start(s32[4]{0:T(128)} %param.19) | copy-start | bytes 52
  10.1 26.4 %all-to-all-start = ((bf16[32,80,2,128]{3,1,2,0:T(8,128)(2,1)}), bf16[32,80,2,128]{3,1,2,0:T(8,128)(2,1)S(1)}, u32[]{:S(2)}, u32[]{:S(2)}) async-start(bf16[32,80,2,128]{3,1,2,0:T(8,128)(2,1)} %pad_maximum_fusion), calls=%async_computation | async-start | bytes 2621440 | tf_op jit(solution)/shard_map/all_to_all | solution.py:35
  45.3 34.6 %all-to-all-start.1 = ((bf16[32,2,64,2,128]{4,2,1,3,0:T(8,128)(2,1)}), bf16[32,2,64,2,128]{4,2,1,3,0:T(8,128)(2,1)}, u32[]{:S(2)}, u32[]{:S(2)}) async-start(bf16[32,2,64,2,128]{4,2,1,3,0:T(8,128)(2,1)} %copy_select_fusion), calls=%async_computation.1 | async-start | bytes 4194304 | tf_op jit(solution)/shard_map/all_to_all | solution.py:41
  51.7 207.3 %reduce-scatter.3.cloned.1.call-start = ((), (), s32[]{:S(2)}) async-start(), calls=%async_computation.8 | async-start | bytes 2654208 | tf_op jit(solution)/shard_map/reduce_scatter | solution.py:216
  87.0 13.0 %collective-permute-start.6 = (bf16[64,512]{1,0:T(8,128)(2,1)S(1)}, bf16[64,512]{1,0:T(8,128)(2,1)S(1)}, u32[]{:S(2)}, u32[]{:S(2)}) collective-permute-start(bf16[64,512]{1,0:T(8,128)(2,1)S(1)} %bitcast.201), channel_id=1, source_target_pairs={{0,7},{1,0},{2,1},{3,2},{4,3},{5,4},{6,5},{7,6},{8,15},{9,8},{10,9... | collective-permute-start | bytes 196616 | tf_op jit(solution)/shard_map/ppermute | solution.py:54
  92.9 10.4 %collective-permute-start = (bf16[64,512]{1,0:T(8,128)(2,1)S(1)}, bf16[64,512]{1,0:T(8,128)(2,1)S(1)}, u32[]{:S(2)}, u32[]{:S(2)}) collective-permute-start(bf16[64,512]{1,0:T(8,128)(2,1)S(1)} %bitcast.198), channel_id=1, source_target_pairs={{0,1},{1,2},{2,3},{3,4},{4,5},{5,6},{6,7},{7,0},{8,9},{9,10},{10,1... | collective-permute-start | bytes 196616 | tf_op jit(solution)/shard_map/ppermute | solution.py:54
  93.2 18.9 %copy-start.9 = (s32[64,2]{1,0:T(8,128)}, s32[64,2]{1,0:T(8,128)S(1)}, u32[]{:S(2)}) copy-start(s32[64,2]{1,0:T(8,128)S(1)} %eq.68) | copy-start | bytes 1540
  93.3 13.2 %collective-permute-start.1 = (bf16[64,512]{1,0:T(8,128)(2,1)S(1)}, bf16[64,512]{1,0:T(8,128)(2,1)S(1)}, u32[]{:S(2)}, u32[]{:S(2)}) collective-permute-start(bf16[64,512]{1,0:T(8,128)(2,1)S(1)} %bitcast.203), channel_id=1, source_target_pairs={{0,2},{1,3},{2,4},{3,5},{4,6},{5,7},{6,0},{7,1},{8,10},{9,11},{10,... | collective-permute-start | bytes 196616 | tf_op jit(solution)/shard_map/ppermute | solution.py:54
  93.4 13.1 %collective-permute-start.2 = (bf16[64,512]{1,0:T(8,128)(2,1)S(1)}, bf16[64,512]{1,0:T(8,128)(2,1)S(1)}, u32[]{:S(2)}, u32[]{:S(2)}) collective-permute-start(bf16[64,512]{1,0:T(8,128)(2,1)S(1)} %bitcast.202), channel_id=1, source_target_pairs={{0,3},{1,4},{2,5},{3,6},{4,7},{5,0},{6,1},{7,2},{8,11},{9,12},{10,... | collective-permute-start | bytes 196616 | tf_op jit(solution)/shard_map/ppermute | solution.py:54
  97.8 8.7 %collective-permute-start.3 = (bf16[64,512]{1,0:T(8,128)(2,1)S(1)}, bf16[64,512]{1,0:T(8,128)(2,1)S(1)}, u32[]{:S(2)}, u32[]{:S(2)}) collective-permute-start(bf16[64,512]{1,0:T(8,128)(2,1)S(1)} %bitcast.199), channel_id=1, source_target_pairs={{0,4},{1,5},{2,6},{3,7},{4,0},{5,1},{6,2},{7,3},{8,12},{9,13},{10,... | collective-permute-start | bytes 196616 | tf_op jit(solution)/shard_map/ppermute | solution.py:54
  100.0 9.4 %collective-permute-start.4 = (bf16[64,512]{1,0:T(8,128)(2,1)S(1)}, bf16[64,512]{1,0:T(8,128)(2,1)S(1)}, u32[]{:S(2)}, u32[]{:S(2)}) collective-permute-start(bf16[64,512]{1,0:T(8,128)(2,1)S(1)} %bitcast.197), channel_id=1, source_target_pairs={{0,5},{1,6},{2,7},{3,0},{4,1},{5,2},{6,3},{7,4},{8,13},{9,14},{10,... | collective-permute-start | bytes 196616 | tf_op jit(solution)/shard_map/ppermute | solution.py:54
  103.3 8.8 %collective-permute-start.5 = (bf16[64,512]{1,0:T(8,128)(2,1)S(1)}, bf16[64,512]{1,0:T(8,128)(2,1)S(1)}, u32[]{:S(2)}, u32[]{:S(2)}) collective-permute-start(bf16[64,512]{1,0:T(8,128)(2,1)S(1)} %bitcast.196), channel_id=1, source_target_pairs={{0,6},{1,7},{2,0},{3,1},{4,2},{5,3},{6,4},{7,5},{8,14},{9,15},{10,... | collective-permute-start | bytes 196616 | tf_op jit(solution)/shard_map/ppermute | solution.py:54
  112.9 11.3 %collective-permute-start.7 = (bf16[64,512]{1,0:T(8,128)(2,1)S(1)}, bf16[64,512]{1,0:T(8,128)(2,1)S(1)}, u32[]{:S(2)}, u32[]{:S(2)}) collective-permute-start(bf16[64,512]{1,0:T(8,128)(2,1)S(1)} %get-tuple-element.20), channel_id=1, source_target_pairs={{0,1},{1,2},{2,3},{3,4},{4,5},{5,6},{6,7},{7,0},{8,9},{9,10},{10,1... | collective-permute-start | bytes 196616 | tf_op jit(solution)/shard_map/ppermute | solution.py:65
  113.5 21.4 %collective-permute-start.12 = (bf16[64,512]{1,0:T(8,128)(2,1)S(1)}, bf16[64,512]{1,0:T(8,128)(2,1)S(1)}, u32[]{:S(2)}, u32[]{:S(2)}) collective-permute-start(bf16[64,512]{1,0:T(8,128)(2,1)S(1)} %get-tuple-element.20), channel_id=1, source_target_pairs={{0,6},{1,7},{2,0},{3,1},{4,2},{5,3},{6,4},{7,5},{8,14},{9,15},{10,... | collective-permute-start | bytes 196616 | tf_op jit(solution)/shard_map/ppermute | solution.py:65
  116.1 18.8 %collective-permute-start.11 = (bf16[64,512]{1,0:T(8,128)(2,1)S(1)}, bf16[64,512]{1,0:T(8,128)(2,1)S(1)}, u32[]{:S(2)}, u32[]{:S(2)}) collective-permute-start(bf16[64,512]{1,0:T(8,128)(2,1)S(1)} %get-tuple-element.20), channel_id=1, source_target_pairs={{0,5},{1,6},{2,7},{3,0},{4,1},{5,2},{6,3},{7,4},{8,13},{9,14},{10,... | collective-permute-start | bytes 196616 | tf_op jit(solution)/shard_map/ppermute | solution.py:65
  119.1 15.7 %collective-permute-start.10 = (bf16[64,512]{1,0:T(8,128)(2,1)S(1)}, bf16[64,512]{1,0:T(8,128)(2,1)S(1)}, u32[]{:S(2)}, u32[]{:S(2)}) collective-permute-start(bf16[64,512]{1,0:T(8,128)(2,1)S(1)} %get-tuple-element.20), channel_id=1, source_target_pairs={{0,4},{1,5},{2,6},{3,7},{4,0},{5,1},{6,2},{7,3},{8,12},{9,13},{10,... | collective-permute-start | bytes 196616 | tf_op jit(solution)/shard_map/ppermute | solution.py:65
  122.6 12.2 %collective-permute-start.9 = (bf16[64,512]{1,0:T(8,128)(2,1)S(1)}, bf16[64,512]{1,0:T(8,128)(2,1)S(1)}, u32[]{:S(2)}, u32[]{:S(2)}) collective-permute-start(bf16[64,512]{1,0:T(8,128)(2,1)S(1)} %get-tuple-element.20), channel_id=1, source_target_pairs={{0,3},{1,4},{2,5},{3,6},{4,7},{5,0},{6,1},{7,2},{8,11},{9,12},{10,... | collective-permute-start | bytes 196616 | tf_op jit(solution)/shard_map/ppermute | solution.py:65
  124.2 7.1 %collective-permute-start.8 = (bf16[64,512]{1,0:T(8,128)(2,1)S(1)}, bf16[64,512]{1,0:T(8,128)(2,1)S(1)}, u32[]{:S(2)}, u32[]{:S(2)}) collective-permute-start(bf16[64,512]{1,0:T(8,128)(2,1)S(1)} %get-tuple-element.20), channel_id=1, source_target_pairs={{0,2},{1,3},{2,4},{3,5},{4,6},{5,7},{6,0},{7,1},{8,10},{9,11},{10,... | collective-permute-start | bytes 196616 | tf_op jit(solution)/shard_map/ppermute | solution.py:65
  131.3 6.0 %collective-permute-start.13 = (bf16[64,512]{1,0:T(8,128)(2,1)S(1)}, bf16[64,512]{1,0:T(8,128)(2,1)S(1)}, u32[]{:S(2)}, u32[]{:S(2)}) collective-permute-start(bf16[64,512]{1,0:T(8,128)(2,1)S(1)} %get-tuple-element.20), channel_id=1, source_target_pairs={{0,7},{1,0},{2,1},{3,2},{4,3},{5,4},{6,5},{7,6},{8,15},{9,8},{10,9... | collective-permute-start | bytes 196616 | tf_op jit(solution)/shard_map/ppermute | solution.py:65
  200.0 96.1 %reduce-scatter.5.cloned.1.call-start = ((), (), s32[]{:S(2)}) async-start(), calls=%async_computation.9 | async-start | bytes 2654208 | tf_op jit(solution)/shard_map/reduce_scatter | solution.py:216
  255.6 10.6 %copy-start.10 = (s32[64,2]{1,0:T(8,128)S(1)}, s32[64,2]{1,0:T(8,128)}, u32[]{:S(2)}) copy-start(s32[64,2]{1,0:T(8,128)} %copy-done.9) | copy-start | bytes 1540
  261.0 37.1 %all-to-all-start.3 = ((bf16[32,36,128]{2,1,0:T(8,128)(2,1)}), bf16[32,36,128]{2,1,0:T(8,128)(2,1)S(1)}, u32[]{:S(2)}, u32[]{:S(2)}) async-start(bf16[32,36,128]{2,1,0:T(8,128)(2,1)} %reshape.318), calls=%async_computation.4 | async-start | bytes 655360 | tf_op jit(solution)/shard_map/all_to_all | solution.py:152
  298.0 15.6 %all-to-all-start.5 = ((bf16[32,36,128]{2,1,0:T(8,128)(2,1)}), bf16[32,36,128]{2,1,0:T(8,128)(2,1)S(1)}, u32[]{:S(2)}, u32[]{:S(2)}) async-start(bf16[32,36,128]{2,1,0:T(8,128)(2,1)} %reshape.325), calls=%async_computation.7 | async-start | bytes 655360 | tf_op jit(solution)/shard_map/all_to_all | solution.py:152
  (10 other events, 47.7 us)
Sparse Core Ops, SparseCore 0:
  200.1 40.3 reduce-scatter.2
  255.7 40.3 reduce-scatter.4

commit v8 on v6

--- a/solution.py
+++ b/solution.py
@@ -128,9 +128,17 @@
 
 
 def expert_apply(arrived, w_gate, w_up, w_down):
-    flat_rows = arrived.reshape(-1, w_gate.shape[1])
-    gate_value = jnp.dot(flat_rows, w_gate[0], preferred_element_type=jnp.float32)
-    up_value = jnp.dot(flat_rows, w_up[0], preferred_element_type=jnp.float32)
+    model_width = w_gate.shape[1]
+    blocks = model_width // LANES
+    packed = arrived.reshape(-1, blocks, LANES)
+    gate_value = jnp.einsum(
+        "rkl,klh->rh", packed, w_gate[0].reshape(blocks, LANES, -1),
+        preferred_element_type=jnp.float32,
+    )
+    up_value = jnp.einsum(
+        "rkl,klh->rh", packed, w_up[0].reshape(blocks, LANES, -1),
+        preferred_element_type=jnp.float32,
+    )
     hidden_units = (jax.nn.silu(gate_value) * up_value).astype(jnp.bfloat16)
     piece_out = jnp.dot(hidden_units, w_down[0], preferred_element_type=jnp.float32).astype(
         jnp.bfloat16

time: 317 us -> 304 us (0.959)
  local copies, waits for them, and re-layouts: 37.9 us -> 29.5 us
  matrix products: 31.4 us -> 27.2 us
    reshape x2 -> x0, local copies, waits for them, and re-layouts: 9.89 us -> none  [expert_apply(): flat_rows = arrived.reshape(-1, w_gate.shape[1])]
    dot_general x2, matrix products: 7.59 us -> 3.19 us  [expert_apply(): jnp.einsum('rkl,klh->rh', packed, w_gate[0].reshape(blocks, LANES, -1), p...]
  transfers between devices with their start and end apart: 8 -> 8, of which waited for: 6 -> 6; matrix products, arithmetic and copies ran while one was open for 10% -> 9% of each run, Pallas kernels for 0% -> 0%
where the time goes in v8:
time: 304 us; the launch traced here: 300 us
  waiting for transfers between devices  110 us (36%)
  blocking collectives  72.2 us (24%)
  starting transfers between devices  38.8 us (13%)
  local copies, waits for them, and re-layouts  29.5 us (10%)
  matrix products  27.2 us (9%)
  between operations  13.9 us (5%)
  other arithmetic  8.54 us (3%)
    all_to_all x2, blocking collectives, per_device(): lax.all_to_all(outgoing, 'req', split_axis=0, concat_axis=0, tiled=True)  72.2 us
    all_to_all x1, waiting for transfers between devices, fetch_prefixes(): arrived = lax.all_to_all(outgoing, 'req', 0, 0, tiled=True)  27.6 us
    reduce_scatter x2, waiting for transfers between devices, per_device(): reduced = lax.psum_scatter(piece_out, 'tp', scatter_dimension=1, tiled=True)  25.8 us
    all_to_all x1, waiting for transfers between devices, fetch_prefixes(): scattered = lax.all_to_all(tagged, 'req', 0, 0, tiled=True)  18.8 us
    all_to_all x1, waiting for transfers between devices, tp_reduce_scatter(): arrived = lax.all_to_all(chunks, 'tp', 0, 0, tiled=True)  17 us
    all_to_all x1, waiting for transfers between devices, tp_all_gather(): arrived = lax.all_to_all(copies, 'tp', 0, 0, tiled=True)  14.9 us
    dot_general x2, matrix products, expert_apply(): jnp.dot(hidden_units, w_down[0], preferred_element_type=jnp.float32)  12.9 us
    all_to_all x2, starting transfers between devices, send_back(): return lax.all_to_all(parts, 'req', split_axis=0, concat_axis=0, tiled=True)  12.5 us
  transfers between devices with their start and end apart: 8, of which 6 were waited for; matrix products, arithmetic and copies ran while one was open for 9% of the time, Pallas kernels for 0%

profile of v8, /device:TPU:2, one launch (start us, length us, event | category | flops | bytes accessed | tf_op | source)
XLA Modules:
  0.0 300.3 jit_solution(2610086734243404592)
XLA Ops:
  10.1 7.6 %all-to-all-start = ((bf16[32,80,2,128]{3,1,2,0:T(8,128)(2,1)}), bf16[32,80,2,128]{3,1,2,0:T(8,128)(2,1)S(1)}, u32[]{:S(2)}, u32[]{:S(2)}) async-start(bf16[32,80,2,128]{3,1,2,0:T(8,128)(2,1)} %pad_maximum_fusion), calls=%async_computation | async-start | bytes 2621440 | tf_op jit(solution)/shard_map/all_to_all | solution.py:35
  17.7 18.8 %all-to-all-done = bf16[32,80,2,128]{3,1,2,0:T(8,128)(2,1)S(1)} async-done(((bf16[32,80,2,128]{3,1,2,0:T(8,128)(2,1)}), bf16[32,80,2,128]{3,1,2,0:T(8,128)(2,1)S(1)}, u32[]{:S(2)}, u32[]{:S(2)}) %all-to-all-start) | async-done | bytes 1310752 | tf_op jit(solution)/shard_map/all_to_all | solution.py:35
  39.9 2.1 gather_fusion.1
  42.0 3.2 %copy_select_fusion = bf16[32,2,64,2,128]{4,2,1,3,0:T(8,128)(2,1)} fusion(bf16[32,2,64,2,128]{4,2,3,1,0:T(8,128)(2,1)} %bitcast.152, pred[32,2]{1,0:T(8,128)(4,1)S(1)} %copy.171), kind=kLoop, calls=%fused_computation.11 | loop fusion | flops 1048576 | bytes 4194368 | tf_op jit(solution)/shard_map/jit(_take)/select_n | solution.py:38
  45.2 6.5 %all-to-all-start.1 = ((bf16[32,2,64,2,128]{4,2,1,3,0:T(8,128)(2,1)}), bf16[32,2,64,2,128]{4,2,1,3,0:T(8,128)(2,1)}, u32[]{:S(2)}, u32[]{:S(2)}) async-start(bf16[32,2,64,2,128]{4,2,1,3,0:T(8,128)(2,1)} %copy_select_fusion), calls=%async_computation.1 | async-start | bytes 4194304 | tf_op jit(solution)/shard_map/all_to_all | solution.py:41
  52.2 27.6 %all-to-all-done.1 = bf16[32,2,64,2,128]{4,2,1,3,0:T(8,128)(2,1)} async-done(((bf16[32,2,64,2,128]{4,2,1,3,0:T(8,128)(2,1)}), bf16[32,2,64,2,128]{4,2,1,3,0:T(8,128)(2,1)}, u32[]{:S(2)}, u32[]{:S(2)}) %all-to-all-start.1) | async-done | bytes 2097184 | tf_op jit(solution)/shard_map/all_to_all | solution.py:41
  86.5 8.5 %all-to-all-start.2 = ((bf16[8,64,512]{2,1,0:T(8,128)(2,1)}), bf16[8,64,512]{2,1,0:T(8,128)(2,1)S(1)}, u32[]{:S(2)}, u32[]{:S(2)}) async-start(bf16[8,64,512]{2,1,0:T(8,128)(2,1)} %bitcast.144), calls=%async_computation.2 | async-start | bytes 1048576 | tf_op jit(solution)/shard_map/all_to_all | solution.py:51
  95.1 17.0 %all-to-all-done.2 = bf16[8,64,512]{2,1,0:T(8,128)(2,1)S(1)} async-done(((bf16[8,64,512]{2,1,0:T(8,128)(2,1)}), bf16[8,64,512]{2,1,0:T(8,128)(2,1)S(1)}, u32[]{:S(2)}, u32[]{:S(2)}) %all-to-all-start.2) | async-done | bytes 524320 | tf_op jit(solution)/shard_map/all_to_all | solution.py:51
  113.0 3.5 %all-to-all-start.3 = ((bf16[8,64,512]{2,1,0:T(8,128)(2,1)}), bf16[8,64,512]{2,1,0:T(8,128)(2,1)S(1)}, u32[]{:S(2)}, u32[]{:S(2)}) async-start(bf16[8,64,512]{2,1,0:T(8,128)(2,1)} %broadcast_in_dim.93), calls=%async_computation.3 | async-start | bytes 1048576 | tf_op jit(solution)/shard_map/all_to_all | solution.py:58
  118.5 14.9 %all-to-all-done.3 = bf16[8,64,512]{2,1,0:T(8,128)(2,1)S(1)} async-done(((bf16[8,64,512]{2,1,0:T(8,128)(2,1)}), bf16[8,64,512]{2,1,0:T(8,128)(2,1)S(1)}, u32[]{:S(2)}, u32[]{:S(2)}) %all-to-all-start.3) | async-done | bytes 524320 | tf_op jit(solution)/shard_map/all_to_all | solution.py:58
  137.1 2.1 tile.20
  140.7 37.2 %all_to_all.40 = bf16[32,288,128]{2,1,0:T(8,128)(2,1)S(1)} all-to-all(bf16[32,288,128]{2,1,0:T(8,128)(2,1)S(1)} %bitcast.150), channel_id=1, replica_groups=mesh['req'=32,'tp'=8] {'req'}, dimensions={0} | all-to-all | bytes 4718592 | tf_op jit(solution)/shard_map/all_to_all | solution.py:212
  179.5 6.5 %convolution_convert_fusion.1 = bf16[288,4096]{1,0:T(8,128)(2,1)} fusion(bf16[1,256,4096]{2,1,0:T(8,128)(2,1)} %param.28, bf16[32,128,256]{2,1,0:T(8,128)(2,1)S(1)} %bitcast.145, bf16[288,32,128]{2,1,0:T(8,128)(2,1)} %bitcast.156, f32[288,256]{1,0:T(8,128)} %fusion.12), kind=kOutput, calls=%fused_computation.3 | convolution fusion | flops 1209581568 | bytes 9207808 | tf_op jit(solution)/shard_map/dot_general | solution.py:143
  186.4 2.2 convolution_convert_fusion.2
  188.6 2.1 tile.23
  192.2 34.9 %all_to_all.41 = bf16[32,288,128]{2,1,0:T(8,128)(2,1)S(1)} all-to-all(bf16[32,288,128]{2,1,0:T(8,128)(2,1)S(1)} %bitcast.151), channel_id=1, replica_groups=mesh['req'=32,'tp'=8] {'req'}, dimensions={0} | all-to-all | bytes 4718592 | tf_op jit(solution)/shard_map/all_to_all | solution.py:212
  230.2 6.4 %convolution_convert_fusion = bf16[288,4096]{1,0:T(8,128)(2,1)} fusion(bf16[1,256,4096]{2,1,0:T(8,128)(2,1)} %param.28, bf16[32,128,256]{2,1,0:T(8,128)(2,1)S(1)} %bitcast.146, bf16[288,32,128]{2,1,0:T(8,128)(2,1)} %bitcast.158, f32[288,256]{1,0:T(8,128)} %fusion.18), kind=kOutput, calls=%fused_computation.2 | convolution fusion | flops 1209581568 | bytes 9207808 | tf_op jit(solution)/shard_map/dot_general | solution.py:143
  237.5 2.1 fusion.52
  240.1 1.9 reshape.319
  242.0 5.1 %all-to-all-start.5 = ((bf16[32,36,128]{2,1,0:T(8,128)(2,1)}), bf16[32,36,128]{2,1,0:T(8,128)(2,1)S(1)}, u32[]{:S(2)}, u32[]{:S(2)}) async-start(bf16[32,36,128]{2,1,0:T(8,128)(2,1)} %reshape.319), calls=%async_computation.6 | async-start | bytes 655360 | tf_op jit(solution)/shard_map/all_to_all | solution.py:150
  247.9 25.8 %reduce-scatter.5.cloned.1.call-done = bf16[288,512]{1,0:T(8,128)(2,1)} async-done(((bf16[288,4096]{1,0:T(8,128)(2,1)}), bf16[288,512]{1,0:T(8,128)(2,1)}) %reduce-scatter.5.cloned.1.call-update) | async-done | bytes 294928 | tf_op jit(solution)/shard_map/reduce_scatter | solution.py:214
  273.8 1.9 reshape.326
  275.7 7.4 %all-to-all-start.7 = ((bf16[32,36,128]{2,1,0:T(8,128)(2,1)}), bf16[32,36,128]{2,1,0:T(8,128)(2,1)S(1)}, u32[]{:S(2)}, u32[]{:S(2)}) async-start(bf16[32,36,128]{2,1,0:T(8,128)(2,1)} %reshape.326), calls=%async_computation.9 | async-start | bytes 655360 | tf_op jit(solution)/shard_map/all_to_all | solution.py:150
  285.3 6.1 %all-to-all-done.7 = bf16[32,36,128]{2,1,0:T(8,128)(2,1)S(1)} async-done(((bf16[32,36,128]{2,1,0:T(8,128)(2,1)}), bf16[32,36,128]{2,1,0:T(8,128)(2,1)S(1)}, u32[]{:S(2)}, u32[]{:S(2)}) %all-to-all-start.7) | async-done | bytes 294944 | tf_op jit(solution)/shard_map/all_to_all | solution.py:150
  (117 shorter events, 35.0 us)
Async XLA Ops:
  6.5 173.0 %copy-start = (bf16[1,4096,256]{2,1,0:T(8,128)(2,1)S(1)}, bf16[1,4096,256]{2,1,0:T(8,128)(2,1)}, u32[]{:S(2)}) copy-start(bf16[1,4096,256]{2,1,0:T(8,128)(2,1)} %param.27) | copy-start | bytes 6291460
  8.9 8.8 %copy-start.13 = (s32[4]{0:T(128)S(1)}, s32[4]{0:T(128)}, u32[]{:S(2)}) copy-start(s32[4]{0:T(128)} %param.19) | copy-start | bytes 52
  10.1 26.4 %all-to-all-start = ((bf16[32,80,2,128]{3,1,2,0:T(8,128)(2,1)}), bf16[32,80,2,128]{3,1,2,0:T(8,128)(2,1)S(1)}, u32[]{:S(2)}, u32[]{:S(2)}) async-start(bf16[32,80,2,128]{3,1,2,0:T(8,128)(2,1)} %pad_maximum_fusion), calls=%async_computation | async-start | bytes 2621440 | tf_op jit(solution)/shard_map/all_to_all | solution.py:35
  45.2 6.5 %copy-start.9 = (bf16[64,2,128]{2,1,0:T(2,128)(2,1)S(1)}, bf16[64,2,128]{2,1,0:T(2,128)(2,1)}, u32[]{:S(2)}) copy-start(bf16[64,2,128]{2,1,0:T(2,128)(2,1)} %param.17) | copy-start | bytes 98308
  45.2 6.5 %copy-start.8 = (bf16[64,512]{1,0:T(8,128)(2,1)S(1)}, bf16[64,512]{1,0:T(8,128)(2,1)}, u32[]{:S(2)}) copy-start(bf16[64,512]{1,0:T(8,128)(2,1)} %param.16) | copy-start | bytes 196612
  45.2 6.5 %copy-start.14 = (s32[2]{0:T(128)S(1)}, s32[2]{0:T(128)}, u32[]{:S(2)}) copy-start(s32[2]{0:T(128)} %param.21) | copy-start | bytes 28
  45.2 34.5 %all-to-all-start.1 = ((bf16[32,2,64,2,128]{4,2,1,3,0:T(8,128)(2,1)}), bf16[32,2,64,2,128]{4,2,1,3,0:T(8,128)(2,1)}, u32[]{:S(2)}, u32[]{:S(2)}) async-start(bf16[32,2,64,2,128]{4,2,1,3,0:T(8,128)(2,1)} %copy_select_fusion), calls=%async_computation.1 | async-start | bytes 4194304 | tf_op jit(solution)/shard_map/all_to_all | solution.py:41
  82.6 2.2 copy-start.3
  85.6 31.2 %copy-start.10 = (s32[64,2]{0,1:T(2,128)S(1)}, s32[64,2]{0,1:T(2,128)}, u32[]{:S(2)}) copy-start(s32[64,2]{0,1:T(2,128)} %param.25) | copy-start | bytes 1540
  86.5 25.6 %all-to-all-start.2 = ((bf16[8,64,512]{2,1,0:T(8,128)(2,1)}), bf16[8,64,512]{2,1,0:T(8,128)(2,1)S(1)}, u32[]{:S(2)}, u32[]{:S(2)}) async-start(bf16[8,64,512]{2,1,0:T(8,128)(2,1)} %bitcast.144), calls=%async_computation.2 | async-start | bytes 1048576 | tf_op jit(solution)/shard_map/all_to_all | solution.py:51
  113.0 20.4 %all-to-all-start.3 = ((bf16[8,64,512]{2,1,0:T(8,128)(2,1)}), bf16[8,64,512]{2,1,0:T(8,128)(2,1)S(1)}, u32[]{:S(2)}, u32[]{:S(2)}) async-start(bf16[8,64,512]{2,1,0:T(8,128)(2,1)} %broadcast_in_dim.93), calls=%async_computation.3 | async-start | bytes 1048576 | tf_op jit(solution)/shard_map/all_to_all | solution.py:58
  116.5 123.6 %reduce-scatter.3.cloned.1.call-start = ((), (), s32[]{:S(2)}) async-start(), calls=%async_computation.10 | async-start | bytes 2654208 | tf_op jit(solution)/shard_map/reduce_scatter | solution.py:214
  133.5 1.5 copy-start.1
  133.5 1.5 copy-start.7
  135.2 0.8 copy-start.2
  140.7 37.3 %copy-start.11 = (bf16[1,4096,256]{2,1,0:T(8,128)(2,1)S(1)}, bf16[1,4096,256]{2,1,0:T(8,128)(2,1)}, u32[]{:S(2)}) copy-start(bf16[1,4096,256]{2,1,0:T(8,128)(2,1)} %param.26) | copy-start | bytes 6291460
  177.9 1.6 copy-start.4
  186.0 87.8 %reduce-scatter.5.cloned.1.call-start = ((), (), s32[]{:S(2)}) async-start(), calls=%async_computation.11 | async-start | bytes 2654208 | tf_op jit(solution)/shard_map/reduce_scatter | solution.py:214
  192.2 36.4 %copy-start.12 = (bf16[1,4096,256]{2,1,0:T(8,128)(2,1)S(1)}, bf16[1,4096,256]{2,1,0:T(8,128)(2,1)}, u32[]{:S(2)}) copy-start(bf16[1,4096,256]{2,1,0:T(8,128)(2,1)} %param.26) | copy-start | bytes 6291460
  227.2 1.4 copy-start.5
  236.6 0.9 copy-start.6
  242.0 33.7 %all-to-all-start.5 = ((bf16[32,36,128]{2,1,0:T(8,128)(2,1)}), bf16[32,36,128]{2,1,0:T(8,128)(2,1)S(1)}, u32[]{:S(2)}, u32[]{:S(2)}) async-start(bf16[32,36,128]{2,1,0:T(8,128)(2,1)} %reshape.319), calls=%async_computation.6 | async-start | bytes 655360 | tf_op jit(solution)/shard_map/all_to_all | solution.py:150
  275.7 15.7 %all-to-all-start.7 = ((bf16[32,36,128]{2,1,0:T(8,128)(2,1)}), bf16[32,36,128]{2,1,0:T(8,128)(2,1)S(1)}, u32[]{:S(2)}, u32[]{:S(2)}) async-start(bf16[32,36,128]{2,1,0:T(8,128)(2,1)} %reshape.326), calls=%async_computation.9 | async-start | bytes 655360 | tf_op jit(solution)/shard_map/all_to_all | solution.py:150
Sparse Core Ops, SparseCore 0:
  186.1 37.1 reduce-scatter.2
  236.8 36.9 reduce-scatter.4

commit v9 on v8

--- a/solution.py
+++ b/solution.py
@@ -12,7 +12,7 @@
 NPFX = 4
 CAP = 18
 LANES = 128
-CHUNKS = 2
+CHUNK_SLOTS = (12, 6)
 
 
 def broadcast(x, axis, root):
@@ -196,14 +196,15 @@
     placing, combining = routing_tables(routes, live_rows, route_weight)
     repeats = req_count // EXPERTS
     tokens = routes.shape[0]
-    chunk_slots = CAP // CHUNKS
-    packed_rows = chunk_slots * model_width // LANES
     placing_blocks = placing.reshape(EXPERTS, CAP, tokens)
     combining_blocks = combining.reshape(tokens, EXPERTS, CAP)
-    share_rows = chunk_slots * share_width // LANES
     mixture_share = jnp.zeros((tokens, share_width), jnp.float32)
-    for chunk in range(CHUNKS):
-        slots = slice(chunk * chunk_slots, (chunk + 1) * chunk_slots)
+    first_slot = 0
+    for chunk_slots in CHUNK_SLOTS:
+        packed_rows = chunk_slots * model_width // LANES
+        share_rows = chunk_slots * share_width // LANES
+        slots = slice(first_slot, first_slot + chunk_slots)
+        first_slot += chunk_slots
         chunk_placing = placing_blocks[:, slots].reshape(EXPERTS * chunk_slots, tokens)
         send_rows = jnp.dot(chunk_placing, normed_full, preferred_element_type=jnp.float32).astype(
             jnp.bfloat16

time: 304 us -> 303 us (level)
  blocking collectives: 72.2 us -> 25.4 us
  waiting for transfers between devices: 110 us -> 146 us
  starting transfers between devices: 38.8 us -> 46.2 us
    all_to_all x2 -> x1, blocking collectives: 72.2 us -> 25.4 us  [tp_reduce_scatter(): arrived = lax.all_to_all(chunks, 'tp', 0, 0, tiled=True)]
    all_to_all x1 -> x2, waiting for transfers between devices: 17 us -> 49.2 us  [per_device(): lax.all_to_all(outgoing, 'req', split_axis=0, concat_axis=0, tiled=True)]
    all_to_all x1 -> x2, starting transfers between devices: 8.47 us -> 15 us  [per_device(): lax.all_to_all(outgoing, 'req', split_axis=0, concat_axis=0, tiled=True)]
    reduce_scatter x2, waiting for transfers between devices: 25.8 us -> 30.9 us  [per_device(): reduced = lax.psum_scatter(piece_out, 'tp', scatter_dimension=1, tiled=True)]
    dot_general x2, matrix products: 3.19 us -> 6.35 us  [expert_apply(): jnp.einsum('rkl,klh->rh', packed, w_gate[0].reshape(blocks, LANES, -1), p...]
    all_to_all x1, waiting for transfers between devices: 14.9 us -> 11.7 us  [tp_all_gather(): arrived = lax.all_to_all(copies, 'tp', 0, 0, tiled=True)]
  transfers between devices with their start and end apart: 8 -> 9, of which waited for: 6 -> 7; matrix products, arithmetic and copies ran while one was open for 9% -> 11% of each run, Pallas kernels for 0% -> 0%
where the time goes in v9:
time: 303 us; the launch traced here: 300 us
  waiting for transfers between devices  146 us (48%)
  starting transfers between devices  46.2 us (15%)
  local copies, waits for them, and re-layouts  30.5 us (10%)
  matrix products  29.5 us (10%)
  blocking collectives  25.4 us (8%)
  between operations  14 us (5%)
  other arithmetic  8.55 us (3%)
    all_to_all x2, waiting for transfers between devices, per_device(): lax.all_to_all(outgoing, 'req', split_axis=0, concat_axis=0, tiled=True)  49.2 us
    reduce_scatter x2, waiting for transfers between devices, per_device(): reduced = lax.psum_scatter(piece_out, 'tp', scatter_dimension=1, tiled=True)  30.9 us
    all_to_all x1, waiting for transfers between devices, fetch_prefixes(): arrived = lax.all_to_all(outgoing, 'req', 0, 0, tiled=True)  27.6 us
    all_to_all x1, blocking collectives, tp_reduce_scatter(): arrived = lax.all_to_all(chunks, 'tp', 0, 0, tiled=True)  25.4 us
    all_to_all x1, waiting for transfers between devices, fetch_prefixes(): scattered = lax.all_to_all(tagged, 'req', 0, 0, tiled=True)  18.8 us
    all_to_all x2, starting transfers between devices, per_device(): lax.all_to_all(outgoing, 'req', split_axis=0, concat_axis=0, tiled=True)  15 us
    all_to_all x2, starting transfers between devices, send_back(): return lax.all_to_all(parts, 'req', split_axis=0, concat_axis=0, tiled=True)  13.3 us
    dot_general x2, matrix products, expert_apply(): jnp.dot(hidden_units, w_down[0], preferred_element_type=jnp.float32)  12.8 us
  transfers between devices with their start and end apart: 9, of which 7 were waited for; matrix products, arithmetic and copies ran while one was open for 11% of the time, Pallas kernels for 0%

profile of v9, /device:TPU:2, one launch (start us, length us, event | category | flops | bytes accessed | tf_op | source)
XLA Modules:
  0.0 300.1 jit_solution(2891688587763217565)
XLA Ops:
  10.1 7.6 %all-to-all-start = ((bf16[32,80,2,128]{3,1,2,0:T(8,128)(2,1)}), bf16[32,80,2,128]{3,1,2,0:T(8,128)(2,1)S(1)}, u32[]{:S(2)}, u32[]{:S(2)}) async-start(bf16[32,80,2,128]{3,1,2,0:T(8,128)(2,1)} %pad_maximum_fusion), calls=%async_computation | async-start | bytes 2621440 | tf_op jit(solution)/shard_map/all_to_all | solution.py:35
  17.8 18.8 %all-to-all-done = bf16[32,80,2,128]{3,1,2,0:T(8,128)(2,1)S(1)} async-done(((bf16[32,80,2,128]{3,1,2,0:T(8,128)(2,1)}), bf16[32,80,2,128]{3,1,2,0:T(8,128)(2,1)S(1)}, u32[]{:S(2)}, u32[]{:S(2)}) %all-to-all-start) | async-done | bytes 1310752 | tf_op jit(solution)/shard_map/all_to_all | solution.py:35
  42.1 3.2 %copy_select_fusion = bf16[32,2,64,2,128]{4,2,1,3,0:T(8,128)(2,1)} fusion(bf16[32,2,64,2,128]{4,2,3,1,0:T(8,128)(2,1)} %bitcast.153, pred[32,2]{1,0:T(8,128)(4,1)S(1)} %copy.171), kind=kLoop, calls=%fused_computation.15 | loop fusion | flops 1048576 | bytes 4194368 | tf_op jit(solution)/shard_map/jit(_take)/select_n | solution.py:38
  45.3 6.5 %all-to-all-start.1 = ((bf16[32,2,64,2,128]{4,2,1,3,0:T(8,128)(2,1)}), bf16[32,2,64,2,128]{4,2,1,3,0:T(8,128)(2,1)}, u32[]{:S(2)}, u32[]{:S(2)}) async-start(bf16[32,2,64,2,128]{4,2,1,3,0:T(8,128)(2,1)} %copy_select_fusion), calls=%async_computation.1 | async-start | bytes 4194304 | tf_op jit(solution)/shard_map/all_to_all | solution.py:41
  52.2 27.6 %all-to-all-done.1 = bf16[32,2,64,2,128]{4,2,1,3,0:T(8,128)(2,1)} async-done(((bf16[32,2,64,2,128]{4,2,1,3,0:T(8,128)(2,1)}), bf16[32,2,64,2,128]{4,2,1,3,0:T(8,128)(2,1)}, u32[]{:S(2)}, u32[]{:S(2)}) %all-to-all-start.1) | async-done | bytes 2097184 | tf_op jit(solution)/shard_map/all_to_all | solution.py:41
  85.7 25.4 %all_to_all.40 = bf16[8,64,512]{2,1,0:T(8,128)(2,1)S(1)} all-to-all(bf16[8,64,512]{2,1,0:T(8,128)(2,1)S(1)} %bitcast.158), channel_id=1, replica_groups=mesh['req'=32,'tp'=8] {'tp'}, dimensions={0} | all-to-all | bytes 1048576 | tf_op jit(solution)/shard_map/all_to_all | solution.py:51
  112.7 3.5 %all-to-all-start.3 = ((bf16[8,64,512]{2,1,0:T(8,128)(2,1)}), bf16[8,64,512]{2,1,0:T(8,128)(2,1)S(1)}, u32[]{:S(2)}, u32[]{:S(2)}) async-start(bf16[8,64,512]{2,1,0:T(8,128)(2,1)} %broadcast_in_dim.93), calls=%async_computation.3 | async-start | bytes 1048576 | tf_op jit(solution)/shard_map/all_to_all | solution.py:58
  120.2 11.7 %all-to-all-done.3 = bf16[8,64,512]{2,1,0:T(8,128)(2,1)S(1)} async-done(((bf16[8,64,512]{2,1,0:T(8,128)(2,1)}), bf16[8,64,512]{2,1,0:T(8,128)(2,1)S(1)}, u32[]{:S(2)}, u32[]{:S(2)}) %all-to-all-start.3) | async-done | bytes 524320 | tf_op jit(solution)/shard_map/all_to_all | solution.py:58
  136.2 2.6 tile.24
  138.8 8.4 %all-to-all-start.6 = ((bf16[32,192,128]{2,1,0:T(8,128)(2,1)}), bf16[32,192,128]{2,1,0:T(8,128)(2,1)}, u32[]{:S(2)}, u32[]{:S(2)}) async-start(bf16[32,192,128]{2,1,0:T(8,128)(2,1)} %bitcast.154), calls=%async_computation.7 | async-start | bytes 3145728 | tf_op jit(solution)/shard_map/all_to_all | solution.py:213
  147.4 2.3 convolution_convert_fusion.2
  149.7 2.2 tile.20
  151.8 17.4 %all-to-all-done.6 = bf16[32,192,128]{2,1,0:T(8,128)(2,1)} async-done(((bf16[32,192,128]{2,1,0:T(8,128)(2,1)}), bf16[32,192,128]{2,1,0:T(8,128)(2,1)}, u32[]{:S(2)}, u32[]{:S(2)}) %all-to-all-start.6) | async-done | bytes 1572896 | tf_op jit(solution)/shard_map/all_to_all | solution.py:213
  169.2 3.5 %tile.21 = bf16[4,8,384,128]{3,2,1,0:T(8,128)(2,1)} broadcast(bf16[8,384,128]{2,1,0:T(8,128)(2,1)} %tile.20), dimensions={1,2,3} | broadcast | bytes 3932160 | tf_op jit(solution)/shard_map/tile | solution.py:212
  172.8 6.6 %all-to-all-start.4 = ((bf16[32,384,128]{2,1,0:T(8,128)(2,1)}), bf16[32,384,128]{2,1,0:T(8,128)(2,1)}, u32[]{:S(2)}, u32[]{:S(2)}) async-start(bf16[32,384,128]{2,1,0:T(8,128)(2,1)} %bitcast.152), calls=%async_computation.4 | async-start | bytes 6291456 | tf_op jit(solution)/shard_map/all_to_all | solution.py:213
  179.6 2.7 fusion.24
  182.3 5.2 %convolution_convert_fusion.1 = bf16[192,4096]{1,0:T(8,128)(2,1)} fusion(bf16[1,256,4096]{2,1,0:T(8,128)(2,1)} %param.28, bf16[32,128,256]{2,1,0:T(8,128)(2,1)S(1)} %bitcast.148, bf16[192,32,128]{2,1,0:T(8,128)(2,1)} %bitcast.42, f32[192,256]{1,0:T(8,128)S(1)} %fusion.24), kind=kOutput, calls=%fused_computation.3 | convolution fusion | flops 806387712 | bytes 7536640 | tf_op jit(solution)/shard_map/dot_general | solution.py:143
  187.6 31.8 %all-to-all-done.4 = bf16[32,384,128]{2,1,0:T(8,128)(2,1)} async-done(((bf16[32,384,128]{2,1,0:T(8,128)(2,1)}), bf16[32,384,128]{2,1,0:T(8,128)(2,1)}, u32[]{:S(2)}, u32[]{:S(2)}) %all-to-all-start.4) | async-done | bytes 3145760 | tf_op jit(solution)/shard_map/all_to_all | solution.py:213
  219.4 3.6 %fusion.12 = f32[384,256]{1,0:T(8,128)S(1)} fusion(bf16[32,128,256]{2,1,0:T(8,128)(2,1)} %bitcast.168, bf16[384,32,128]{2,1,0:T(8,128)(2,1)} %bitcast.34), kind=kOutput, calls=%fused_computation.24 | convolution fusion | flops 805306368 | bytes 5636096 | tf_op jit(solution)/shard_map/rkl,klh->rh/dot_general | solution.py:134
  223.0 7.7 %convolution_convert_fusion = bf16[384,4096]{1,0:T(8,128)(2,1)} fusion(bf16[1,256,4096]{2,1,0:T(8,128)(2,1)} %param.28, bf16[32,128,256]{2,1,0:T(8,128)(2,1)S(1)} %bitcast.147, bf16[384,32,128]{2,1,0:T(8,128)(2,1)} %bitcast.34, f32[384,256]{1,0:T(8,128)S(1)} %fusion.12), kind=kOutput, calls=%fused_computation.2 | convolution fusion | flops 1612775424 | bytes 10878976 | tf_op jit(solution)/shard_map/dot_general | solution.py:143
  235.9 5.9 %all-to-all-start.7 = ((bf16[32,24,128]{2,1,0:T(8,128)(2,1)}), bf16[32,24,128]{2,1,0:T(8,128)(2,1)S(1)}, u32[]{:S(2)}, u32[]{:S(2)}) async-start(bf16[32,24,128]{2,1,0:T(8,128)(2,1)} %reshape.326), calls=%async_computation.9 | async-start | bytes 393216 | tf_op jit(solution)/shard_map/all_to_all | solution.py:150
  241.8 30.9 %reduce-scatter.3.cloned.1.call-done = bf16[384,512]{1,0:T(8,128)(2,1)} async-done(((bf16[384,4096]{1,0:T(8,128)(2,1)}), bf16[384,512]{1,0:T(8,128)(2,1)}) %reduce-scatter.3.cloned.1.call-update) | async-done | bytes 393232 | tf_op jit(solution)/shard_map/reduce_scatter | solution.py:215
  274.7 7.4 %all-to-all-start.5 = ((bf16[32,48,128]{2,1,0:T(8,128)(2,1)}), bf16[32,48,128]{2,1,0:T(8,128)(2,1)S(1)}, u32[]{:S(2)}, u32[]{:S(2)}) async-start(bf16[32,48,128]{2,1,0:T(8,128)(2,1)} %reshape.319), calls=%async_computation.6 | async-start | bytes 786432 | tf_op jit(solution)/shard_map/all_to_all | solution.py:150
  283.4 7.6 %all-to-all-done.5 = bf16[32,48,128]{2,1,0:T(8,128)(2,1)S(1)} async-done(((bf16[32,48,128]{2,1,0:T(8,128)(2,1)}), bf16[32,48,128]{2,1,0:T(8,128)(2,1)S(1)}, u32[]{:S(2)}, u32[]{:S(2)}) %all-to-all-start.5) | async-done | bytes 393248 | tf_op jit(solution)/shard_map/all_to_all | solution.py:150
  (136 shorter events, 36.0 us)
Async XLA Ops:
  6.5 175.8 %copy-start = (bf16[1,4096,256]{2,1,0:T(8,128)(2,1)S(1)}, bf16[1,4096,256]{2,1,0:T(8,128)(2,1)}, u32[]{:S(2)}) copy-start(bf16[1,4096,256]{2,1,0:T(8,128)(2,1)} %param.27) | copy-start | bytes 6291460
  8.9 8.8 %copy-start.22 = (s32[4]{0:T(128)S(1)}, s32[4]{0:T(128)}, u32[]{:S(2)}) copy-start(s32[4]{0:T(128)} %param.19) | copy-start | bytes 52
  10.1 26.4 %all-to-all-start = ((bf16[32,80,2,128]{3,1,2,0:T(8,128)(2,1)}), bf16[32,80,2,128]{3,1,2,0:T(8,128)(2,1)S(1)}, u32[]{:S(2)}, u32[]{:S(2)}) async-start(bf16[32,80,2,128]{3,1,2,0:T(8,128)(2,1)} %pad_maximum_fusion), calls=%async_computation | async-start | bytes 2621440 | tf_op jit(solution)/shard_map/all_to_all | solution.py:35
  45.3 6.5 %copy-start.14 = (bf16[64,2,128]{2,1,0:T(2,128)(2,1)S(1)}, bf16[64,2,128]{2,1,0:T(2,128)(2,1)}, u32[]{:S(2)}) copy-start(bf16[64,2,128]{2,1,0:T(2,128)(2,1)} %param.17) | copy-start | bytes 98308
  45.3 6.5 %copy-start.13 = (bf16[64,512]{1,0:T(8,128)(2,1)S(1)}, bf16[64,512]{1,0:T(8,128)(2,1)}, u32[]{:S(2)}) copy-start(bf16[64,512]{1,0:T(8,128)(2,1)} %param.16) | copy-start | bytes 196612
  45.3 6.6 %copy-start.23 = (s32[2]{0:T(128)S(1)}, s32[2]{0:T(128)}, u32[]{:S(2)}) copy-start(s32[2]{0:T(128)} %param.21) | copy-start | bytes 28
  45.3 34.6 %all-to-all-start.1 = ((bf16[32,2,64,2,128]{4,2,1,3,0:T(8,128)(2,1)}), bf16[32,2,64,2,128]{4,2,1,3,0:T(8,128)(2,1)}, u32[]{:S(2)}, u32[]{:S(2)}) async-start(bf16[32,2,64,2,128]{4,2,1,3,0:T(8,128)(2,1)} %copy_select_fusion), calls=%async_computation.1 | async-start | bytes 4194304 | tf_op jit(solution)/shard_map/all_to_all | solution.py:41
  82.6 2.2 copy-start.3
  85.6 31.0 %copy-start.21 = (s32[64,2]{0,1:T(2,128)S(1)}, s32[64,2]{0,1:T(2,128)}, u32[]{:S(2)}) copy-start(s32[64,2]{0,1:T(2,128)} %param.25) | copy-start | bytes 1540
  112.7 19.2 %all-to-all-start.3 = ((bf16[8,64,512]{2,1,0:T(8,128)(2,1)}), bf16[8,64,512]{2,1,0:T(8,128)(2,1)S(1)}, u32[]{:S(2)}, u32[]{:S(2)}) async-start(bf16[8,64,512]{2,1,0:T(8,128)(2,1)} %broadcast_in_dim.93), calls=%async_computation.3 | async-start | bytes 1048576 | tf_op jit(solution)/shard_map/all_to_all | solution.py:58
  116.4 15.5 %copy-start.19 = (pred[64]{0:T(512)(128)(4,1)}, pred[64]{0:T(512)(128)(4,1)S(1)}, u32[]{:S(2)}) copy-start(pred[64]{0:T(512)(128)(4,1)S(1)} %fusion.88) | copy-start | bytes 196
  132.0 2.0 copy-start.1
  132.1 2.8 copy-start.12
  136.2 11.0 %copy-start.7 = (bf16[8,18,64]{1,0,2:T(8,128)(2,1)S(1)}, bf16[8,18,64]{1,0,2:T(8,128)(2,1)}, u32[]{:S(2)}) copy-start(bf16[8,18,64]{1,0,2:T(8,128)(2,1)} %copy-done.6) | copy-start | bytes 55300
  138.8 30.5 %all-to-all-start.6 = ((bf16[32,192,128]{2,1,0:T(8,128)(2,1)}), bf16[32,192,128]{2,1,0:T(8,128)(2,1)}, u32[]{:S(2)}, u32[]{:S(2)}) async-start(bf16[32,192,128]{2,1,0:T(8,128)(2,1)} %bitcast.154), calls=%async_computation.7 | async-start | bytes 3145728 | tf_op jit(solution)/shard_map/all_to_all | solution.py:213
  172.8 46.6 %all-to-all-start.4 = ((bf16[32,384,128]{2,1,0:T(8,128)(2,1)}), bf16[32,384,128]{2,1,0:T(8,128)(2,1)}, u32[]{:S(2)}, u32[]{:S(2)}) async-start(bf16[32,384,128]{2,1,0:T(8,128)(2,1)} %bitcast.152), calls=%async_computation.4 | async-start | bytes 6291456 | tf_op jit(solution)/shard_map/all_to_all | solution.py:213
  179.4 54.8 %reduce-scatter.5.cloned.1.call-start = ((), (), s32[]{:S(2)}) async-start(), calls=%async_computation.11 | async-start | bytes 1769472 | tf_op jit(solution)/shard_map/reduce_scatter | solution.py:215
  187.5 85.2 %reduce-scatter.3.cloned.1.call-start = ((), (), s32[]{:S(2)}) async-start(), calls=%async_computation.10 | async-start | bytes 3538944 | tf_op jit(solution)/shard_map/reduce_scatter | solution.py:215
  230.7 3.0 copy-start.9
  231.6 50.6 %copy-start.16 = (s32[64,2]{1,0:T(8,128)S(1)}, s32[64,2]{1,0:T(8,128)}, u32[]{:S(2)}) copy-start(s32[64,2]{1,0:T(8,128)} %copy-done.15) | copy-start | bytes 1540
  231.6 50.6 %copy-start.20 = (pred[64]{0:T(512)(128)(4,1)S(1)}, pred[64]{0:T(512)(128)(4,1)}, u32[]{:S(2)}) copy-start(pred[64]{0:T(512)(128)(4,1)} %copy-done.19) | copy-start | bytes 196
  235.9 38.8 %all-to-all-start.7 = ((bf16[32,24,128]{2,1,0:T(8,128)(2,1)}), bf16[32,24,128]{2,1,0:T(8,128)(2,1)S(1)}, u32[]{:S(2)}, u32[]{:S(2)}) async-start(bf16[32,24,128]{2,1,0:T(8,128)(2,1)} %reshape.326), calls=%async_computation.9 | async-start | bytes 393216 | tf_op jit(solution)/shard_map/all_to_all | solution.py:150
  274.7 16.4 %all-to-all-start.5 = ((bf16[32,48,128]{2,1,0:T(8,128)(2,1)}), bf16[32,48,128]{2,1,0:T(8,128)(2,1)S(1)}, u32[]{:S(2)}, u32[]{:S(2)}) async-start(bf16[32,48,128]{2,1,0:T(8,128)(2,1)} %reshape.319), calls=%async_computation.6 | async-start | bytes 786432 | tf_op jit(solution)/shard_map/all_to_all | solution.py:150
  282.2 9.2 %copy-start.5 = (f32[64,512]{1,0:T(8,128)S(1)}, f32[64,512]{1,0:T(8,128)}, u32[]{:S(2)}) copy-start(f32[64,512]{1,0:T(8,128)} %copy-done.4) | copy-start | bytes 393220
  (9 other events, 7.7 us)
Sparse Core Ops, SparseCore 0:
  187.6 36.8 reduce-scatter.4
  230.8 41.8 reduce-scatter.2

commit v10 on v9

--- a/solution.py
+++ b/solution.py
@@ -33,9 +33,9 @@
         [pieces, jnp.broadcast_to(tags[None], (req_count, tag_rows, 2, width))], axis=1
     )
     scattered = lax.all_to_all(tagged, "req", 0, 0, tiled=True)
-    owner_pieces = jnp.take(scattered[:, :piece], prefix_owner, axis=0)
     wanted = scattered[:, piece, 0, :requests].astype(jnp.int32)
-    outgoing = jnp.take(owner_pieces, wanted.reshape(-1), axis=0).reshape(
+    sources = jnp.take(prefix_owner, wanted.reshape(-1), axis=0)
+    outgoing = jnp.take(scattered, sources, axis=0)[:, :piece].reshape(
         req_count, requests, piece, 2, width
     )
     arrived = lax.all_to_all(outgoing, "req", 0, 0, tiled=True)
@@ -197,6 +197,7 @@
     repeats = req_count // EXPERTS
     tokens = routes.shape[0]
     placing_blocks = placing.reshape(EXPERTS, CAP, tokens)
+    normed_packed = normed_full.reshape(tokens, model_width // LANES, LANES)
     combining_blocks = combining.reshape(tokens, EXPERTS, CAP)
     mixture_share = jnp.zeros((tokens, share_width), jnp.float32)
     first_slot = 0
@@ -205,11 +206,13 @@
         share_rows = chunk_slots * share_width // LANES
         slots = slice(first_slot, first_slot + chunk_slots)
         first_slot += chunk_slots
-        chunk_placing = placing_blocks[:, slots].reshape(EXPERTS * chunk_slots, tokens)
-        send_rows = jnp.dot(chunk_placing, normed_full, preferred_element_type=jnp.float32).astype(
-            jnp.bfloat16
-        )
-        outgoing = jnp.tile(send_rows.reshape(EXPERTS, packed_rows, LANES), (repeats, 1, 1))
+        chunk_placing = jnp.tile(
+            placing_blocks[:, slots].reshape(EXPERTS * chunk_slots, tokens), (repeats, 1)
+        )
+        send_rows = jnp.einsum(
+            "ct,tkl->ckl", chunk_placing, normed_packed, preferred_element_type=jnp.float32
+        ).astype(jnp.bfloat16)
+        outgoing = send_rows.reshape(req_count, packed_rows, LANES)
         arrived = lax.all_to_all(outgoing, "req", split_axis=0, concat_axis=0, tiled=True)
         piece_out = expert_apply(arrived, w_gate, w_up, w_down).reshape(-1, model_width)
         reduced = lax.psum_scatter(piece_out, "tp", scatter_dimension=1, tiled=True)

time: 303 us -> 297 us (0.980)
  local copies, waits for them, and re-layouts: 30.5 us -> 23.8 us
    another operation x5 -> x7, local copies, waits for them, and re-layouts: 9.21 us -> 0.51 us  [the longest x6 0.49 us: per_device(): jnp.tile(placing_blocks[:, slots].reshape(EXPERTS * chunk_slots, tokens),...]
    convert_element_type x0 -> x2, local copies, waits for them, and re-layouts: none -> 5.85 us  [per_device(): send_rows = jnp.einsum('ct,tkl->ckl', chunk_placing, normed_packed, prefe...]
  transfers between devices with their start and end apart: 9 -> 9, of which waited for: 7 -> 7; matrix products, arithmetic and copies ran while one was open for 11% -> 12% of each run, Pallas kernels for 0% -> 0%
where the time goes in v10:
time: 297 us; the launch traced here: 294 us
  waiting for transfers between devices  144 us (48%)
  starting transfers between devices  46.3 us (16%)
  matrix products  30.3 us (10%)
  blocking collectives  25.4 us (9%)
  local copies, waits for them, and re-layouts  23.8 us (8%)
  between operations  14 us (5%)
  other arithmetic  9.67 us (3%)
    all_to_all x2, waiting for transfers between devices, per_device(): lax.all_to_all(outgoing, 'req', split_axis=0, concat_axis=0, tiled=True)  48.1 us
    reduce_scatter x2, waiting for transfers between devices, per_device(): reduced = lax.psum_scatter(piece_out, 'tp', scatter_dimension=1, tiled=True)  29.4 us
    all_to_all x1, waiting for transfers between devices, fetch_prefixes(): arrived = lax.all_to_all(outgoing, 'req', 0, 0, tiled=True)  27.6 us
    all_to_all x1, blocking collectives, tp_reduce_scatter(): arrived = lax.all_to_all(chunks, 'tp', 0, 0, tiled=True)  25.4 us
    all_to_all x1, waiting for transfers between devices, fetch_prefixes(): scattered = lax.all_to_all(tagged, 'req', 0, 0, tiled=True)  18.1 us
    all_to_all x2, starting transfers between devices, per_device(): lax.all_to_all(outgoing, 'req', split_axis=0, concat_axis=0, tiled=True)  15 us
    all_to_all x2, starting transfers between devices, send_back(): return lax.all_to_all(parts, 'req', split_axis=0, concat_axis=0, tiled=True)  13.6 us
    all_to_all x1, waiting for transfers between devices, tp_all_gather(): arrived = lax.all_to_all(copies, 'tp', 0, 0, tiled=True)  13.5 us
  transfers between devices with their start and end apart: 9, of which 7 were waited for; matrix products, arithmetic and copies ran while one was open for 12% of the time, Pallas kernels for 0%

profile of v10, /device:TPU:2, one launch (start us, length us, event | category | flops | bytes accessed | tf_op | source)
XLA Modules:
  0.0 293.8 jit_solution(5531023382999097810)
XLA Ops:
  10.1 7.6 %all-to-all-start = ((bf16[32,80,2,128]{3,1,2,0:T(8,128)(2,1)}), bf16[32,80,2,128]{3,1,2,0:T(8,128)(2,1)S(1)}, u32[]{:S(2)}, u32[]{:S(2)}) async-start(bf16[32,80,2,128]{3,1,2,0:T(8,128)(2,1)} %pad_maximum_fusion), calls=%async_computation | async-start | bytes 2621440 | tf_op jit(solution)/shard_map/all_to_all | solution.py:35
  18.4 18.1 %all-to-all-done = bf16[32,80,2,128]{3,1,2,0:T(8,128)(2,1)S(1)} async-done(((bf16[32,80,2,128]{3,1,2,0:T(8,128)(2,1)}), bf16[32,80,2,128]{3,1,2,0:T(8,128)(2,1)S(1)}, u32[]{:S(2)}, u32[]{:S(2)}) %all-to-all-start) | async-done | bytes 1310752 | tf_op jit(solution)/shard_map/all_to_all | solution.py:35
  36.8 2.6 compare_and_fusion
  39.4 2.4 gather_fusion
  45.2 6.5 %all-to-all-start.1 = ((bf16[32,2,64,2,128]{4,2,1,3,0:T(8,128)(2,1)}), bf16[32,2,64,2,128]{4,2,1,3,0:T(8,128)(2,1)}, u32[]{:S(2)}, u32[]{:S(2)}) async-start(bf16[32,2,64,2,128]{4,2,1,3,0:T(8,128)(2,1)} %copy.197), calls=%async_computation.1 | async-start | bytes 4194304 | tf_op jit(solution)/shard_map/all_to_all | solution.py:41
  52.1 27.6 %all-to-all-done.1 = bf16[32,2,64,2,128]{4,2,1,3,0:T(8,128)(2,1)} async-done(((bf16[32,2,64,2,128]{4,2,1,3,0:T(8,128)(2,1)}), bf16[32,2,64,2,128]{4,2,1,3,0:T(8,128)(2,1)}, u32[]{:S(2)}, u32[]{:S(2)}) %all-to-all-start.1) | async-done | bytes 2097184 | tf_op jit(solution)/shard_map/all_to_all | solution.py:41
  85.6 25.4 %all_to_all.40 = bf16[8,64,512]{2,1,0:T(8,128)(2,1)S(1)} all-to-all(bf16[8,64,512]{2,1,0:T(8,128)(2,1)S(1)} %bitcast.175), channel_id=1, replica_groups=mesh['req'=32,'tp'=8] {'tp'}, dimensions={0} | all-to-all | bytes 1048576 | tf_op jit(solution)/shard_map/all_to_all | solution.py:51
  112.0 3.5 %all-to-all-start.3 = ((bf16[8,64,512]{2,1,0:T(8,128)(2,1)}), bf16[8,64,512]{2,1,0:T(8,128)(2,1)S(1)}, u32[]{:S(2)}, u32[]{:S(2)}) async-start(bf16[8,64,512]{2,1,0:T(8,128)(2,1)} %broadcast_in_dim.88), calls=%async_computation.3 | async-start | bytes 1048576 | tf_op jit(solution)/shard_map/all_to_all | solution.py:58
  117.6 13.5 %all-to-all-done.3 = bf16[8,64,512]{2,1,0:T(8,128)(2,1)S(1)} async-done(((bf16[8,64,512]{2,1,0:T(8,128)(2,1)}), bf16[8,64,512]{2,1,0:T(8,128)(2,1)S(1)}, u32[]{:S(2)}, u32[]{:S(2)}) %all-to-all-start.3) | async-done | bytes 524320 | tf_op jit(solution)/shard_map/all_to_all | solution.py:58
  134.3 2.2 copy.223
  136.5 8.4 %all-to-all-start.6 = ((bf16[32,192,128]{2,1,0:T(8,128)(2,1)}), bf16[32,192,128]{2,1,0:T(8,128)(2,1)}, u32[]{:S(2)}, u32[]{:S(2)}) async-start(bf16[32,192,128]{2,1,0:T(8,128)(2,1)} %bitcast.171), calls=%async_computation.7 | async-start | bytes 3145728 | tf_op jit(solution)/shard_map/all_to_all | solution.py:216
  147.3 3.7 %copy.216 = bf16[384,32,128]{2,1,0:T(8,128)(2,1)} copy(bf16[384,32,128]{2,0,1:T(8,128)(2,1)S(1)} %convolution_convert_fusion.3) | data formatting | bytes 6291456 | tf_op jit(solution)/shard_map/convert_element_type | solution.py:214
  151.0 16.0 %all-to-all-done.6 = bf16[32,192,128]{2,1,0:T(8,128)(2,1)} async-done(((bf16[32,192,128]{2,1,0:T(8,128)(2,1)}), bf16[32,192,128]{2,1,0:T(8,128)(2,1)}, u32[]{:S(2)}, u32[]{:S(2)}) %all-to-all-start.6) | async-done | bytes 1572896 | tf_op jit(solution)/shard_map/all_to_all | solution.py:216
  166.9 6.6 %all-to-all-start.4 = ((bf16[32,384,128]{2,1,0:T(8,128)(2,1)}), bf16[32,384,128]{2,1,0:T(8,128)(2,1)}, u32[]{:S(2)}, u32[]{:S(2)}) async-start(bf16[32,384,128]{2,1,0:T(8,128)(2,1)} %bitcast.169), calls=%async_computation.4 | async-start | bytes 6291456 | tf_op jit(solution)/shard_map/all_to_all | solution.py:216
  173.6 2.7 fusion.24
  176.3 5.1 %convolution_convert_fusion.1 = bf16[192,4096]{1,0:T(8,128)(2,1)} fusion(bf16[1,256,4096]{2,1,0:T(8,128)(2,1)} %param.28, bf16[32,128,256]{2,1,0:T(8,128)(2,1)S(1)} %bitcast.165, bf16[192,32,128]{2,1,0:T(8,128)(2,1)} %bitcast.48, f32[192,256]{1,0:T(8,128)S(1)} %fusion.24), kind=kOutput, calls=%fused_computation.2 | convolution fusion | flops 806387712 | bytes 7536640 | tf_op jit(solution)/shard_map/dot_general | solution.py:143
  181.5 32.1 %all-to-all-done.4 = bf16[32,384,128]{2,1,0:T(8,128)(2,1)} async-done(((bf16[32,384,128]{2,1,0:T(8,128)(2,1)}), bf16[32,384,128]{2,1,0:T(8,128)(2,1)}, u32[]{:S(2)}, u32[]{:S(2)}) %all-to-all-start.4) | async-done | bytes 3145760 | tf_op jit(solution)/shard_map/all_to_all | solution.py:216
  213.5 4.4 %fusion.12 = f32[384,256]{1,0:T(8,128)} fusion(bf16[32,128,256]{2,1,0:T(8,128)(2,1)} %bitcast.187, bf16[384,32,128]{2,1,0:T(8,128)(2,1)} %bitcast.38), kind=kOutput, calls=%fused_computation.23 | convolution fusion | flops 805306368 | bytes 5636096 | tf_op jit(solution)/shard_map/rkl,klh->rh/dot_general | solution.py:134
  217.9 7.8 %convolution_convert_fusion = bf16[384,4096]{1,0:T(8,128)(2,1)} fusion(bf16[1,256,4096]{2,1,0:T(8,128)(2,1)} %param.28, bf16[32,128,256]{2,1,0:T(8,128)(2,1)S(1)} %bitcast.164, bf16[384,32,128]{2,1,0:T(8,128)(2,1)} %bitcast.38, f32[384,256]{1,0:T(8,128)} %fusion.12), kind=kOutput, calls=%fused_computation.1 | convolution fusion | flops 1612775424 | bytes 10878976 | tf_op jit(solution)/shard_map/dot_general | solution.py:143
  226.6 2.1 fusion.52
  230.9 6.2 %all-to-all-start.7 = ((bf16[32,24,128]{2,1,0:T(8,128)(2,1)}), bf16[32,24,128]{2,1,0:T(8,128)(2,1)S(1)}, u32[]{:S(2)}, u32[]{:S(2)}) async-start(bf16[32,24,128]{2,1,0:T(8,128)(2,1)} %reshape.361), calls=%async_computation.9 | async-start | bytes 393216 | tf_op jit(solution)/shard_map/all_to_all | solution.py:150
  237.1 29.3 %reduce-scatter.3.cloned.1.call-done = bf16[384,512]{1,0:T(8,128)(2,1)} async-done(((bf16[384,4096]{1,0:T(8,128)(2,1)}), bf16[384,512]{1,0:T(8,128)(2,1)}) %reduce-scatter.3.cloned.1.call-update) | async-done | bytes 393232 | tf_op jit(solution)/shard_map/reduce_scatter | solution.py:218
  268.4 7.5 %all-to-all-start.5 = ((bf16[32,48,128]{2,1,0:T(8,128)(2,1)}), bf16[32,48,128]{2,1,0:T(8,128)(2,1)S(1)}, u32[]{:S(2)}, u32[]{:S(2)}) async-start(bf16[32,48,128]{2,1,0:T(8,128)(2,1)} %reshape.354), calls=%async_computation.6 | async-start | bytes 786432 | tf_op jit(solution)/shard_map/all_to_all | solution.py:150
  277.2 7.7 %all-to-all-done.5 = bf16[32,48,128]{2,1,0:T(8,128)(2,1)S(1)} async-done(((bf16[32,48,128]{2,1,0:T(8,128)(2,1)}), bf16[32,48,128]{2,1,0:T(8,128)(2,1)S(1)}, u32[]{:S(2)}, u32[]{:S(2)}) %all-to-all-start.5) | async-done | bytes 393248 | tf_op jit(solution)/shard_map/all_to_all | solution.py:150
  (115 shorter events, 31.0 us)
Async XLA Ops:
  6.5 169.8 %copy-start = (bf16[1,4096,256]{2,1,0:T(8,128)(2,1)S(1)}, bf16[1,4096,256]{2,1,0:T(8,128)(2,1)}, u32[]{:S(2)}) copy-start(bf16[1,4096,256]{2,1,0:T(8,128)(2,1)} %param.27) | copy-start | bytes 6291460
  8.9 8.8 %copy-start.8 = (s32[4]{0:T(128)S(1)}, s32[4]{0:T(128)}, u32[]{:S(2)}) copy-start(s32[4]{0:T(128)} %param.19) | copy-start | bytes 52
  10.1 26.4 %all-to-all-start = ((bf16[32,80,2,128]{3,1,2,0:T(8,128)(2,1)}), bf16[32,80,2,128]{3,1,2,0:T(8,128)(2,1)S(1)}, u32[]{:S(2)}, u32[]{:S(2)}) async-start(bf16[32,80,2,128]{3,1,2,0:T(8,128)(2,1)} %pad_maximum_fusion), calls=%async_computation | async-start | bytes 2621440 | tf_op jit(solution)/shard_map/all_to_all | solution.py:35
  45.2 6.5 %copy-start.7 = (bf16[64,2,128]{2,1,0:T(2,128)(2,1)S(1)}, bf16[64,2,128]{2,1,0:T(2,128)(2,1)}, u32[]{:S(2)}) copy-start(bf16[64,2,128]{2,1,0:T(2,128)(2,1)} %param.17) | copy-start | bytes 98308
  45.2 6.5 %copy-start.6 = (bf16[64,512]{1,0:T(8,128)(2,1)S(1)}, bf16[64,512]{1,0:T(8,128)(2,1)}, u32[]{:S(2)}) copy-start(bf16[64,512]{1,0:T(8,128)(2,1)} %param.16) | copy-start | bytes 196612
  45.2 6.5 %copy-start.14 = (s32[2]{0:T(128)S(1)}, s32[2]{0:T(128)}, u32[]{:S(2)}) copy-start(s32[2]{0:T(128)} %param.21) | copy-start | bytes 28
  45.2 34.5 %all-to-all-start.1 = ((bf16[32,2,64,2,128]{4,2,1,3,0:T(8,128)(2,1)}), bf16[32,2,64,2,128]{4,2,1,3,0:T(8,128)(2,1)}, u32[]{:S(2)}, u32[]{:S(2)}) async-start(bf16[32,2,64,2,128]{4,2,1,3,0:T(8,128)(2,1)} %copy.197), calls=%async_computation.1 | async-start | bytes 4194304 | tf_op jit(solution)/shard_map/all_to_all | solution.py:41
  82.5 2.2 copy-start.3
  85.5 30.3 %copy-start.13 = (s32[64,2]{0,1:T(2,128)S(1)}, s32[64,2]{0,1:T(2,128)}, u32[]{:S(2)}) copy-start(s32[64,2]{0,1:T(2,128)} %param.25) | copy-start | bytes 1540
  112.0 19.2 %all-to-all-start.3 = ((bf16[8,64,512]{2,1,0:T(8,128)(2,1)}), bf16[8,64,512]{2,1,0:T(8,128)(2,1)S(1)}, u32[]{:S(2)}, u32[]{:S(2)}) async-start(bf16[8,64,512]{2,1,0:T(8,128)(2,1)} %broadcast_in_dim.88), calls=%async_computation.3 | async-start | bytes 1048576 | tf_op jit(solution)/shard_map/all_to_all | solution.py:58
  115.6 15.5 %copy-start.11 = (pred[64]{0:T(512)(128)(4,1)}, pred[64]{0:T(512)(128)(4,1)S(1)}, u32[]{:S(2)}) copy-start(pred[64]{0:T(512)(128)(4,1)S(1)} %fusion.93) | copy-start | bytes 196
  131.3 1.5 copy-start.1
  131.3 1.5 copy-start.5
  132.8 1.6 copy-start.9
  133.0 0.8 copy-start.2
  136.5 30.5 %all-to-all-start.6 = ((bf16[32,192,128]{2,1,0:T(8,128)(2,1)}), bf16[32,192,128]{2,1,0:T(8,128)(2,1)}, u32[]{:S(2)}, u32[]{:S(2)}) async-start(bf16[32,192,128]{2,1,0:T(8,128)(2,1)} %bitcast.171), calls=%async_computation.7 | async-start | bytes 3145728 | tf_op jit(solution)/shard_map/all_to_all | solution.py:216
  166.9 46.6 %all-to-all-start.4 = ((bf16[32,384,128]{2,1,0:T(8,128)(2,1)}), bf16[32,384,128]{2,1,0:T(8,128)(2,1)}, u32[]{:S(2)}, u32[]{:S(2)}) async-start(bf16[32,384,128]{2,1,0:T(8,128)(2,1)} %bitcast.169), calls=%async_computation.4 | async-start | bytes 6291456 | tf_op jit(solution)/shard_map/all_to_all | solution.py:216
  173.5 55.6 %reduce-scatter.5.cloned.1.call-start = ((), (), s32[]{:S(2)}) async-start(), calls=%async_computation.11 | async-start | bytes 1769472 | tf_op jit(solution)/shard_map/reduce_scatter | solution.py:218
  181.4 85.0 %reduce-scatter.3.cloned.1.call-start = ((), (), s32[]{:S(2)}) async-start(), calls=%async_computation.10 | async-start | bytes 3538944 | tf_op jit(solution)/shard_map/reduce_scatter | solution.py:218
  225.7 0.9 copy-start.4
  225.7 0.9 copy-start.10
  228.7 47.3 %copy-start.12 = (pred[64]{0:T(512)(128)(4,1)S(1)}, pred[64]{0:T(512)(128)(4,1)}, u32[]{:S(2)}) copy-start(pred[64]{0:T(512)(128)(4,1)} %copy-done.11) | copy-start | bytes 196
  230.9 37.5 %all-to-all-start.7 = ((bf16[32,24,128]{2,1,0:T(8,128)(2,1)}), bf16[32,24,128]{2,1,0:T(8,128)(2,1)S(1)}, u32[]{:S(2)}, u32[]{:S(2)}) async-start(bf16[32,24,128]{2,1,0:T(8,128)(2,1)} %reshape.361), calls=%async_computation.9 | async-start | bytes 393216 | tf_op jit(solution)/shard_map/all_to_all | solution.py:150
  268.4 16.5 %all-to-all-start.5 = ((bf16[32,48,128]{2,1,0:T(8,128)(2,1)}), bf16[32,48,128]{2,1,0:T(8,128)(2,1)S(1)}, u32[]{:S(2)}, u32[]{:S(2)}) async-start(bf16[32,48,128]{2,1,0:T(8,128)(2,1)} %reshape.354), calls=%async_computation.6 | async-start | bytes 786432 | tf_op jit(solution)/shard_map/all_to_all | solution.py:150
Sparse Core Ops, SparseCore 0:
  181.5 36.8 reduce-scatter.4
  225.8 40.5 reduce-scatter.2

commit v11 on v10

--- a/solution.py
+++ b/solution.py
@@ -12,7 +12,7 @@
 NPFX = 4
 CAP = 18
 LANES = 128
-CHUNK_SLOTS = (12, 6)
+CHUNK_SLOTS = (6, 6, 6)
 
 
 def broadcast(x, axis, root):

time: 297 us -> 320 us (1.077)
  blocking collectives: 25.4 us -> 81.6 us
  waiting for transfers between devices: 144 us -> 107 us
  local copies, waits for them, and re-layouts: 23.8 us -> 27.7 us
    all_to_all x1 -> x3, blocking collectives: 25.4 us -> 81.6 us  [per_device(): lax.all_to_all(outgoing, 'req', split_axis=0, concat_axis=0, tiled=True)]
    all_to_all x2 -> x1, waiting for transfers between devices: 48.1 us -> 17 us  [tp_reduce_scatter(): arrived = lax.all_to_all(chunks, 'tp', 0, 0, tiled=True)]
    reduce_scatter x2 -> x3, waiting for transfers between devices: 29.4 us -> 20.6 us  [per_device(): reduced = lax.psum_scatter(piece_out, 'tp', scatter_dimension=1, tiled=True)]
    all_to_all x2 -> x1, starting transfers between devices: 15 us -> 8.47 us  [tp_reduce_scatter(): arrived = lax.all_to_all(chunks, 'tp', 0, 0, tiled=True)]
    all_to_all x2 -> x3, starting transfers between devices: 13.6 us -> 17.9 us  [send_back(): return lax.all_to_all(parts, 'req', split_axis=0, concat_axis=0, tiled=True)]
    dot_general x2 -> x3, matrix products: 7.09 us -> 3.29 us  [expert_apply(): jnp.einsum('rkl,klh->rh', packed, w_gate[0].reshape(blocks, LANES, -1), p...]
    dot_general x2 -> x3, matrix products: 12.8 us -> 15.5 us  [expert_apply(): jnp.dot(hidden_units, w_down[0], preferred_element_type=jnp.float32)]
    all_to_all x2 -> x3, waiting for transfers between devices: 7.67 us -> 10 us  [send_back(): return lax.all_to_all(parts, 'req', split_axis=0, concat_axis=0, tiled=True)]
  transfers between devices with their start and end apart: 9 -> 10, of which waited for: 7 -> 7; matrix products, arithmetic and copies ran while one was open for 12% -> 11% of each run, Pallas kernels for 0% -> 0%
where the time goes in v11:
time: 320 us; the launch traced here: 316 us
  waiting for transfers between devices  107 us (33%)
  blocking collectives  81.6 us (25%)
  starting transfers between devices  44.3 us (14%)
  matrix products  31.2 us (10%)
  local copies, waits for them, and re-layouts  27.7 us (9%)
  between operations  13.8 us (4%)
  other arithmetic  10.6 us (3%)
    all_to_all x3, blocking collectives, per_device(): lax.all_to_all(outgoing, 'req', split_axis=0, concat_axis=0, tiled=True)  81.6 us
    all_to_all x1, waiting for transfers between devices, fetch_prefixes(): arrived = lax.all_to_all(outgoing, 'req', 0, 0, tiled=True)  27.6 us
    reduce_scatter x3, waiting for transfers between devices, per_device(): reduced = lax.psum_scatter(piece_out, 'tp', scatter_dimension=1, tiled=True)  20.6 us
    all_to_all x1, waiting for transfers between devices, fetch_prefixes(): scattered = lax.all_to_all(tagged, 'req', 0, 0, tiled=True)  18.1 us
    all_to_all x3, starting transfers between devices, send_back(): return lax.all_to_all(parts, 'req', split_axis=0, concat_axis=0, tiled=True)  17.9 us
    all_to_all x1, waiting for transfers between devices, tp_reduce_scatter(): arrived = lax.all_to_all(chunks, 'tp', 0, 0, tiled=True)  17 us
    dot_general x3, matrix products, expert_apply(): jnp.dot(hidden_units, w_down[0], preferred_element_type=jnp.float32)  15.5 us
    all_to_all x1, waiting for transfers between devices, tp_all_gather(): arrived = lax.all_to_all(copies, 'tp', 0, 0, tiled=True)  13.5 us
  transfers between devices with their start and end apart: 10, of which 7 were waited for; matrix products, arithmetic and copies ran while one was open for 11% of the time, Pallas kernels for 0%

profile of v11, /device:TPU:2, one launch (start us, length us, event | category | flops | bytes accessed | tf_op | source)
XLA Modules:
  0.0 316.2 jit_solution(16183024272874525826)
XLA Ops:
  10.1 7.6 %all-to-all-start = ((bf16[32,80,2,128]{3,1,2,0:T(8,128)(2,1)}), bf16[32,80,2,128]{3,1,2,0:T(8,128)(2,1)S(1)}, u32[]{:S(2)}, u32[]{:S(2)}) async-start(bf16[32,80,2,128]{3,1,2,0:T(8,128)(2,1)} %pad_maximum_fusion), calls=%async_computation | async-start | bytes 2621440 | tf_op jit(solution)/shard_map/all_to_all | solution.py:35
  18.4 18.1 %all-to-all-done = bf16[32,80,2,128]{3,1,2,0:T(8,128)(2,1)S(1)} async-done(((bf16[32,80,2,128]{3,1,2,0:T(8,128)(2,1)}), bf16[32,80,2,128]{3,1,2,0:T(8,128)(2,1)S(1)}, u32[]{:S(2)}, u32[]{:S(2)}) %all-to-all-start) | async-done | bytes 1310752 | tf_op jit(solution)/shard_map/all_to_all | solution.py:35
  36.8 2.5 compare_and_fusion
  39.4 2.4 gather_fusion
  41.8 1.8 slice_select_fusion
  45.2 6.5 %all-to-all-start.1 = ((bf16[32,2,64,2,128]{4,2,1,3,0:T(8,128)(2,1)}), bf16[32,2,64,2,128]{4,2,1,3,0:T(8,128)(2,1)}, u32[]{:S(2)}, u32[]{:S(2)}) async-start(bf16[32,2,64,2,128]{4,2,1,3,0:T(8,128)(2,1)} %copy.239), calls=%async_computation.1 | async-start | bytes 4194304 | tf_op jit(solution)/shard_map/all_to_all | solution.py:41
  52.1 27.6 %all-to-all-done.1 = bf16[32,2,64,2,128]{4,2,1,3,0:T(8,128)(2,1)} async-done(((bf16[32,2,64,2,128]{4,2,1,3,0:T(8,128)(2,1)}), bf16[32,2,64,2,128]{4,2,1,3,0:T(8,128)(2,1)}, u32[]{:S(2)}, u32[]{:S(2)}) %all-to-all-start.1) | async-done | bytes 2097184 | tf_op jit(solution)/shard_map/all_to_all | solution.py:41
  86.4 8.5 %all-to-all-start.2 = ((bf16[8,64,512]{2,1,0:T(8,128)(2,1)}), bf16[8,64,512]{2,1,0:T(8,128)(2,1)S(1)}, u32[]{:S(2)}, u32[]{:S(2)}) async-start(bf16[8,64,512]{2,1,0:T(8,128)(2,1)} %bitcast.190), calls=%async_computation.2 | async-start | bytes 1048576 | tf_op jit(solution)/shard_map/all_to_all | solution.py:51
  95.0 17.0 %all-to-all-done.2 = bf16[8,64,512]{2,1,0:T(8,128)(2,1)S(1)} async-done(((bf16[8,64,512]{2,1,0:T(8,128)(2,1)}), bf16[8,64,512]{2,1,0:T(8,128)(2,1)S(1)}, u32[]{:S(2)}, u32[]{:S(2)}) %all-to-all-start.2) | async-done | bytes 524320 | tf_op jit(solution)/shard_map/all_to_all | solution.py:51
  113.0 3.5 %all-to-all-start.3 = ((bf16[8,64,512]{2,1,0:T(8,128)(2,1)}), bf16[8,64,512]{2,1,0:T(8,128)(2,1)S(1)}, u32[]{:S(2)}, u32[]{:S(2)}) async-start(bf16[8,64,512]{2,1,0:T(8,128)(2,1)} %broadcast_in_dim.88), calls=%async_computation.3 | async-start | bytes 1048576 | tf_op jit(solution)/shard_map/all_to_all | solution.py:58
  119.7 13.5 %all-to-all-done.3 = bf16[8,64,512]{2,1,0:T(8,128)(2,1)S(1)} async-done(((bf16[8,64,512]{2,1,0:T(8,128)(2,1)}), bf16[8,64,512]{2,1,0:T(8,128)(2,1)S(1)}, u32[]{:S(2)}, u32[]{:S(2)}) %all-to-all-start.3) | async-done | bytes 524320 | tf_op jit(solution)/shard_map/all_to_all | solution.py:58
  137.5 28.8 %all_to_all.50 = bf16[32,192,128]{2,1,0:T(8,128)(2,1)S(1)} all-to-all(bf16[32,192,128]{2,1,0:T(8,128)(2,1)S(1)} %bitcast.204), channel_id=1, replica_groups=mesh['req'=32,'tp'=8] {'req'}, dimensions={0} | all-to-all | bytes 3145728 | tf_op jit(solution)/shard_map/all_to_all | solution.py:216
  167.7 5.2 %convolution_convert_fusion.2 = bf16[192,4096]{1,0:T(8,128)(2,1)} fusion(bf16[1,256,4096]{2,1,0:T(8,128)(2,1)} %param.28, bf16[32,128,256]{2,1,0:T(8,128)(2,1)S(1)} %bitcast.191, bf16[192,32,128]{2,1,0:T(8,128)(2,1)} %bitcast.199, f32[192,256]{1,0:T(8,128)} %fusion.17), kind=kOutput, calls=%fused_computation.3 | convolution fusion | flops 806387712 | bytes 7536640 | tf_op jit(solution)/shard_map/dot_general | solution.py:143
  177.3 26.4 %all_to_all.51 = bf16[32,192,128]{2,1,0:T(8,128)(2,1)S(1)} all-to-all(bf16[32,192,128]{2,1,0:T(8,128)(2,1)S(1)} %bitcast.205), channel_id=1, replica_groups=mesh['req'=32,'tp'=8] {'req'}, dimensions={0} | all-to-all | bytes 3145728 | tf_op jit(solution)/shard_map/all_to_all | solution.py:216
  206.2 5.2 %convolution_convert_fusion.1 = bf16[192,4096]{1,0:T(8,128)(2,1)} fusion(bf16[1,256,4096]{2,1,0:T(8,128)(2,1)} %param.28, bf16[32,128,256]{2,1,0:T(8,128)(2,1)S(1)} %bitcast.192, bf16[192,32,128]{2,1,0:T(8,128)(2,1)} %bitcast.201, f32[192,256]{1,0:T(8,128)} %fusion.23), kind=kOutput, calls=%fused_computation.2 | convolution fusion | flops 806387712 | bytes 7536640 | tf_op jit(solution)/shard_map/dot_general | solution.py:143
  214.4 26.4 %all_to_all.52 = bf16[32,192,128]{2,1,0:T(8,128)(2,1)S(1)} all-to-all(bf16[32,192,128]{2,1,0:T(8,128)(2,1)S(1)} %bitcast.206), channel_id=1, replica_groups=mesh['req'=32,'tp'=8] {'req'}, dimensions={0} | all-to-all | bytes 3145728 | tf_op jit(solution)/shard_map/all_to_all | solution.py:216
  242.6 5.1 %convolution_convert_fusion = bf16[192,4096]{1,0:T(8,128)(2,1)} fusion(bf16[1,256,4096]{2,1,0:T(8,128)(2,1)} %param.28, bf16[32,128,256]{2,1,0:T(8,128)(2,1)S(1)} %bitcast.193, bf16[192,32,128]{2,1,0:T(8,128)(2,1)} %bitcast.203, f32[192,256]{1,0:T(8,128)S(1)} %fusion.29), kind=kOutput, calls=%fused_computation.1 | convolution fusion | flops 806387712 | bytes 7536640 | tf_op jit(solution)/shard_map/dot_general | solution.py:143
  247.7 2.1 fusion.71
  252.2 5.0 %all-to-all-start.5 = ((bf16[32,24,128]{2,1,0:T(8,128)(2,1)}), bf16[32,24,128]{2,1,0:T(8,128)(2,1)S(1)}, u32[]{:S(2)}, u32[]{:S(2)}) async-start(bf16[32,24,128]{2,1,0:T(8,128)(2,1)} %reshape.379), calls=%async_computation.6 | async-start | bytes 393216 | tf_op jit(solution)/shard_map/all_to_all | solution.py:150
  260.3 4.0 %all-to-all-done.5 = bf16[32,24,128]{2,1,0:T(8,128)(2,1)S(1)} async-done(((bf16[32,24,128]{2,1,0:T(8,128)(2,1)}), bf16[32,24,128]{2,1,0:T(8,128)(2,1)S(1)}, u32[]{:S(2)}, u32[]{:S(2)}) %all-to-all-start.5) | async-done | bytes 196640 | tf_op jit(solution)/shard_map/all_to_all | solution.py:150
  264.3 5.5 %all-to-all-start.7 = ((bf16[32,24,128]{2,1,0:T(8,128)(2,1)}), bf16[32,24,128]{2,1,0:T(8,128)(2,1)}, u32[]{:S(2)}, u32[]{:S(2)}) async-start(bf16[32,24,128]{2,1,0:T(8,128)(2,1)} %reshape.386), calls=%async_computation.9 | async-start | bytes 393216 | tf_op jit(solution)/shard_map/all_to_all | solution.py:150
  270.5 20.6 %reduce-scatter.8.cloned.1.call-done = bf16[192,512]{1,0:T(8,128)(2,1)} async-done(((bf16[192,4096]{1,0:T(8,128)(2,1)}), bf16[192,512]{1,0:T(8,128)(2,1)}) %reduce-scatter.8.cloned.1.call-update) | async-done | bytes 196624 | tf_op jit(solution)/shard_map/reduce_scatter | solution.py:218
  292.8 7.4 %all-to-all-start.9 = ((bf16[32,24,128]{2,1,0:T(8,128)(2,1)}), bf16[32,24,128]{2,1,0:T(8,128)(2,1)S(1)}, u32[]{:S(2)}, u32[]{:S(2)}) async-start(bf16[32,24,128]{2,1,0:T(8,128)(2,1)} %reshape.393), calls=%async_computation.12 | async-start | bytes 393216 | tf_op jit(solution)/shard_map/all_to_all | solution.py:150
  301.3 6.0 %all-to-all-done.9 = bf16[32,24,128]{2,1,0:T(8,128)(2,1)S(1)} async-done(((bf16[32,24,128]{2,1,0:T(8,128)(2,1)}), bf16[32,24,128]{2,1,0:T(8,128)(2,1)S(1)}, u32[]{:S(2)}, u32[]{:S(2)}) %all-to-all-start.9) | async-done | bytes 196640 | tf_op jit(solution)/shard_map/all_to_all | solution.py:150
  (150 shorter events, 45.5 us)
Async XLA Ops:
  6.5 161.2 %copy-start = (bf16[1,4096,256]{2,1,0:T(8,128)(2,1)S(1)}, bf16[1,4096,256]{2,1,0:T(8,128)(2,1)}, u32[]{:S(2)}) copy-start(bf16[1,4096,256]{2,1,0:T(8,128)(2,1)} %param.27) | copy-start | bytes 6291460
  8.9 8.8 %copy-start.15 = (s32[4]{0:T(128)S(1)}, s32[4]{0:T(128)}, u32[]{:S(2)}) copy-start(s32[4]{0:T(128)} %param.19) | copy-start | bytes 52
  10.1 26.4 %all-to-all-start = ((bf16[32,80,2,128]{3,1,2,0:T(8,128)(2,1)}), bf16[32,80,2,128]{3,1,2,0:T(8,128)(2,1)S(1)}, u32[]{:S(2)}, u32[]{:S(2)}) async-start(bf16[32,80,2,128]{3,1,2,0:T(8,128)(2,1)} %pad_maximum_fusion), calls=%async_computation | async-start | bytes 2621440 | tf_op jit(solution)/shard_map/all_to_all | solution.py:35
  45.2 6.5 %copy-start.10 = (bf16[64,512]{1,0:T(8,128)(2,1)S(1)}, bf16[64,512]{1,0:T(8,128)(2,1)}, u32[]{:S(2)}) copy-start(bf16[64,512]{1,0:T(8,128)(2,1)} %param.16) | copy-start | bytes 196612
  45.2 6.5 %copy-start.12 = (bf16[64,2,128]{2,1,0:T(2,128)(2,1)S(1)}, bf16[64,2,128]{2,1,0:T(2,128)(2,1)}, u32[]{:S(2)}) copy-start(bf16[64,2,128]{2,1,0:T(2,128)(2,1)} %param.17) | copy-start | bytes 98308
  45.2 6.5 %copy-start.23 = (s32[2]{0:T(128)S(1)}, s32[2]{0:T(128)}, u32[]{:S(2)}) copy-start(s32[2]{0:T(128)} %param.21) | copy-start | bytes 28
  45.2 34.5 %all-to-all-start.1 = ((bf16[32,2,64,2,128]{4,2,1,3,0:T(8,128)(2,1)}), bf16[32,2,64,2,128]{4,2,1,3,0:T(8,128)(2,1)}, u32[]{:S(2)}, u32[]{:S(2)}) async-start(bf16[32,2,64,2,128]{4,2,1,3,0:T(8,128)(2,1)} %copy.239), calls=%async_computation.1 | async-start | bytes 4194304 | tf_op jit(solution)/shard_map/all_to_all | solution.py:41
  82.5 2.2 copy-start.6
  85.5 31.0 %copy-start.19 = (s32[64,2]{0,1:T(2,128)S(1)}, s32[64,2]{0,1:T(2,128)}, u32[]{:S(2)}) copy-start(s32[64,2]{0,1:T(2,128)} %param.25) | copy-start | bytes 1540
  86.4 25.6 %all-to-all-start.2 = ((bf16[8,64,512]{2,1,0:T(8,128)(2,1)}), bf16[8,64,512]{2,1,0:T(8,128)(2,1)S(1)}, u32[]{:S(2)}, u32[]{:S(2)}) async-start(bf16[8,64,512]{2,1,0:T(8,128)(2,1)} %bitcast.190), calls=%async_computation.2 | async-start | bytes 1048576 | tf_op jit(solution)/shard_map/all_to_all | solution.py:51
  113.0 20.3 %all-to-all-start.3 = ((bf16[8,64,512]{2,1,0:T(8,128)(2,1)}), bf16[8,64,512]{2,1,0:T(8,128)(2,1)S(1)}, u32[]{:S(2)}, u32[]{:S(2)}) async-start(bf16[8,64,512]{2,1,0:T(8,128)(2,1)} %broadcast_in_dim.88), calls=%async_computation.3 | async-start | bytes 1048576 | tf_op jit(solution)/shard_map/all_to_all | solution.py:58
  116.5 134.0 %reduce-scatter.4.cloned.1.call-start = ((), (), s32[]{:S(2)}) async-start(), calls=%async_computation.13 | async-start | bytes 1769472 | tf_op jit(solution)/shard_map/reduce_scatter | solution.py:218
  116.5 16.8 %copy-start.17 = (pred[64]{0:T(512)(128)(4,1)}, pred[64]{0:T(512)(128)(4,1)S(1)}, u32[]{:S(2)}) copy-start(pred[64]{0:T(512)(128)(4,1)S(1)} %fusion.120) | copy-start | bytes 196
  137.5 28.8 %copy-start.20 = (bf16[1,4096,256]{2,1,0:T(8,128)(2,1)S(1)}, bf16[1,4096,256]{2,1,0:T(8,128)(2,1)}, u32[]{:S(2)}) copy-start(bf16[1,4096,256]{2,1,0:T(8,128)(2,1)} %param.26) | copy-start | bytes 6291460
  172.9 85.7 %reduce-scatter.6.cloned.1.call-start = ((), (), s32[]{:S(2)}) async-start(), calls=%async_computation.14 | async-start | bytes 1769472 | tf_op jit(solution)/shard_map/reduce_scatter | solution.py:218
  177.3 27.6 %copy-start.21 = (bf16[1,4096,256]{2,1,0:T(8,128)(2,1)S(1)}, bf16[1,4096,256]{2,1,0:T(8,128)(2,1)}, u32[]{:S(2)}) copy-start(bf16[1,4096,256]{2,1,0:T(8,128)(2,1)} %param.26) | copy-start | bytes 6291460
  211.4 79.6 %reduce-scatter.8.cloned.1.call-start = ((), (), s32[]{:S(2)}) async-start(), calls=%async_computation.15 | async-start | bytes 1769472 | tf_op jit(solution)/shard_map/reduce_scatter | solution.py:218
  214.4 27.6 %copy-start.22 = (bf16[1,4096,256]{2,1,0:T(8,128)(2,1)S(1)}, bf16[1,4096,256]{2,1,0:T(8,128)(2,1)}, u32[]{:S(2)}) copy-start(bf16[1,4096,256]{2,1,0:T(8,128)(2,1)} %param.26) | copy-start | bytes 6291460
  247.7 2.2 copy-start.8
  247.7 9.5 %copy-start.14 = (s32[64,2]{1,0:T(8,128)S(1)}, s32[64,2]{1,0:T(8,128)}, u32[]{:S(2)}) copy-start(s32[64,2]{1,0:T(8,128)} %copy-done.13) | copy-start | bytes 1540
  252.2 12.2 %all-to-all-start.5 = ((bf16[32,24,128]{2,1,0:T(8,128)(2,1)}), bf16[32,24,128]{2,1,0:T(8,128)(2,1)S(1)}, u32[]{:S(2)}, u32[]{:S(2)}) async-start(bf16[32,24,128]{2,1,0:T(8,128)(2,1)} %reshape.379), calls=%async_computation.6 | async-start | bytes 393216 | tf_op jit(solution)/shard_map/all_to_all | solution.py:150
  264.3 28.5 %all-to-all-start.7 = ((bf16[32,24,128]{2,1,0:T(8,128)(2,1)}), bf16[32,24,128]{2,1,0:T(8,128)(2,1)}, u32[]{:S(2)}, u32[]{:S(2)}) async-start(bf16[32,24,128]{2,1,0:T(8,128)(2,1)} %reshape.386), calls=%async_computation.9 | async-start | bytes 393216 | tf_op jit(solution)/shard_map/all_to_all | solution.py:150
  270.0 37.8 %copy-start.18 = (pred[64]{0:T(512)(128)(4,1)S(1)}, pred[64]{0:T(512)(128)(4,1)}, u32[]{:S(2)}) copy-start(pred[64]{0:T(512)(128)(4,1)} %copy-done.17) | copy-start | bytes 196
  292.8 14.5 %all-to-all-start.9 = ((bf16[32,24,128]{2,1,0:T(8,128)(2,1)}), bf16[32,24,128]{2,1,0:T(8,128)(2,1)S(1)}, u32[]{:S(2)}, u32[]{:S(2)}) async-start(bf16[32,24,128]{2,1,0:T(8,128)(2,1)} %reshape.393), calls=%async_computation.12 | async-start | bytes 393216 | tf_op jit(solution)/shard_map/all_to_all | solution.py:150
  (10 other events, 11.1 us)
Sparse Core Ops, SparseCore 0:
  173.0 34.2 reduce-scatter.3
  211.6 37.4 reduce-scatter.5
  251.7 39.3 reduce-scatter.7

commit v12 on v10

--- a/solution.py
+++ b/solution.py
@@ -223,7 +223,7 @@
         mixture_share = mixture_share + jnp.dot(
             combining_blocks[:, :, slots].reshape(tokens, EXPERTS * chunk_slots),
             summed.reshape(EXPERTS * chunk_slots, share_width),
-            precision=lax.Precision.HIGHEST,
+            precision=lax.Precision.HIGH,
         )
     layer_out = jnp.where(live_rows[:, None], hidden_share + mixture_share, 0.0)
     return layer_out.astype(jnp.bfloat16)

time: 297 us -> 297 us (level)
  no operation moved by 1% of the time
where the time goes in v12:
time: 297 us; the launch traced here: 294 us
  waiting for transfers between devices  144 us (48%)
  starting transfers between devices  46.3 us (16%)
  matrix products  30.2 us (10%)
  blocking collectives  25.4 us (9%)
  local copies, waits for them, and re-layouts  23.8 us (8%)
  between operations  14 us (5%)
  other arithmetic  9.67 us (3%)
    all_to_all x2, waiting for transfers between devices, per_device(): lax.all_to_all(outgoing, 'req', split_axis=0, concat_axis=0, tiled=True)  48.1 us
    reduce_scatter x2, waiting for transfers between devices, per_device(): reduced = lax.psum_scatter(piece_out, 'tp', scatter_dimension=1, tiled=True)  29.4 us
    all_to_all x1, waiting for transfers between devices, fetch_prefixes(): arrived = lax.all_to_all(outgoing, 'req', 0, 0, tiled=True)  27.6 us
    all_to_all x1, blocking collectives, tp_reduce_scatter(): arrived = lax.all_to_all(chunks, 'tp', 0, 0, tiled=True)  25.4 us
    all_to_all x1, waiting for transfers between devices, fetch_prefixes(): scattered = lax.all_to_all(tagged, 'req', 0, 0, tiled=True)  18.1 us
    all_to_all x2, starting transfers between devices, per_device(): lax.all_to_all(outgoing, 'req', split_axis=0, concat_axis=0, tiled=True)  15 us
    all_to_all x2, starting transfers between devices, send_back(): return lax.all_to_all(parts, 'req', split_axis=0, concat_axis=0, tiled=True)  13.6 us
    all_to_all x1, waiting for transfers between devices, tp_all_gather(): arrived = lax.all_to_all(copies, 'tp', 0, 0, tiled=True)  13.5 us
  transfers between devices with their start and end apart: 9, of which 7 were waited for; matrix products, arithmetic and copies ran while one was open for 12% of the time, Pallas kernels for 0%

profile of v12, /device:TPU:2, one launch (start us, length us, event | category | flops | bytes accessed | tf_op | source)
XLA Modules:
  0.0 293.7 jit_solution(12111504875095741170)
XLA Ops:
  10.1 7.6 %all-to-all-start = ((bf16[32,80,2,128]{3,1,2,0:T(8,128)(2,1)}), bf16[32,80,2,128]{3,1,2,0:T(8,128)(2,1)S(1)}, u32[]{:S(2)}, u32[]{:S(2)}) async-start(bf16[32,80,2,128]{3,1,2,0:T(8,128)(2,1)} %pad_maximum_fusion), calls=%async_computation | async-start | bytes 2621440 | tf_op jit(solution)/shard_map/all_to_all | solution.py:35
  18.4 18.1 %all-to-all-done = bf16[32,80,2,128]{3,1,2,0:T(8,128)(2,1)S(1)} async-done(((bf16[32,80,2,128]{3,1,2,0:T(8,128)(2,1)}), bf16[32,80,2,128]{3,1,2,0:T(8,128)(2,1)S(1)}, u32[]{:S(2)}, u32[]{:S(2)}) %all-to-all-start) | async-done | bytes 1310752 | tf_op jit(solution)/shard_map/all_to_all | solution.py:35
  36.8 2.6 compare_and_fusion
  39.4 2.4 gather_fusion
  45.2 6.5 %all-to-all-start.1 = ((bf16[32,2,64,2,128]{4,2,1,3,0:T(8,128)(2,1)}), bf16[32,2,64,2,128]{4,2,1,3,0:T(8,128)(2,1)}, u32[]{:S(2)}, u32[]{:S(2)}) async-start(bf16[32,2,64,2,128]{4,2,1,3,0:T(8,128)(2,1)} %copy.197), calls=%async_computation.1 | async-start | bytes 4194304 | tf_op jit(solution)/shard_map/all_to_all | solution.py:41
  52.1 27.6 %all-to-all-done.1 = bf16[32,2,64,2,128]{4,2,1,3,0:T(8,128)(2,1)} async-done(((bf16[32,2,64,2,128]{4,2,1,3,0:T(8,128)(2,1)}), bf16[32,2,64,2,128]{4,2,1,3,0:T(8,128)(2,1)}, u32[]{:S(2)}, u32[]{:S(2)}) %all-to-all-start.1) | async-done | bytes 2097184 | tf_op jit(solution)/shard_map/all_to_all | solution.py:41
  85.6 25.4 %all_to_all.40 = bf16[8,64,512]{2,1,0:T(8,128)(2,1)S(1)} all-to-all(bf16[8,64,512]{2,1,0:T(8,128)(2,1)S(1)} %bitcast.175), channel_id=1, replica_groups=mesh['req'=32,'tp'=8] {'tp'}, dimensions={0} | all-to-all | bytes 1048576 | tf_op jit(solution)/shard_map/all_to_all | solution.py:51
  112.0 3.5 %all-to-all-start.3 = ((bf16[8,64,512]{2,1,0:T(8,128)(2,1)}), bf16[8,64,512]{2,1,0:T(8,128)(2,1)S(1)}, u32[]{:S(2)}, u32[]{:S(2)}) async-start(bf16[8,64,512]{2,1,0:T(8,128)(2,1)} %broadcast_in_dim.88), calls=%async_computation.3 | async-start | bytes 1048576 | tf_op jit(solution)/shard_map/all_to_all | solution.py:58
  117.6 13.5 %all-to-all-done.3 = bf16[8,64,512]{2,1,0:T(8,128)(2,1)S(1)} async-done(((bf16[8,64,512]{2,1,0:T(8,128)(2,1)}), bf16[8,64,512]{2,1,0:T(8,128)(2,1)S(1)}, u32[]{:S(2)}, u32[]{:S(2)}) %all-to-all-start.3) | async-done | bytes 524320 | tf_op jit(solution)/shard_map/all_to_all | solution.py:58
  134.3 2.2 copy.223
  136.5 8.4 %all-to-all-start.6 = ((bf16[32,192,128]{2,1,0:T(8,128)(2,1)}), bf16[32,192,128]{2,1,0:T(8,128)(2,1)}, u32[]{:S(2)}, u32[]{:S(2)}) async-start(bf16[32,192,128]{2,1,0:T(8,128)(2,1)} %bitcast.171), calls=%async_computation.7 | async-start | bytes 3145728 | tf_op jit(solution)/shard_map/all_to_all | solution.py:216
  147.3 3.7 %copy.216 = bf16[384,32,128]{2,1,0:T(8,128)(2,1)} copy(bf16[384,32,128]{2,0,1:T(8,128)(2,1)S(1)} %convolution_convert_fusion.3) | data formatting | bytes 6291456 | tf_op jit(solution)/shard_map/convert_element_type | solution.py:214
  151.0 16.0 %all-to-all-done.6 = bf16[32,192,128]{2,1,0:T(8,128)(2,1)} async-done(((bf16[32,192,128]{2,1,0:T(8,128)(2,1)}), bf16[32,192,128]{2,1,0:T(8,128)(2,1)}, u32[]{:S(2)}, u32[]{:S(2)}) %all-to-all-start.6) | async-done | bytes 1572896 | tf_op jit(solution)/shard_map/all_to_all | solution.py:216
  166.9 6.6 %all-to-all-start.4 = ((bf16[32,384,128]{2,1,0:T(8,128)(2,1)}), bf16[32,384,128]{2,1,0:T(8,128)(2,1)}, u32[]{:S(2)}, u32[]{:S(2)}) async-start(bf16[32,384,128]{2,1,0:T(8,128)(2,1)} %bitcast.169), calls=%async_computation.4 | async-start | bytes 6291456 | tf_op jit(solution)/shard_map/all_to_all | solution.py:216
  173.6 2.7 fusion.24
  176.3 5.1 %convolution_convert_fusion.1 = bf16[192,4096]{1,0:T(8,128)(2,1)} fusion(bf16[1,256,4096]{2,1,0:T(8,128)(2,1)} %param.28, bf16[32,128,256]{2,1,0:T(8,128)(2,1)S(1)} %bitcast.165, bf16[192,32,128]{2,1,0:T(8,128)(2,1)} %bitcast.48, f32[192,256]{1,0:T(8,128)S(1)} %fusion.24), kind=kOutput, calls=%fused_computation.2 | convolution fusion | flops 806387712 | bytes 7536640 | tf_op jit(solution)/shard_map/dot_general | solution.py:143
  181.5 32.1 %all-to-all-done.4 = bf16[32,384,128]{2,1,0:T(8,128)(2,1)} async-done(((bf16[32,384,128]{2,1,0:T(8,128)(2,1)}), bf16[32,384,128]{2,1,0:T(8,128)(2,1)}, u32[]{:S(2)}, u32[]{:S(2)}) %all-to-all-start.4) | async-done | bytes 3145760 | tf_op jit(solution)/shard_map/all_to_all | solution.py:216
  213.5 4.4 %fusion.12 = f32[384,256]{1,0:T(8,128)} fusion(bf16[32,128,256]{2,1,0:T(8,128)(2,1)} %bitcast.187, bf16[384,32,128]{2,1,0:T(8,128)(2,1)} %bitcast.38), kind=kOutput, calls=%fused_computation.23 | convolution fusion | flops 805306368 | bytes 5636096 | tf_op jit(solution)/shard_map/rkl,klh->rh/dot_general | solution.py:134
  217.9 7.8 %convolution_convert_fusion = bf16[384,4096]{1,0:T(8,128)(2,1)} fusion(bf16[1,256,4096]{2,1,0:T(8,128)(2,1)} %param.28, bf16[32,128,256]{2,1,0:T(8,128)(2,1)S(1)} %bitcast.164, bf16[384,32,128]{2,1,0:T(8,128)(2,1)} %bitcast.38, f32[384,256]{1,0:T(8,128)} %fusion.12), kind=kOutput, calls=%fused_computation.1 | convolution fusion | flops 1612775424 | bytes 10878976 | tf_op jit(solution)/shard_map/dot_general | solution.py:143
  226.6 2.1 fusion.52
  230.9 6.2 %all-to-all-start.7 = ((bf16[32,24,128]{2,1,0:T(8,128)(2,1)}), bf16[32,24,128]{2,1,0:T(8,128)(2,1)S(1)}, u32[]{:S(2)}, u32[]{:S(2)}) async-start(bf16[32,24,128]{2,1,0:T(8,128)(2,1)} %reshape.361), calls=%async_computation.9 | async-start | bytes 393216 | tf_op jit(solution)/shard_map/all_to_all | solution.py:150
  237.1 29.3 %reduce-scatter.3.cloned.1.call-done = bf16[384,512]{1,0:T(8,128)(2,1)} async-done(((bf16[384,4096]{1,0:T(8,128)(2,1)}), bf16[384,512]{1,0:T(8,128)(2,1)}) %reduce-scatter.3.cloned.1.call-update) | async-done | bytes 393232 | tf_op jit(solution)/shard_map/reduce_scatter | solution.py:218
  268.4 7.5 %all-to-all-start.5 = ((bf16[32,48,128]{2,1,0:T(8,128)(2,1)}), bf16[32,48,128]{2,1,0:T(8,128)(2,1)S(1)}, u32[]{:S(2)}, u32[]{:S(2)}) async-start(bf16[32,48,128]{2,1,0:T(8,128)(2,1)} %reshape.354), calls=%async_computation.6 | async-start | bytes 786432 | tf_op jit(solution)/shard_map/all_to_all | solution.py:150
  277.2 7.7 %all-to-all-done.5 = bf16[32,48,128]{2,1,0:T(8,128)(2,1)S(1)} async-done(((bf16[32,48,128]{2,1,0:T(8,128)(2,1)}), bf16[32,48,128]{2,1,0:T(8,128)(2,1)S(1)}, u32[]{:S(2)}, u32[]{:S(2)}) %all-to-all-start.5) | async-done | bytes 393248 | tf_op jit(solution)/shard_map/all_to_all | solution.py:150
  (115 shorter events, 30.9 us)
Async XLA Ops:
  6.5 169.8 %copy-start = (bf16[1,4096,256]{2,1,0:T(8,128)(2,1)S(1)}, bf16[1,4096,256]{2,1,0:T(8,128)(2,1)}, u32[]{:S(2)}) copy-start(bf16[1,4096,256]{2,1,0:T(8,128)(2,1)} %param.27) | copy-start | bytes 6291460
  8.9 8.8 %copy-start.8 = (s32[4]{0:T(128)S(1)}, s32[4]{0:T(128)}, u32[]{:S(2)}) copy-start(s32[4]{0:T(128)} %param.19) | copy-start | bytes 52
  10.1 26.4 %all-to-all-start = ((bf16[32,80,2,128]{3,1,2,0:T(8,128)(2,1)}), bf16[32,80,2,128]{3,1,2,0:T(8,128)(2,1)S(1)}, u32[]{:S(2)}, u32[]{:S(2)}) async-start(bf16[32,80,2,128]{3,1,2,0:T(8,128)(2,1)} %pad_maximum_fusion), calls=%async_computation | async-start | bytes 2621440 | tf_op jit(solution)/shard_map/all_to_all | solution.py:35
  45.2 6.5 %copy-start.7 = (bf16[64,2,128]{2,1,0:T(2,128)(2,1)S(1)}, bf16[64,2,128]{2,1,0:T(2,128)(2,1)}, u32[]{:S(2)}) copy-start(bf16[64,2,128]{2,1,0:T(2,128)(2,1)} %param.17) | copy-start | bytes 98308
  45.2 6.5 %copy-start.6 = (bf16[64,512]{1,0:T(8,128)(2,1)S(1)}, bf16[64,512]{1,0:T(8,128)(2,1)}, u32[]{:S(2)}) copy-start(bf16[64,512]{1,0:T(8,128)(2,1)} %param.16) | copy-start | bytes 196612
  45.2 6.5 %copy-start.14 = (s32[2]{0:T(128)S(1)}, s32[2]{0:T(128)}, u32[]{:S(2)}) copy-start(s32[2]{0:T(128)} %param.21) | copy-start | bytes 28
  45.2 34.5 %all-to-all-start.1 = ((bf16[32,2,64,2,128]{4,2,1,3,0:T(8,128)(2,1)}), bf16[32,2,64,2,128]{4,2,1,3,0:T(8,128)(2,1)}, u32[]{:S(2)}, u32[]{:S(2)}) async-start(bf16[32,2,64,2,128]{4,2,1,3,0:T(8,128)(2,1)} %copy.197), calls=%async_computation.1 | async-start | bytes 4194304 | tf_op jit(solution)/shard_map/all_to_all | solution.py:41
  82.5 2.2 copy-start.3
  85.5 30.3 %copy-start.13 = (s32[64,2]{0,1:T(2,128)S(1)}, s32[64,2]{0,1:T(2,128)}, u32[]{:S(2)}) copy-start(s32[64,2]{0,1:T(2,128)} %param.25) | copy-start | bytes 1540
  112.0 19.2 %all-to-all-start.3 = ((bf16[8,64,512]{2,1,0:T(8,128)(2,1)}), bf16[8,64,512]{2,1,0:T(8,128)(2,1)S(1)}, u32[]{:S(2)}, u32[]{:S(2)}) async-start(bf16[8,64,512]{2,1,0:T(8,128)(2,1)} %broadcast_in_dim.88), calls=%async_computation.3 | async-start | bytes 1048576 | tf_op jit(solution)/shard_map/all_to_all | solution.py:58
  115.6 15.5 %copy-start.11 = (pred[64]{0:T(512)(128)(4,1)}, pred[64]{0:T(512)(128)(4,1)S(1)}, u32[]{:S(2)}) copy-start(pred[64]{0:T(512)(128)(4,1)S(1)} %fusion.93) | copy-start | bytes 196
  131.3 1.5 copy-start.1
  131.3 1.5 copy-start.5
  132.8 1.6 copy-start.9
  133.0 0.8 copy-start.2
  136.5 30.5 %all-to-all-start.6 = ((bf16[32,192,128]{2,1,0:T(8,128)(2,1)}), bf16[32,192,128]{2,1,0:T(8,128)(2,1)}, u32[]{:S(2)}, u32[]{:S(2)}) async-start(bf16[32,192,128]{2,1,0:T(8,128)(2,1)} %bitcast.171), calls=%async_computation.7 | async-start | bytes 3145728 | tf_op jit(solution)/shard_map/all_to_all | solution.py:216
  166.9 46.6 %all-to-all-start.4 = ((bf16[32,384,128]{2,1,0:T(8,128)(2,1)}), bf16[32,384,128]{2,1,0:T(8,128)(2,1)}, u32[]{:S(2)}, u32[]{:S(2)}) async-start(bf16[32,384,128]{2,1,0:T(8,128)(2,1)} %bitcast.169), calls=%async_computation.4 | async-start | bytes 6291456 | tf_op jit(solution)/shard_map/all_to_all | solution.py:216
  173.5 55.6 %reduce-scatter.5.cloned.1.call-start = ((), (), s32[]{:S(2)}) async-start(), calls=%async_computation.11 | async-start | bytes 1769472 | tf_op jit(solution)/shard_map/reduce_scatter | solution.py:218
  181.4 85.0 %reduce-scatter.3.cloned.1.call-start = ((), (), s32[]{:S(2)}) async-start(), calls=%async_computation.10 | async-start | bytes 3538944 | tf_op jit(solution)/shard_map/reduce_scatter | solution.py:218
  225.7 0.9 copy-start.4
  225.7 0.9 copy-start.10
  228.7 47.3 %copy-start.12 = (pred[64]{0:T(512)(128)(4,1)S(1)}, pred[64]{0:T(512)(128)(4,1)}, u32[]{:S(2)}) copy-start(pred[64]{0:T(512)(128)(4,1)} %copy-done.11) | copy-start | bytes 196
  230.9 37.5 %all-to-all-start.7 = ((bf16[32,24,128]{2,1,0:T(8,128)(2,1)}), bf16[32,24,128]{2,1,0:T(8,128)(2,1)S(1)}, u32[]{:S(2)}, u32[]{:S(2)}) async-start(bf16[32,24,128]{2,1,0:T(8,128)(2,1)} %reshape.361), calls=%async_computation.9 | async-start | bytes 393216 | tf_op jit(solution)/shard_map/all_to_all | solution.py:150
  268.4 16.5 %all-to-all-start.5 = ((bf16[32,48,128]{2,1,0:T(8,128)(2,1)}), bf16[32,48,128]{2,1,0:T(8,128)(2,1)S(1)}, u32[]{:S(2)}, u32[]{:S(2)}) async-start(bf16[32,48,128]{2,1,0:T(8,128)(2,1)} %reshape.354), calls=%async_computation.6 | async-start | bytes 786432 | tf_op jit(solution)/shard_map/all_to_all | solution.py:150
Sparse Core Ops, SparseCore 0:
  181.5 36.8 reduce-scatter.4
  225.8 40.5 reduce-scatter.2

commit v13 on v11

--- a/solution.py
+++ b/solution.py
@@ -12,7 +12,7 @@
 NPFX = 4
 CAP = 18
 LANES = 128
-CHUNK_SLOTS = (6, 6, 6)
+CHUNK_SLOTS = (11, 7)
 
 
 def broadcast(x, axis, root):

time: 320 us -> 301 us (0.941)
  blocking collectives: 81.6 us -> 25.4 us
  waiting for transfers between devices: 107 us -> 149 us
  local copies, waits for them, and re-layouts: 27.7 us -> 22.8 us
    all_to_all x3 -> x1, blocking collectives: 81.6 us -> 25.4 us  [tp_reduce_scatter(): arrived = lax.all_to_all(chunks, 'tp', 0, 0, tiled=True)]
    all_to_all x1 -> x2, waiting for transfers between devices: 17 us -> 47.6 us  [per_device(): lax.all_to_all(outgoing, 'req', split_axis=0, concat_axis=0, tiled=True)]
    reduce_scatter x3 -> x2, waiting for transfers between devices: 20.6 us -> 34 us  [per_device(): reduced = lax.psum_scatter(piece_out, 'tp', scatter_dimension=1, tiled=True)]
    all_to_all x1 -> x2, starting transfers between devices: 8.47 us -> 15.1 us  [per_device(): lax.all_to_all(outgoing, 'req', split_axis=0, concat_axis=0, tiled=True)]
    all_to_all x3 -> x2, starting transfers between devices: 17.9 us -> 13.3 us  [send_back(): return lax.all_to_all(parts, 'req', split_axis=0, concat_axis=0, tiled=True)]
    dot_general x3 -> x2, matrix products: 3.29 us -> 7.8 us  [expert_apply(): jnp.einsum('rkl,klh->rh', packed, w_gate[0].reshape(blocks, LANES, -1), p...]
    dot_general x3 -> x2, matrix products: 15.5 us -> 13.1 us  [expert_apply(): jnp.dot(hidden_units, w_down[0], preferred_element_type=jnp.float32)]
    all_to_all x3 -> x2, waiting for transfers between devices: 10 us -> 7.77 us  [send_back(): return lax.all_to_all(parts, 'req', split_axis=0, concat_axis=0, tiled=True)]
  transfers between devices with their start and end apart: 10 -> 9, of which waited for: 7 -> 7; matrix products, arithmetic and copies ran while one was open for 11% -> 12% of each run, Pallas kernels for 0% -> 0%
where the time goes in v13:
time: 301 us; the launch traced here: 298 us
  waiting for transfers between devices  149 us (50%)
  starting transfers between devices  46.2 us (15%)
  matrix products  31.3 us (10%)
  blocking collectives  25.4 us (8%)
  local copies, waits for them, and re-layouts  22.8 us (8%)
  between operations  13.9 us (5%)
  other arithmetic  9.69 us (3%)
    all_to_all x2, waiting for transfers between devices, per_device(): lax.all_to_all(outgoing, 'req', split_axis=0, concat_axis=0, tiled=True)  47.6 us
    reduce_scatter x2, waiting for transfers between devices, per_device(): reduced = lax.psum_scatter(piece_out, 'tp', scatter_dimension=1, tiled=True)  34 us
    all_to_all x1, waiting for transfers between devices, fetch_prefixes(): arrived = lax.all_to_all(outgoing, 'req', 0, 0, tiled=True)  27.6 us
    all_to_all x1, blocking collectives, tp_reduce_scatter(): arrived = lax.all_to_all(chunks, 'tp', 0, 0, tiled=True)  25.4 us
    all_to_all x1, waiting for transfers between devices, fetch_prefixes(): scattered = lax.all_to_all(tagged, 'req', 0, 0, tiled=True)  18.1 us
    all_to_all x2, starting transfers between devices, per_device(): lax.all_to_all(outgoing, 'req', split_axis=0, concat_axis=0, tiled=True)  15.1 us
    all_to_all x1, waiting for transfers between devices, tp_all_gather(): arrived = lax.all_to_all(copies, 'tp', 0, 0, tiled=True)  13.5 us
    all_to_all x2, starting transfers between devices, send_back(): return lax.all_to_all(parts, 'req', split_axis=0, concat_axis=0, tiled=True)  13.3 us
  transfers between devices with their start and end apart: 9, of which 7 were waited for; matrix products, arithmetic and copies ran while one was open for 12% of the time, Pallas kernels for 0%

profile of v13, /device:TPU:2, one launch (start us, length us, event | category | flops | bytes accessed | tf_op | source)
XLA Modules:
  0.0 297.9 jit_solution(14383217133564312844)
XLA Ops:
  10.1 7.6 %all-to-all-start = ((bf16[32,80,2,128]{3,1,2,0:T(8,128)(2,1)}), bf16[32,80,2,128]{3,1,2,0:T(8,128)(2,1)S(1)}, u32[]{:S(2)}, u32[]{:S(2)}) async-start(bf16[32,80,2,128]{3,1,2,0:T(8,128)(2,1)} %pad_maximum_fusion), calls=%async_computation | async-start | bytes 2621440 | tf_op jit(solution)/shard_map/all_to_all | solution.py:35
  18.4 18.1 %all-to-all-done = bf16[32,80,2,128]{3,1,2,0:T(8,128)(2,1)S(1)} async-done(((bf16[32,80,2,128]{3,1,2,0:T(8,128)(2,1)}), bf16[32,80,2,128]{3,1,2,0:T(8,128)(2,1)S(1)}, u32[]{:S(2)}, u32[]{:S(2)}) %all-to-all-start) | async-done | bytes 1310752 | tf_op jit(solution)/shard_map/all_to_all | solution.py:35
  36.8 2.6 compare_and_fusion
  39.4 2.4 gather_fusion
  45.2 6.5 %all-to-all-start.1 = ((bf16[32,2,64,2,128]{4,2,1,3,0:T(8,128)(2,1)}), bf16[32,2,64,2,128]{4,2,1,3,0:T(8,128)(2,1)}, u32[]{:S(2)}, u32[]{:S(2)}) async-start(bf16[32,2,64,2,128]{4,2,1,3,0:T(8,128)(2,1)} %copy.197), calls=%async_computation.1 | async-start | bytes 4194304 | tf_op jit(solution)/shard_map/all_to_all | solution.py:41
  52.1 27.6 %all-to-all-done.1 = bf16[32,2,64,2,128]{4,2,1,3,0:T(8,128)(2,1)} async-done(((bf16[32,2,64,2,128]{4,2,1,3,0:T(8,128)(2,1)}), bf16[32,2,64,2,128]{4,2,1,3,0:T(8,128)(2,1)}, u32[]{:S(2)}, u32[]{:S(2)}) %all-to-all-start.1) | async-done | bytes 2097184 | tf_op jit(solution)/shard_map/all_to_all | solution.py:41
  85.6 25.4 %all_to_all.40 = bf16[8,64,512]{2,1,0:T(8,128)(2,1)S(1)} all-to-all(bf16[8,64,512]{2,1,0:T(8,128)(2,1)S(1)} %bitcast.174), channel_id=1, replica_groups=mesh['req'=32,'tp'=8] {'tp'}, dimensions={0} | all-to-all | bytes 1048576 | tf_op jit(solution)/shard_map/all_to_all | solution.py:51
  112.0 3.5 %all-to-all-start.3 = ((bf16[8,64,512]{2,1,0:T(8,128)(2,1)}), bf16[8,64,512]{2,1,0:T(8,128)(2,1)S(1)}, u32[]{:S(2)}, u32[]{:S(2)}) async-start(bf16[8,64,512]{2,1,0:T(8,128)(2,1)} %broadcast_in_dim.88), calls=%async_computation.3 | async-start | bytes 1048576 | tf_op jit(solution)/shard_map/all_to_all | solution.py:58
  117.7 13.5 %all-to-all-done.3 = bf16[8,64,512]{2,1,0:T(8,128)(2,1)S(1)} async-done(((bf16[8,64,512]{2,1,0:T(8,128)(2,1)}), bf16[8,64,512]{2,1,0:T(8,128)(2,1)S(1)}, u32[]{:S(2)}, u32[]{:S(2)}) %all-to-all-start.3) | async-done | bytes 524320 | tf_op jit(solution)/shard_map/all_to_all | solution.py:58
  136.4 8.4 %all-to-all-start.6 = ((bf16[32,224,128]{2,1,0:T(8,128)(2,1)}), bf16[32,224,128]{2,1,0:T(8,128)(2,1)}, u32[]{:S(2)}, u32[]{:S(2)}) async-start(bf16[32,224,128]{2,1,0:T(8,128)(2,1)} %bitcast.170), calls=%async_computation.7 | async-start | bytes 3670016 | tf_op jit(solution)/shard_map/all_to_all | solution.py:216
  147.1 2.7 copy.216
  149.8 20.1 %all-to-all-done.6 = bf16[32,224,128]{2,1,0:T(8,128)(2,1)} async-done(((bf16[32,224,128]{2,1,0:T(8,128)(2,1)}), bf16[32,224,128]{2,1,0:T(8,128)(2,1)}, u32[]{:S(2)}, u32[]{:S(2)}) %all-to-all-start.6) | async-done | bytes 1835040 | tf_op jit(solution)/shard_map/all_to_all | solution.py:216
  169.9 6.6 %all-to-all-start.4 = ((bf16[32,352,128]{2,1,0:T(8,128)(2,1)}), bf16[32,352,128]{2,1,0:T(8,128)(2,1)}, u32[]{:S(2)}, u32[]{:S(2)}) async-start(bf16[32,352,128]{2,1,0:T(8,128)(2,1)} %bitcast.168), calls=%async_computation.4 | async-start | bytes 5767168 | tf_op jit(solution)/shard_map/all_to_all | solution.py:216
  176.8 3.6 %fusion.24 = f32[224,256]{1,0:T(8,128)} fusion(bf16[32,128,256]{2,1,0:T(8,128)(2,1)} %bitcast.184, bf16[224,32,128]{2,1,0:T(8,128)(2,1)} %bitcast.46), kind=kOutput, calls=%fused_computation.27 | convolution fusion | flops 469762048 | bytes 4161536 | tf_op jit(solution)/shard_map/rkl,klh->rh/dot_general | solution.py:134
  180.3 5.6 %convolution_convert_fusion.1 = bf16[224,4096]{1,0:T(8,128)(2,1)} fusion(bf16[1,256,4096]{2,1,0:T(8,128)(2,1)} %param.28, bf16[32,128,256]{2,1,0:T(8,128)(2,1)S(1)} %bitcast.164, bf16[224,32,128]{2,1,0:T(8,128)(2,1)} %bitcast.46, f32[224,256]{1,0:T(8,128)} %fusion.24), kind=kOutput, calls=%fused_computation.2 | convolution fusion | flops 940785664 | bytes 8093696 | tf_op jit(solution)/shard_map/dot_general | solution.py:143
  186.1 27.5 %all-to-all-done.4 = bf16[32,352,128]{2,1,0:T(8,128)(2,1)} async-done(((bf16[32,352,128]{2,1,0:T(8,128)(2,1)}), bf16[32,352,128]{2,1,0:T(8,128)(2,1)}, u32[]{:S(2)}, u32[]{:S(2)}) %all-to-all-start.4) | async-done | bytes 2883616 | tf_op jit(solution)/shard_map/all_to_all | solution.py:216
  213.6 4.2 %fusion.12 = f32[352,256]{1,0:T(8,128)} fusion(bf16[32,128,256]{2,1,0:T(8,128)(2,1)} %bitcast.185, bf16[352,32,128]{2,1,0:T(8,128)(2,1)} %bitcast.38), kind=kOutput, calls=%fused_computation.23 | convolution fusion | flops 738197504 | bytes 5341184 | tf_op jit(solution)/shard_map/rkl,klh->rh/dot_general | solution.py:134
  217.8 7.4 %convolution_convert_fusion = bf16[352,4096]{1,0:T(8,128)(2,1)} fusion(bf16[1,256,4096]{2,1,0:T(8,128)(2,1)} %param.28, bf16[32,128,256]{2,1,0:T(8,128)(2,1)S(1)} %bitcast.163, bf16[352,32,128]{2,1,0:T(8,128)(2,1)} %bitcast.38, f32[352,256]{1,0:T(8,128)} %fusion.12), kind=kOutput, calls=%fused_computation.1 | convolution fusion | flops 1478377472 | bytes 10321920 | tf_op jit(solution)/shard_map/dot_general | solution.py:143
  226.1 2.1 fusion.52
  230.5 5.9 %all-to-all-start.7 = ((bf16[32,28,128]{2,1,0:T(8,128)(2,1)}), bf16[32,28,128]{2,1,0:T(8,128)(2,1)S(1)}, u32[]{:S(2)}, u32[]{:S(2)}) async-start(bf16[32,28,128]{2,1,0:T(8,128)(2,1)} %reshape.361), calls=%async_computation.9 | async-start | bytes 524288 | tf_op jit(solution)/shard_map/all_to_all | solution.py:150
  236.6 34.0 %reduce-scatter.3.cloned.1.call-done = bf16[352,512]{1,0:T(8,128)(2,1)} async-done(((bf16[352,4096]{1,0:T(8,128)(2,1)}), bf16[352,512]{1,0:T(8,128)(2,1)}) %reduce-scatter.3.cloned.1.call-update) | async-done | bytes 360464 | tf_op jit(solution)/shard_map/reduce_scatter | solution.py:218
  270.6 2.0 reshape.354
  272.6 7.4 %all-to-all-start.5 = ((bf16[32,44,128]{2,1,0:T(8,128)(2,1)}), bf16[32,44,128]{2,1,0:T(8,128)(2,1)S(1)}, u32[]{:S(2)}, u32[]{:S(2)}) async-start(bf16[32,44,128]{2,1,0:T(8,128)(2,1)} %reshape.354), calls=%async_computation.6 | async-start | bytes 786432 | tf_op jit(solution)/shard_map/all_to_all | solution.py:150
  281.2 7.8 %all-to-all-done.5 = bf16[32,44,128]{2,1,0:T(8,128)(2,1)S(1)} async-done(((bf16[32,44,128]{2,1,0:T(8,128)(2,1)}), bf16[32,44,128]{2,1,0:T(8,128)(2,1)S(1)}, u32[]{:S(2)}, u32[]{:S(2)}) %all-to-all-start.5) | async-done | bytes 360480 | tf_op jit(solution)/shard_map/all_to_all | solution.py:150
  (107 shorter events, 31.4 us)
Async XLA Ops:
  6.5 173.8 %copy-start = (bf16[1,4096,256]{2,1,0:T(8,128)(2,1)S(1)}, bf16[1,4096,256]{2,1,0:T(8,128)(2,1)}, u32[]{:S(2)}) copy-start(bf16[1,4096,256]{2,1,0:T(8,128)(2,1)} %param.27) | copy-start | bytes 6291460
  8.9 8.8 %copy-start.8 = (s32[4]{0:T(128)S(1)}, s32[4]{0:T(128)}, u32[]{:S(2)}) copy-start(s32[4]{0:T(128)} %param.19) | copy-start | bytes 52
  10.1 26.4 %all-to-all-start = ((bf16[32,80,2,128]{3,1,2,0:T(8,128)(2,1)}), bf16[32,80,2,128]{3,1,2,0:T(8,128)(2,1)S(1)}, u32[]{:S(2)}, u32[]{:S(2)}) async-start(bf16[32,80,2,128]{3,1,2,0:T(8,128)(2,1)} %pad_maximum_fusion), calls=%async_computation | async-start | bytes 2621440 | tf_op jit(solution)/shard_map/all_to_all | solution.py:35
  45.2 6.5 %copy-start.7 = (bf16[64,2,128]{2,1,0:T(2,128)(2,1)S(1)}, bf16[64,2,128]{2,1,0:T(2,128)(2,1)}, u32[]{:S(2)}) copy-start(bf16[64,2,128]{2,1,0:T(2,128)(2,1)} %param.17) | copy-start | bytes 98308
  45.2 6.5 %copy-start.6 = (bf16[64,512]{1,0:T(8,128)(2,1)S(1)}, bf16[64,512]{1,0:T(8,128)(2,1)}, u32[]{:S(2)}) copy-start(bf16[64,512]{1,0:T(8,128)(2,1)} %param.16) | copy-start | bytes 196612
  45.2 6.5 %copy-start.10 = (s32[2]{0:T(128)S(1)}, s32[2]{0:T(128)}, u32[]{:S(2)}) copy-start(s32[2]{0:T(128)} %param.21) | copy-start | bytes 28
  45.2 34.5 %all-to-all-start.1 = ((bf16[32,2,64,2,128]{4,2,1,3,0:T(8,128)(2,1)}), bf16[32,2,64,2,128]{4,2,1,3,0:T(8,128)(2,1)}, u32[]{:S(2)}, u32[]{:S(2)}) async-start(bf16[32,2,64,2,128]{4,2,1,3,0:T(8,128)(2,1)} %copy.197), calls=%async_computation.1 | async-start | bytes 4194304 | tf_op jit(solution)/shard_map/all_to_all | solution.py:41
  82.5 2.2 copy-start.3
  85.5 30.3 %copy-start.9 = (s32[64,2]{0,1:T(2,128)S(1)}, s32[64,2]{0,1:T(2,128)}, u32[]{:S(2)}) copy-start(s32[64,2]{0,1:T(2,128)} %param.25) | copy-start | bytes 1540
  112.0 19.2 %all-to-all-start.3 = ((bf16[8,64,512]{2,1,0:T(8,128)(2,1)}), bf16[8,64,512]{2,1,0:T(8,128)(2,1)S(1)}, u32[]{:S(2)}, u32[]{:S(2)}) async-start(bf16[8,64,512]{2,1,0:T(8,128)(2,1)} %broadcast_in_dim.88), calls=%async_computation.3 | async-start | bytes 1048576 | tf_op jit(solution)/shard_map/all_to_all | solution.py:58
  131.3 1.5 copy-start.1
  131.3 1.5 copy-start.5
  133.0 0.8 copy-start.2
  136.4 33.5 %all-to-all-start.6 = ((bf16[32,224,128]{2,1,0:T(8,128)(2,1)}), bf16[32,224,128]{2,1,0:T(8,128)(2,1)}, u32[]{:S(2)}, u32[]{:S(2)}) async-start(bf16[32,224,128]{2,1,0:T(8,128)(2,1)} %bitcast.170), calls=%async_computation.7 | async-start | bytes 3670016 | tf_op jit(solution)/shard_map/all_to_all | solution.py:216
  169.9 43.7 %all-to-all-start.4 = ((bf16[32,352,128]{2,1,0:T(8,128)(2,1)}), bf16[32,352,128]{2,1,0:T(8,128)(2,1)}, u32[]{:S(2)}, u32[]{:S(2)}) async-start(bf16[32,352,128]{2,1,0:T(8,128)(2,1)} %bitcast.168), calls=%async_computation.4 | async-start | bytes 5767168 | tf_op jit(solution)/shard_map/all_to_all | solution.py:216
  176.5 52.1 %reduce-scatter.5.cloned.1.call-start = ((), (), s32[]{:S(2)}) async-start(), calls=%async_computation.11 | async-start | bytes 2064384 | tf_op jit(solution)/shard_map/reduce_scatter | solution.py:218
  186.0 84.6 %reduce-scatter.3.cloned.1.call-start = ((), (), s32[]{:S(2)}) async-start(), calls=%async_computation.10 | async-start | bytes 3244032 | tf_op jit(solution)/shard_map/reduce_scatter | solution.py:218
  225.2 0.9 copy-start.4
  230.5 42.0 %all-to-all-start.7 = ((bf16[32,28,128]{2,1,0:T(8,128)(2,1)}), bf16[32,28,128]{2,1,0:T(8,128)(2,1)S(1)}, u32[]{:S(2)}, u32[]{:S(2)}) async-start(bf16[32,28,128]{2,1,0:T(8,128)(2,1)} %reshape.361), calls=%async_computation.9 | async-start | bytes 524288 | tf_op jit(solution)/shard_map/all_to_all | solution.py:150
  272.6 16.4 %all-to-all-start.5 = ((bf16[32,44,128]{2,1,0:T(8,128)(2,1)}), bf16[32,44,128]{2,1,0:T(8,128)(2,1)S(1)}, u32[]{:S(2)}, u32[]{:S(2)}) async-start(bf16[32,44,128]{2,1,0:T(8,128)(2,1)} %reshape.354), calls=%async_computation.6 | async-start | bytes 786432 | tf_op jit(solution)/shard_map/all_to_all | solution.py:150
Sparse Core Ops, SparseCore 0:
  186.1 37.8 reduce-scatter.4
  226.6 43.9 reduce-scatter.2
